TPU v7x, 32 devices: a whole 2x2x4 slice. The times are simulated.
32 devices in a mesh: row: 8 (over z, y), col: 4 (over x, core).
Axes of the slice: x: 2, y: 2, z: 4, core: 2. Of those that a mesh axis runs over, the one named last changes fastest.
Arguments:
- density: float32 [4, 256, 2048], P('col', 'row'), may hold values from 0.5 to 2
- momentum: float32 [3, 4, 256, 2048], P(None, 'col', 'row'), may hold values from -6 to 6
- energy: float32 [4, 256, 2048], P('col', 'row'), may hold values from 2 to 5
Outputs:
- tendency: float32 [5, 4, 256, 2048], P(None, 'col', 'row')
All inputs are finite; a program needn't handle non-finite values.
Results may differ from a plain program's by a relative error of at most 0.000053.
Values sent between devices are 32-bit elements; how exact they have to be, the bound alone decides.
No kernel may reach another device: no remote copies, remote signals or barrier semaphores. Data moves between devices by JAX's collectives and lax.ppermute only.
A program may use at most 64 MiB of HBM per device.

v0:
```python
import jax
import jax.numpy as jnp
import numpy as np
from jax import lax
from jax.sharding import PartitionSpec as P


def operator_column(count):
    steps = np.arange(count)
    wave = 2.0 * np.pi * steps / count
    upper = (
        17.0 / 12.0 * np.sin(wave)
        + 101.0 / 300.0 * np.sin(2.0 * wave)
        + 1.0 / 300.0 * np.sin(3.0 * wave)
    )
    lower = 1.0 + np.cos(wave) + 0.1 * np.cos(2.0 * wave)
    ratio = upper / lower
    phase = 2.0 * np.pi * (steps[:, None] * steps[None, :] % count) / count
    return -np.sum(ratio[:, None] * np.sin(phase), axis=0) / count


def operator_table(count):
    column = operator_column(count)
    steps = np.arange(count)
    offsets = (steps[None, :] - steps[:, None]) % count
    return column[offsets].astype(np.float32)


def block_weights(count):
    table = operator_table(count)
    width = 128
    w_self = table[:width, :width]
    w_prev = table[:width, width : 2 * width]
    w_next = table[width : 2 * width, :width]
    return jnp.asarray(np.concatenate([w_prev, w_self, w_next], axis=1))


def compact_last(field):
    count = field.shape[-1]
    width = 128
    blocks = field.reshape(field.shape[:-1] + (count // width, width))
    parts = jnp.einsum(
        "...bj,jk->...bk", blocks, block_weights(count), precision=lax.Precision.HIGHEST
    )
    result = (
        jnp.roll(parts[..., :width], 1, axis=-2)
        + parts[..., width : 2 * width]
        + jnp.roll(parts[..., 2 * width :], -1, axis=-2)
    )
    return result.reshape(field.shape)


def compact_second(field):
    count = field.shape[-2]
    if count <= 256:
        weights = jnp.asarray(operator_table(count))
        return jnp.einsum("...jc,ji->...ic", field, weights, precision=lax.Precision.HIGHEST)
    width = 128
    blocks = field.reshape(field.shape[:-2] + (count // width, width, field.shape[-1]))
    parts = jnp.einsum(
        "...bjc,jk->...bkc", blocks, block_weights(count), precision=lax.Precision.HIGHEST
    )
    result = (
        jnp.roll(parts[..., :width, :], 1, axis=-3)
        + parts[..., width : 2 * width, :]
        + jnp.roll(parts[..., 2 * width :, :], -1, axis=-3)
    )
    return result.reshape(field.shape)


def fluxes(density, momentum, energy):
    speed = momentum / density[None]
    pressure = 0.4 * (energy - 0.5 * jnp.sum(momentum * momentum, axis=0) / density)
    enthalpy = energy + pressure
    vel_x, vel_y = (speed[0], speed[1])
    flux_x = jnp.stack(
        [
            momentum[0],
            momentum[0] * vel_x + pressure,
            momentum[1] * vel_x,
            momentum[2] * vel_x,
            enthalpy * vel_x,
        ]
    )
    flux_y = jnp.stack(
        [
            momentum[1],
            momentum[0] * vel_y,
            momentum[1] * vel_y + pressure,
            momentum[2] * vel_y,
            enthalpy * vel_y,
        ],
        axis=2,
    )
    return (flux_x, flux_y)


def local(density, momentum, energy):
    flux_x, flux_y = fluxes(density, momentum, energy)
    planes, owned, length = (flux_y.shape[0], flux_y.shape[1], flux_y.shape[3])
    packed = flux_y.reshape(planes, owned, 5 * length)
    derivative_x = compact_last(flux_x)
    y_lines = lax.all_to_all(packed, "row", split_axis=2, concat_axis=1, tiled=True)
    derivative_lines = compact_second(y_lines)
    derived = lax.all_to_all(derivative_lines, "row", split_axis=1, concat_axis=2, tiled=True)
    derivative_y = jnp.transpose(derived.reshape(planes, owned, 5, length), (2, 0, 1, 3))
    return -(derivative_x + derivative_y)


def solution(mesh):
    in_specs = (P("col", "row", None), P(None, "col", "row", None), P("col", "row", None))
    out_specs = P(None, "col", "row", None)
    return jax.shard_map(local, mesh=mesh, in_specs=in_specs, out_specs=out_specs, check_vma=False)
```

profile of v0, /device:TPU:0, one launch (start us, length us, event | category | flops | bytes accessed | tf_op | source)
XLA Modules:
  0.0 174.0 jit_solution(4821467168655819884)
XLA Ops:
  0.0 0.0 copy-start
  0.0 1.0 bitcast_dynamic-update-slice_fusion.9
  1.0 0.0 copy-start.1
  1.1 0.0 copy-start.2
  1.1 1.4 multiply_reduce_fusion
  2.5 0.0 copy-done
  2.5 0.0 copy-done.1
  2.5 0.0 copy-done.2
  2.5 0.1 bitcast_dynamic-update-slice_fusion.7
  2.7 3.8 %copy.31 = f32[1,32,5,2048]{1,3,2,0:T(8,128)} copy(f32[1,32,5,2048]{3,1,2,0:T(8,128)S(1)} %bitcast_dynamic-update-slice_fusion.5) | data formatting | bytes 2621440 | tf_op jit(solution)/shard_map/reshape | solution.py:101
  6.5 0.5 broadcast.11
  7.0 47.4 %reduce.1 = f32[10240,32]{1,0:T(8,128)} reduce(f32[10240,1,32]{2,1,0:T(1,128)} %bitcast.106, f32[]{:T(128)} %broadcast.11), dimensions={1}, to_apply=%bitcast.93.reduce_sub_computation | reduce | bytes 2621444
  54.4 5.3 %reshape.146 = f32[8,1,40960]{2,1,0:T(1,128)} reshape(f32[10240,32]{1,0:T(8,128)} %reduce.1) | data formatting | bytes 2621440
  59.8 38.7 %all_to_all.30 = f32[8,1,40960]{2,1,0:T(1,128)S(1)} all-to-all(f32[8,1,40960]{2,1,0:T(1,128)} %reshape.146), channel_id=1, replica_groups=mesh['row'=8,'col'=4] {'row'}, dimensions={0} | all-to-all | bytes 2621440 | tf_op jit(solution)/shard_map/all_to_all | solution.py:103
  98.4 5.2 %reduce.2 = f32[8,40960]{1,0:T(8,128)} reduce(f32[8,1,40960]{2,1,0:T(1,128)S(1)} %all_to_all.30, f32[]{:T(128)} %broadcast.11), dimensions={1}, to_apply=%all_to_all.22.reduce_sub_computation | reduce | bytes 2621444 | tf_op jit(solution)/shard_map/all_to_all | solution.py:103
  103.7 12.0 %reshape.147 = f32[10240,1,32]{2,1,0:T(1,128)} reshape(f32[8,40960]{1,0:T(8,128)} %reduce.2) | data formatting | bytes 2621440
  115.6 10.6 %copy.26 = f32[1,32,10240]{2,1,0:T(8,128)} copy(f32[1,32,10240]{1,0,2:T(1,128)} %bitcast.107) | data formatting | bytes 2621440 | tf_op jit(solution)/shard_map/all_to_all | solution.py:103
  126.2 1.5 reshape.141
  127.8 2.2 %convolution_bitcast_fusion = f32[1,256,1280]{2,1,0:T(8,128)S(1)} fusion(f32[256,256]{1,0:T(8,128)} %constant.17, f32[256,1280]{1,0:T(8,128)S(1)} %reshape.141), kind=kOutput, calls=%fused_computation | convolution fusion | flops 1006632960 | bytes 2883584 | tf_op jit(solution)/shard_map/...jc,ji->...ic/dot_general | solution.py:57
  130.0 2.4 %copy.27 = f32[1,256,1280]{2,0,1:T(1,128)} copy(f32[1,256,1280]{2,1,0:T(8,128)S(1)} %convolution_bitcast_fusion) | data formatting | bytes 2621440 | tf_op jit(solution)/shard_map/...jc,ji->...ic/transpose | solution.py:57
  132.4 4.3 %all-to-all-start.1 = ((f32[1,256,1280]{2,0,1:T(1,128)}), f32[1,256,1280]{2,0,1:T(1,128)}, u32[]{:S(2)}, u32[]{:S(2)}) async-start(f32[1,256,1280]{2,0,1:T(1,128)} %copy.27), calls=%async_computation.1 | async-start | bytes 2621440 | tf_op jit(solution)/shard_map/all_to_all | solution.py:105
  136.6 0.1 multiply_bitcast_fusion
  136.9 0.1 fusion.7
  137.1 0.0 copy-start.3
  137.2 0.8 copy-done.3
  138.0 3.5 %convolution_bitcast_fusion.1 = f32[5,1,32,16,384]{4,3,2,0,1:T(8,128)S(1)} fusion(f32[5,32,16,128]{3,2,1,0:T(8,128)S(1)} %bitcast_dynamic-update-slice_fusion, f32[128,384,1,1]{1,0,3,2:T(8,128)S(1)} %copy-done.3), kind=kOutput, calls=%fused_computation.1 | convolution fusion | flops 1509949440 | bytes 5439488 | tf_op jit(solution)/shard_map/...bj,jk->...bk/dot_general | solution.py:42
  141.5 0.1 fusion.10
  141.6 0.2 fusion.9
  141.9 0.4 fusion
  142.2 0.2 reshape.137
  142.4 24.9 %all-to-all-done.1 = f32[1,256,1280]{2,0,1:T(1,128)} async-done(((f32[1,256,1280]{2,0,1:T(1,128)}), f32[1,256,1280]{2,0,1:T(1,128)}, u32[]{:S(2)}, u32[]{:S(2)}) %all-to-all-start.1) | async-done | bytes 1310752 | tf_op jit(solution)/shard_map/all_to_all | solution.py:105
  167.3 3.1 %copy.40 = f32[1,8,32,1280]{3,1,2,0:T(8,128)} copy(f32[1,8,32,1280]{3,0,2,1:T(1,128)} %bitcast.16) | data formatting | bytes 2621440 | tf_op jit(solution)/shard_map/all_to_all | solution.py:105
  170.5 1.5 reshape.140
  172.0 2.0 %fusion.1 = f32[5,1,32,2048]{3,2,1,0:T(8,128)} fusion(f32[5,1,32,2048]{3,2,1,0:T(8,128)S(1)} %reshape.137, f32[1,32,5,2048]{3,2,1,0:T(8,128)S(1)} %reshape.140), kind=kLoop, calls=%fused_computation.5 | loop fusion | flops 655360 | bytes 3932160 | tf_op jit(solution)/shard_map/neg | solution.py:107
  (13 shorter events, 0.4 us)
Async XLA Ops:
  0.0 2.5 %copy-start = (f32[3,1,32,2048]{3,2,1,0:T(8,128)S(1)}, f32[3,1,32,2048]{3,2,1,0:T(8,128)}, u32[]{:S(2)}) copy-start(f32[3,1,32,2048]{3,2,1,0:T(8,128)} %param.6) | copy-start | bytes 2359300
  1.0 1.5 copy-start.1
  1.1 1.5 copy-start.2
  132.4 35.0 %all-to-all-start.1 = ((f32[1,256,1280]{2,0,1:T(1,128)}), f32[1,256,1280]{2,0,1:T(1,128)}, u32[]{:S(2)}, u32[]{:S(2)}) async-start(f32[1,256,1280]{2,0,1:T(1,128)} %copy.27), calls=%async_computation.1 | async-start | bytes 2621440 | tf_op jit(solution)/shard_map/all_to_all | solution.py:105
  137.1 0.9 copy-start.3
where the time goes:
time: 175 us; the launch traced here: 174 us
  other arithmetic  56.7 us (32%)
  local copies, waits for them, and re-layouts  43.5 us (25%)
  blocking collectives  38.7 us (22%)
  waiting for transfers between devices  24.9 us (14%)
  matrix products  5.71 us (3%)
  starting transfers between devices  4.26 us (2%)
    unnamed x6, other arithmetic  47.7 us
    all_to_all x1, blocking collectives, local(): lax.all_to_all(packed, 'row', split_axis=2, concat_axis=1, tiled=True)  38.7 us
    all_to_all x1, waiting for transfers between devices, local(): lax.all_to_all(derivative_lines, 'row', split_axis=1, concat_axis=2, tile...  24.9 us
    unnamed x21, local copies, waits for them, and re-layouts  20 us
    all_to_all x1, local copies, waits for them, and re-layouts, local(): lax.all_to_all(packed, 'row', split_axis=2, concat_axis=1, tiled=True)  10.6 us
    all_to_all x1, other arithmetic, local(): lax.all_to_all(packed, 'row', split_axis=2, concat_axis=1, tiled=True)  5.24 us
    all_to_all x1, starting transfers between devices, local(): lax.all_to_all(derivative_lines, 'row', split_axis=1, concat_axis=2, tile...  4.26 us
    reshape x1, local copies, waits for them, and re-layouts, local(): packed = flux_y.reshape(planes, owned, 5 * length)  3.76 us
  transfers between devices with their start and end apart: 1, of which 1 were waited for; matrix products, arithmetic and copies ran while one was open for 3% of the time, Pallas kernels for 0%

commit v1 on v0

--- a/solution.py
+++ b/solution.py
@@ -50,22 +50,40 @@
     return result.reshape(field.shape)
 
 
-def compact_second(field):
-    count = field.shape[-2]
-    if count <= 256:
-        weights = jnp.asarray(operator_table(count))
-        return jnp.einsum("...jc,ji->...ic", field, weights, precision=lax.Precision.HIGHEST)
-    width = 128
-    blocks = field.reshape(field.shape[:-2] + (count // width, width, field.shape[-1]))
-    parts = jnp.einsum(
-        "...bjc,jk->...bkc", blocks, block_weights(count), precision=lax.Precision.HIGHEST
-    )
-    result = (
-        jnp.roll(parts[..., :width, :], 1, axis=-3)
-        + parts[..., width : 2 * width, :]
-        + jnp.roll(parts[..., 2 * width :, :], -1, axis=-3)
-    )
-    return result.reshape(field.shape)
+def column_basis(block, tol=1e-12):
+    rest = block.copy()
+    basis = []
+    while len(basis) < block.shape[1]:
+        norms = np.sqrt(np.sum(rest * rest, axis=0))
+        pick = int(np.argmax(norms))
+        if norms[pick] <= tol:
+            break
+        vec = rest[:, pick].copy()
+        for _ in range(2):
+            for q in basis:
+                vec = vec - np.sum(q * vec) * q
+        vec = vec / np.sqrt(np.sum(vec * vec))
+        basis.append(vec)
+        rest = rest - vec[:, None] * np.sum(vec[:, None] * rest, axis=0)[None, :]
+    return basis
+
+
+def y_operator(rows, groups):
+    count = rows * groups
+    column = operator_column(count)
+    steps = np.arange(count)
+    full = column[(steps[:, None] - steps[None, :]) % count]
+    own = full[:rows, :rows].astype(np.float32)
+    shifts = []
+    for e in range(1, groups):
+        block = full[:rows, rows * e : rows * (e + 1)]
+        basis = column_basis(block)
+        if not basis:
+            continue
+        q = np.stack(basis, axis=1)
+        w = np.sum(q[:, :, None] * block[:, None, :], axis=0)
+        shifts.append((e, q.astype(np.float32), w.astype(np.float32)))
+    return own, shifts
 
 
 def fluxes(density, momentum, energy):
@@ -89,25 +107,45 @@
             momentum[1] * vel_y + pressure,
             momentum[2] * vel_y,
             enthalpy * vel_y,
-        ],
-        axis=2,
+        ]
     )
     return (flux_x, flux_y)
 
 
-def local(density, momentum, energy):
-    flux_x, flux_y = fluxes(density, momentum, energy)
-    planes, owned, length = (flux_y.shape[0], flux_y.shape[1], flux_y.shape[3])
-    packed = flux_y.reshape(planes, owned, 5 * length)
-    derivative_x = compact_last(flux_x)
-    y_lines = lax.all_to_all(packed, "row", split_axis=2, concat_axis=1, tiled=True)
-    derivative_lines = compact_second(y_lines)
-    derived = lax.all_to_all(derivative_lines, "row", split_axis=1, concat_axis=2, tiled=True)
-    derivative_y = jnp.transpose(derived.reshape(planes, owned, 5, length), (2, 0, 1, 3))
-    return -(derivative_x + derivative_y)
+def make_local(groups):
+    def local(density, momentum, energy):
+        flux_x, flux_y = fluxes(density, momentum, energy)
+        rows = flux_y.shape[2]
+        own, shifts = y_operator(rows, groups)
+        derivative_x = compact_last(flux_x)
+        hi = lax.Precision.HIGHEST
+        weights = jnp.asarray(np.concatenate([w for _, _, w in shifts], axis=0))
+        moments = jnp.einsum("rq,fzqx->rfzx", weights, flux_y, precision=hi)
+        received = []
+        start = 0
+        for e, q, w in shifts:
+            part = moments[start : start + w.shape[0]]
+            start += w.shape[0]
+            perm = [(j, (j - e) % groups) for j in range(groups)]
+            received.append(lax.ppermute(part, "row", perm))
+        received = jnp.concatenate(received, axis=0)
+        spread = jnp.asarray(np.concatenate([q for _, q, _ in shifts], axis=1))
+        derivative_y = jnp.einsum("pq,fzqx->fzpx", jnp.asarray(own), flux_y, precision=hi)
+        derivative_y = derivative_y + jnp.einsum(
+            "pr,rfzx->fzpx", spread, received, precision=hi
+        )
+        return -(derivative_x + derivative_y)
+
+    return local
 
 
 def solution(mesh):
     in_specs = (P("col", "row", None), P(None, "col", "row", None), P("col", "row", None))
     out_specs = P(None, "col", "row", None)
-    return jax.shard_map(local, mesh=mesh, in_specs=in_specs, out_specs=out_specs, check_vma=False)
+    return jax.shard_map(
+        make_local(mesh.shape["row"]),
+        mesh=mesh,
+        in_specs=in_specs,
+        out_specs=out_specs,
+        check_vma=False,
+    )

time: 175 us -> 28.2 us (0.16)
  other arithmetic: 56.7 us -> 3.15 us
  blocking collectives: 38.7 us -> 0 us
  local copies, waits for them, and re-layouts: 43.5 us -> 5.82 us
  waiting for transfers between devices: 24.9 us -> 0.01 us
  starting transfers between devices: 4.26 us -> 9.88 us
  matrix products: 5.71 us -> 8.69 us
    unnamed x6 -> x5, other arithmetic: 47.7 us -> 0.27 us
    all_to_all x1 -> x0, blocking collectives: 38.7 us -> none  [local(): lax.all_to_all(packed, 'row', split_axis=2, concat_axis=1, tiled=True)]
    all_to_all x1 -> x0, waiting for transfers between devices: 24.9 us -> none  [local(): lax.all_to_all(derivative_lines, 'row', split_axis=1, concat_axis=2, tile...]
    unnamed x21 -> x24, local copies, waits for them, and re-layouts: 20 us -> 3.22 us
    all_to_all x2 -> x0, local copies, waits for them, and re-layouts: 13.8 us -> none  [the longest x1 10.6 us: local(): lax.all_to_all(packed, 'row', split_axis=2, concat_axis=1, tiled=True)]
    ppermute x0 -> x4, starting transfers between devices: none -> 9.88 us  [local(): received.append(lax.ppermute(part, 'row', perm))]
    reshape x2 -> x0, local copies, waits for them, and re-layouts: 5.3 us -> none  [the longest x1 3.76 us: local(): packed = flux_y.reshape(planes, owned, 5 * length)]
    all_to_all x1 -> x0, other arithmetic: 5.24 us -> none  [local(): lax.all_to_all(packed, 'row', split_axis=2, concat_axis=1, tiled=True)]
  transfers between devices with their start and end apart: 1 -> 4, of which waited for: 1 -> 0; matrix products, arithmetic and copies ran while one was open for 3% -> 31% of each run, Pallas kernels for 0% -> 0%
where the time goes in v1:
time: 28.2 us; the launch traced here: 27.8 us
  starting transfers between devices  9.88 us (35%)
  matrix products  8.69 us (31%)
  local copies, waits for them, and re-layouts  5.82 us (21%)
  other arithmetic  3.15 us (11%)
  between operations  0.29 us (1%)
    ppermute x4, starting transfers between devices, local(): received.append(lax.ppermute(part, 'row', perm))  9.88 us
    dot_general x1, matrix products, compact_last(): jnp.einsum('...bj,jk->...bk', blocks, block_weights(count), precision=lax...  3.51 us
    unnamed x24, local copies, waits for them, and re-layouts  3.22 us
    dot_general x1, matrix products, local(): jnp.einsum('pr,rfzx->fzpx', spread, received, precision=hi)  3.19 us
    reshape x1, local copies, waits for them, and re-layouts, compact_last(): return result.reshape(field.shape)  1.48 us
    add x1, other arithmetic, compact_last(): jnp.roll(parts[..., :width], 1, axis=-2) + parts[..., width:2 * width]  1.46 us
    reduce_sum x1, other arithmetic, fluxes(): jnp.sum(momentum * momentum, axis=0)  1.38 us
    dot_general x1, matrix products, local(): jnp.einsum('pq,fzqx->fzpx', jnp.asarray(own), flux_y, precision=hi)  1.25 us
  transfers between devices with their start and end apart: 4, of which 0 were waited for; matrix products, arithmetic and copies ran while one was open for 31% of the time, Pallas kernels for 0%

profile of v1, /device:TPU:0, one launch (start us, length us, event | category | flops | bytes accessed | tf_op | source)
XLA Modules:
  0.0 27.8 jit_solution(8661733881052557079)
XLA Ops:
  0.0 0.0 copy-start
  0.0 1.0 %bitcast_dynamic-update-slice_fusion.9 = f32[5,1,32,2048]{3,2,0,1:T(8,128)S(1)} fusion(f32[3,1,32,2048]{3,2,1,0:T(8,128)} %param.8), kind=kLoop, calls=%fused_computation.33 | loop fusion | bytes 524288
  1.0 0.0 copy-start.1
  1.1 0.0 copy-start.2
  1.1 1.4 %multiply_reduce_fusion = (f32[32,2048]{1,0:T(8,128)S(1)}, f32[3,1,32,2048]{3,2,1,0:T(8,128)S(1)}) fusion(f32[3,1,32,2048]{3,2,1,0:T(8,128)} %param.8, f32[32,2048]{1,0:T(8,128)} %bitcast.130), kind=kLoop, calls=%fused_computation.12 | loop fusion | flops 524288 | bytes 2097152 | tf_op jit(solution)/shard_map/reduce_sum | solution.py:91
  2.5 0.0 copy-done
  2.5 0.0 copy-done.1
  2.5 0.0 copy-done.2
  2.5 0.1 bitcast_dynamic-update-slice_fusion.5
  2.6 0.0 copy-start.6
  2.7 0.6 %copy-done.6 = f32[8,32,1]{1,0,2:T(8,128)S(1)} copy-done((f32[8,32,1]{1,0,2:T(8,128)S(1)}, f32[8,32,1]{1,0,2:T(8,128)}, u32[]{:S(2)}) %copy-start.6) | copy-done | bytes 1048
  3.3 0.7 %fusion.5 = f32[8,5,2048]{2,0,1:T(8,128)S(1)} fusion(f32[8,32,1]{1,0,2:T(8,128)S(1)} %copy-done.6, f32[5,1,32,2048]{3,2,0,1:T(8,128)S(1)} %bitcast_dynamic-update-slice_fusion.6), kind=kOutput, calls=%fused_computation.8 | convolution fusion | flops 31457280 | bytes 1639424 | tf_op jit(solution)/shard_map/rq,fzqx->rfzx/dot_general | solution.py:123
  4.0 0.7 %slice_bitcast_fusion.4 = (f32[1,5,1,2048]{3,0,1,2:T(1,128)}, f32[1,5,1,2048]{3,0,1,2:T(1,128)}) fusion(f32[8,5,2048]{2,0,1:T(8,128)S(1)} %fusion.5), kind=kLoop, calls=%fused_computation.48 | loop fusion | bytes 163840 | tf_op jit(solution)/shard_map/slice | solution.py:127
  4.7 5.0 %collective-permute-start.1 = (f32[1,5,1,2048]{3,0,1,2:T(1,128)}, f32[1,5,1,2048]{3,0,1,2:T(1,128)}, u32[]{:S(2)}, u32[]{:S(2)}) collective-permute-start(f32[1,5,1,2048]{3,0,1,2:T(1,128)} %get-tuple-element.20), channel_id=1, source_target_pairs={{0,24},{4,28},{8,0},{12,4},{16,8},{20,12},{24,16},{28,20},{1,25},{... | collective-permute-start | bytes 122888 | tf_op jit(solution)/shard_map/ppermute | solution.py:130
  9.8 0.0 collective-permute-start.2
  9.8 0.1 slice_bitcast_fusion.2
  9.8 4.8 %collective-permute-start = (f32[3,5,1,2048]{3,0,1,2:T(4,128)S(1)}, f32[3,5,1,2048]{3,0,1,2:T(4,128)S(1)}, u32[]{:S(2)}, u32[]{:S(2)}) collective-permute-start(f32[3,5,1,2048]{3,0,1,2:T(4,128)S(1)} %get-tuple-element.18), channel_id=1, source_target_pairs={{0,28},{4,0},{8,4},{12,8},{16,12},{20,16},{24,20},{28,24},{1,29},{... | collective-permute-start | bytes 368648 | tf_op jit(solution)/shard_map/ppermute | solution.py:130
  14.7 0.0 collective-permute-start.3
  14.7 0.1 multiply_bitcast_fusion
  14.8 0.1 fusion.20
  15.1 0.0 copy-start.3
  15.3 0.8 %copy-done.3 = f32[128,384,1,1]{1,0,3,2:T(8,128)S(1)} copy-done((f32[128,384,1,1]{1,0,3,2:T(8,128)S(1)}, f32[128,384,1,1]{1,0,3,2:T(8,128)}, u32[]{:S(2)}) %copy-start.3) | copy-done | bytes 196632
  16.0 3.5 %convolution_bitcast_fusion = f32[5,1,32,16,384]{4,3,2,0,1:T(8,128)S(1)} fusion(f32[5,32,16,128]{3,2,1,0:T(8,128)S(1)} %bitcast_dynamic-update-slice_fusion, f32[128,384,1,1]{1,0,3,2:T(8,128)S(1)} %copy-done.3), kind=kOutput, calls=%fused_computation.5 | convolution fusion | flops 1509949440 | bytes 5439488 | tf_op jit(solution)/shard_map/...bj,jk->...bk/dot_general | solution.py:42
  19.5 0.1 fusion.24
  19.7 0.0 copy-start.4
  19.7 0.2 fusion.23
  19.9 0.5 %copy-done.4 = f32[32,32,1]{1,0,2:T(8,128)S(1)} copy-done((f32[32,32,1]{1,0,2:T(8,128)S(1)}, f32[32,32,1]{1,0,2:T(8,128)}, u32[]{:S(2)}) %copy-start.4) | copy-done | bytes 4120
  20.4 1.2 %fusion.7 = f32[5,2048,32]{1,2,0:T(8,128)S(1)} fusion(f32[32,32,1]{1,0,2:T(8,128)S(1)} %copy-done.4, f32[5,1,32,2048]{3,2,0,1:T(8,128)S(1)} %bitcast_dynamic-update-slice_fusion.6), kind=kOutput, calls=%fused_computation.10 | convolution fusion | flops 125829120 | bytes 2625536 | tf_op jit(solution)/shard_map/pq,fzqx->fzpx/dot_general | solution.py:133
  21.6 1.5 %fusion.4 = f32[5,1,32,16,128]{4,3,2,0,1:T(8,128)} fusion(f32[5,1,32,16,384]{4,3,2,0,1:T(8,128)S(1)} %convolution_bitcast_fusion, f32[5,1,32,15,128]{4,3,2,0,1:T(8,128)S(1)} %get-tuple-element.8, f32[5,1,32,1,128]{4,3,2,0,1:T(1,128)S(1)} %get-tuple-element.10, f32[5,1,32,1,128]{4,3,2,0,1:T(1,128)S(1)} %get-tuple-element.9, ...), kind=kLoop, calls=%fused_computation.7 | loop fusion | flops 1310720 | bytes 5242880 | tf_op jit(solution)/shard_map/add | solution.py:46
  23.1 0.0 copy-start.5
  23.1 1.5 %reshape.103 = f32[5,1,32,2048]{3,2,0,1:T(8,128)S(1)} reshape(f32[5,1,32,16,128]{4,3,2,0,1:T(8,128)} %fusion.4) | data formatting | bytes 2621440 | tf_op jit(solution)/shard_map/reshape | solution.py:50
  24.6 0.0 collective-permute-done.1
  24.6 0.0 collective-permute-done.2
  24.6 0.0 collective-permute-done
  24.6 0.0 collective-permute-done.3
  24.6 0.0 copy-done.5
  24.6 3.2 %fusion.3 = f32[5,1,32,2048]{3,2,1,0:T(8,128)} fusion(f32[5,1,32,2048]{3,2,0,1:T(8,128)S(1)} %reshape.103, f32[5,2048,32]{1,2,0:T(8,128)S(1)} %fusion.7, f32[32,8,1]{0,1,2:T(8,128)S(1)} %copy-done.5, f32[3,5,1,2048]{3,0,1,2:T(4,128)S(1)} %collective-permute-done.3, f32[1,5,1,2048]{3,0,1,2:T(1,128)} %collective-permute-done.2, ...), kind=kOutput, calls=%fused_computation.4 | convolution fusion | flops 32686080 | bytes 4260864 | tf_op jit(solution)/shard_map/pr,rfzx->fzpx/dot_general | solution.py:134
  (13 shorter events, 0.4 us)
Async XLA Ops:
  0.0 2.5 %copy-start = (f32[3,1,32,2048]{3,2,1,0:T(8,128)S(1)}, f32[3,1,32,2048]{3,2,1,0:T(8,128)}, u32[]{:S(2)}) copy-start(f32[3,1,32,2048]{3,2,1,0:T(8,128)} %param.8) | copy-start | bytes 2359300
  1.0 1.5 %copy-start.1 = (f32[1,32,2048]{2,1,0:T(8,128)S(1)}, f32[1,32,2048]{2,1,0:T(8,128)}, u32[]{:S(2)}) copy-start(f32[1,32,2048]{2,1,0:T(8,128)} %param.9) | copy-start | bytes 786436
  1.1 1.5 %copy-start.2 = (f32[1,32,2048]{2,1,0:T(8,128)S(1)}, f32[1,32,2048]{2,1,0:T(8,128)}, u32[]{:S(2)}) copy-start(f32[1,32,2048]{2,1,0:T(8,128)} %param.7) | copy-start | bytes 786436
  2.6 0.7 %copy-start.6 = (f32[8,32,1]{1,0,2:T(8,128)S(1)}, f32[8,32,1]{1,0,2:T(8,128)}, u32[]{:S(2)}) copy-start(f32[8,32,1]{1,0,2:T(8,128)} %constant.23) | copy-start | bytes 3076
  4.7 19.9 %collective-permute-start.1 = (f32[1,5,1,2048]{3,0,1,2:T(1,128)}, f32[1,5,1,2048]{3,0,1,2:T(1,128)}, u32[]{:S(2)}, u32[]{:S(2)}) collective-permute-start(f32[1,5,1,2048]{3,0,1,2:T(1,128)} %get-tuple-element.20), channel_id=1, source_target_pairs={{0,24},{4,28},{8,0},{12,4},{16,8},{20,12},{24,16},{28,20},{1,25},{... | collective-permute-start | bytes 122888 | tf_op jit(solution)/shard_map/ppermute | solution.py:130
  9.8 14.8 %collective-permute-start.2 = (f32[1,5,1,2048]{3,0,1,2:T(1,128)}, f32[1,5,1,2048]{3,0,1,2:T(1,128)}, u32[]{:S(2)}, u32[]{:S(2)}) collective-permute-start(f32[1,5,1,2048]{3,0,1,2:T(1,128)} %get-tuple-element.21), channel_id=1, source_target_pairs={{0,8},{4,12},{8,16},{12,20},{16,24},{20,28},{24,0},{28,4},{1,9},{5... | collective-permute-start | bytes 122888 | tf_op jit(solution)/shard_map/ppermute | solution.py:130
  9.8 14.8 %collective-permute-start = (f32[3,5,1,2048]{3,0,1,2:T(4,128)S(1)}, f32[3,5,1,2048]{3,0,1,2:T(4,128)S(1)}, u32[]{:S(2)}, u32[]{:S(2)}) collective-permute-start(f32[3,5,1,2048]{3,0,1,2:T(4,128)S(1)} %get-tuple-element.18), channel_id=1, source_target_pairs={{0,28},{4,0},{8,4},{12,8},{16,12},{20,16},{24,20},{28,24},{1,29},{... | collective-permute-start | bytes 368648 | tf_op jit(solution)/shard_map/ppermute | solution.py:130
  14.7 9.9 %collective-permute-start.3 = (f32[3,5,1,2048]{3,0,1,2:T(4,128)S(1)}, f32[3,5,1,2048]{3,0,1,2:T(4,128)S(1)}, u32[]{:S(2)}, u32[]{:S(2)}) collective-permute-start(f32[3,5,1,2048]{3,0,1,2:T(4,128)S(1)} %get-tuple-element.19), channel_id=1, source_target_pairs={{0,4},{4,8},{8,12},{12,16},{16,20},{20,24},{24,28},{28,0},{1,5},{5... | collective-permute-start | bytes 368648 | tf_op jit(solution)/shard_map/ppermute | solution.py:130
  15.1 0.9 %copy-start.3 = (f32[128,384,1,1]{1,0,3,2:T(8,128)S(1)}, f32[128,384,1,1]{1,0,3,2:T(8,128)}, u32[]{:S(2)}) copy-start(f32[128,384,1,1]{1,0,3,2:T(8,128)} %constant.21) | copy-start | bytes 589828
  19.7 0.7 %copy-start.4 = (f32[32,32,1]{1,0,2:T(8,128)S(1)}, f32[32,32,1]{1,0,2:T(8,128)}, u32[]{:S(2)}) copy-start(f32[32,32,1]{1,0,2:T(8,128)} %constant.22) | copy-start | bytes 12292
  23.1 1.5 %copy-start.5 = (f32[32,8,1]{0,1,2:T(8,128)S(1)}, f32[32,8,1]{0,1,2:T(8,128)}, u32[]{:S(2)}) copy-start(f32[32,8,1]{0,1,2:T(8,128)} %constant.24) | copy-start | bytes 3076

commit v2 on v1

v2 whole, which is shorter than its diff:
```python
import jax
import jax.numpy as jnp
import numpy as np
from jax import lax
from jax.experimental import pallas as pl
from jax.experimental.pallas import tpu as pltpu
from jax.sharding import PartitionSpec as P


def operator_column(count):
    steps = np.arange(count)
    wave = 2.0 * np.pi * steps / count
    upper = (
        17.0 / 12.0 * np.sin(wave)
        + 101.0 / 300.0 * np.sin(2.0 * wave)
        + 1.0 / 300.0 * np.sin(3.0 * wave)
    )
    lower = 1.0 + np.cos(wave) + 0.1 * np.cos(2.0 * wave)
    ratio = upper / lower
    phase = 2.0 * np.pi * (steps[:, None] * steps[None, :] % count) / count
    return -np.sum(ratio[:, None] * np.sin(phase), axis=0) / count


def operator_table(count):
    column = operator_column(count)
    steps = np.arange(count)
    offsets = (steps[None, :] - steps[:, None]) % count
    return column[offsets].astype(np.float32)


def block_weights(count):
    table = operator_table(count)
    width = 128
    w_self = table[:width, :width]
    w_prev = table[:width, width : 2 * width]
    w_next = table[width : 2 * width, :width]
    return jnp.asarray(np.concatenate([w_prev, w_self, w_next], axis=1))


def column_basis(block, tol=1e-12):
    rest = block.copy()
    basis = []
    while len(basis) < block.shape[1]:
        norms = np.sqrt(np.sum(rest * rest, axis=0))
        pick = int(np.argmax(norms))
        if norms[pick] <= tol:
            break
        vec = rest[:, pick].copy()
        for _ in range(2):
            for q in basis:
                vec = vec - np.sum(q * vec) * q
        vec = vec / np.sqrt(np.sum(vec * vec))
        basis.append(vec)
        rest = rest - vec[:, None] * np.sum(vec[:, None] * rest, axis=0)[None, :]
    return basis


def y_operator(rows, groups):
    count = rows * groups
    column = operator_column(count)
    steps = np.arange(count)
    full = column[(steps[:, None] - steps[None, :]) % count]
    own = full[:rows, :rows].astype(np.float32)
    shifts = []
    for e in range(1, groups):
        block = full[:rows, rows * e : rows * (e + 1)]
        basis = column_basis(block)
        if not basis:
            continue
        q = np.stack(basis, axis=1)
        w = np.sum(q[:, :, None] * block[:, None, :], axis=0)
        shifts.append((e, q.astype(np.float32), w.astype(np.float32)))
    return own, shifts


HI = lax.Precision.HIGHEST
WIDTH = 128


def dot(a, b):
    return jnp.dot(a, b, precision=HI, preferred_element_type=jnp.float32)


def plane_fluxes(rho_ref, mom_ref, energy_ref):
    rho = rho_ref[0]
    m_x = mom_ref[0, 0]
    m_y = mom_ref[1, 0]
    m_z = mom_ref[2, 0]
    energy = energy_ref[0]
    vel_x = m_x / rho
    vel_y = m_y / rho
    pressure = 0.4 * (energy - 0.5 * (m_x * m_x + m_y * m_y + m_z * m_z) / rho)
    enthalpy = energy + pressure
    flux_x = (m_x, m_x * vel_x + pressure, m_y * vel_x, m_z * vel_x, enthalpy * vel_x)
    flux_y = (m_y, m_x * vel_y, m_y * vel_y + pressure, m_z * vel_y, enthalpy * vel_y)
    return flux_x, flux_y


def moments_kernel(splits, weights_ref, rho_ref, mom_ref, energy_ref, *out_refs):
    _, flux_y = plane_fluxes(rho_ref, mom_ref, energy_ref)
    weights = weights_ref[...]
    for f in range(5):
        moments = dot(weights, flux_y[f])
        for (lo, hi), out_ref in zip(splits, out_refs):
            out_ref[0, f] = moments[lo:hi]


def tendency_kernel(count, wx_ref, own_ref, spread_ref, rho_ref, mom_ref, energy_ref, *refs):
    recv_refs, out_ref = refs[:-1], refs[-1]
    flux_x, flux_y = plane_fluxes(rho_ref, mom_ref, energy_ref)
    wx = wx_ref[...]
    own = own_ref[...]
    spread = spread_ref[...]
    nb = count // WIDTH
    for f in range(5):
        received = jnp.concatenate([r[0, f] for r in recv_refs], axis=0)
        d_y = dot(own, flux_y[f]) + dot(spread, received)
        fx = flux_x[f]
        rows = fx.shape[0]
        stacked = jnp.concatenate([fx[:, b * WIDTH : (b + 1) * WIDTH] for b in range(nb)], axis=0)
        parts = dot(stacked, wx)
        for b in range(nb):
            bp = (b - 1) % nb
            bn = (b + 1) % nb
            d_x = (
                parts[bp * rows : (bp + 1) * rows, :WIDTH]
                + parts[b * rows : (b + 1) * rows, WIDTH : 2 * WIDTH]
                + parts[bn * rows : (bn + 1) * rows, 2 * WIDTH :]
            )
            out_ref[f, 0, :, b * WIDTH : (b + 1) * WIDTH] = -(d_x + d_y[:, b * WIDTH : (b + 1) * WIDTH])


def full_spec(shape):
    return pl.BlockSpec(shape, lambda z: (0,) * len(shape))


def make_local(groups):
    def local(density, momentum, energy):
        planes, rows, count = density.shape
        own, shifts = y_operator(rows, groups)
        weights = np.concatenate([w for _, _, w in shifts], axis=0)
        spread = np.concatenate([q for _, q, _ in shifts], axis=1)
        splits = []
        lo = 0
        for _, _, w in shifts:
            splits.append((lo, lo + w.shape[0]))
            lo += w.shape[0]
        plane_specs = [
            pl.BlockSpec((1, rows, count), lambda z: (z, 0, 0)),
            pl.BlockSpec((3, 1, rows, count), lambda z: (0, z, 0, 0)),
            pl.BlockSpec((1, rows, count), lambda z: (z, 0, 0)),
        ]
        moment_shapes = [
            jax.ShapeDtypeStruct((planes, 5, hi - lo, count), jnp.float32) for lo, hi in splits
        ]
        moment_specs = [
            pl.BlockSpec((1, 5, hi - lo, count), lambda z: (z, 0, 0, 0)) for lo, hi in splits
        ]
        moments = pl.pallas_call(
            lambda *r: moments_kernel(splits, *r),
            grid=(planes,),
            in_specs=[full_spec(weights.shape)] + plane_specs,
            out_specs=moment_specs,
            out_shape=moment_shapes,
        )(jnp.asarray(weights), density, momentum, energy)
        received = [
            lax.ppermute(part, "row", [(j, (j - e) % groups) for j in range(groups)])
            for (e, _, _), part in zip(shifts, moments)
        ]
        wx = block_weights(count)
        return pl.pallas_call(
            lambda *r: tendency_kernel(count, *r),
            grid=(planes,),
            in_specs=[full_spec(wx.shape), full_spec(own.shape), full_spec(spread.shape)]
            + plane_specs
            + moment_specs,
            out_specs=pl.BlockSpec((5, 1, rows, count), lambda z: (0, z, 0, 0)),
            out_shape=jax.ShapeDtypeStruct((5, planes, rows, count), jnp.float32),
        )(wx, jnp.asarray(own), jnp.asarray(spread), density, momentum, energy, *received)

    return local


def solution(mesh):
    in_specs = (P("col", "row", None), P(None, "col", "row", None), P("col", "row", None))
    out_specs = P(None, "col", "row", None)
    return jax.shard_map(
        make_local(mesh.shape["row"]),
        mesh=mesh,
        in_specs=in_specs,
        out_specs=out_specs,
        check_vma=False,
    )
```

time: 28.2 us -> 27.1 us (0.961)
  Pallas kernels: 0 us -> 10.8 us
  matrix products: 8.69 us -> 0 us
  waiting for transfers between devices: 0.01 us -> 7.41 us
  local copies, waits for them, and re-layouts: 5.82 us -> 0.65 us
  other arithmetic: 3.15 us -> 0 us
  starting transfers between devices: 9.88 us -> 8.03 us
    pallas_call x0 -> x2, Pallas kernels: none -> 10.8 us  [the longest x1 7.83 us: local(): pl.pallas_call(lambda *r: tendency_kernel(count, *r), grid=(planes,), in_...]
    dot_general x4 -> x0, matrix products: 8.69 us -> none  [the longest x1 3.51 us: compact_last(): jnp.einsum('...bj,jk->...bk', blocks, block_weights(count), precision=lax...]
    ppermute x4, waiting for transfers between devices: 0.01 us -> 7.41 us  [local(): lax.ppermute(part, 'row', [(j, (j - e) % groups) for j in range(groups)])]
    unnamed x24 -> x8, local copies, waits for them, and re-layouts: 3.22 us -> 0.65 us
    ppermute x4, starting transfers between devices: 9.88 us -> 8.03 us  [local(): lax.ppermute(part, 'row', [(j, (j - e) % groups) for j in range(groups)])]
    reshape x1 -> x0, local copies, waits for them, and re-layouts: 1.48 us -> none  [compact_last(): return result.reshape(field.shape)]
    add x1 -> x0, other arithmetic: 1.46 us -> none  [compact_last(): jnp.roll(parts[..., :width], 1, axis=-2) + parts[..., width:2 * width]]
    reduce_sum x1 -> x0, other arithmetic: 1.38 us -> none  [fluxes(): jnp.sum(momentum * momentum, axis=0)]
  transfers between devices with their start and end apart: 4 -> 4, of which waited for: 0 -> 3; matrix products, arithmetic and copies ran while one was open for 31% -> 0% of each run, Pallas kernels for 0% -> 0%
where the time goes in v2:
time: 27.1 us; the launch traced here: 26.9 us
  Pallas kernels  10.8 us (40%)
  starting transfers between devices  8.03 us (30%)
  waiting for transfers between devices  7.41 us (27%)
  local copies, waits for them, and re-layouts  0.65 us (2%)
    ppermute x4, starting transfers between devices, local(): lax.ppermute(part, 'row', [(j, (j - e) % groups) for j in range(groups)])  8.03 us
    pallas_call x1, Pallas kernels, local(): pl.pallas_call(lambda *r: tendency_kernel(count, *r), grid=(planes,), in_...  7.83 us
    ppermute x4, waiting for transfers between devices, local(): lax.ppermute(part, 'row', [(j, (j - e) % groups) for j in range(groups)])  7.41 us
    pallas_call x1, Pallas kernels, local(): pl.pallas_call(lambda *r: moments_kernel(splits, *r), grid=(planes,), in_...  2.96 us
    unnamed x8, local copies, waits for them, and re-layouts  0.65 us
  transfers between devices with their start and end apart: 4, of which 3 were waited for; matrix products, arithmetic and copies ran while one was open for 0% of the time, Pallas kernels for 0%

profile of v2, /device:TPU:0, one launch (start us, length us, event | category | flops | bytes accessed | tf_op | source)
XLA Modules:
  0.0 26.9 jit_solution(11562841396694119114)
XLA Ops:
  0.0 3.0 %shard_map.73 = (f32[1,5,3,2048]{3,2,1,0:T(4,128)}, f32[1,5,1,2048]{3,2,1,0:T(1,128)}, f32[1,5,1,2048]{3,2,1,0:T(1,128)}, f32[1,5,3,2048]{3,2,1,0:T(4,128)}) custom-call(f32[8,32]{1,0:T(8,128)} %constant.8.clone.r_0_, f32[1,32,2048]{2,1,0:T(8,128)} %r_3_.3, f32[3,1,32,2048]{3,2,1,0:T(8,128)} %r_4_.1, f32[1,32,2048]{2,1,0:T(8,128)} %r_5_.1), custom_call_target="tpu_custom_call" | custom-call | tf_op jit(solution)/shard_map/pallas_call | solution.py:159
  3.0 6.0 %collective-permute-start = (f32[1,5,3,2048]{3,2,1,0:T(4,128)}, f32[1,5,3,2048]{3,2,1,0:T(4,128)S(1)}, u32[]{:S(2)}, u32[]{:S(2)}) collective-permute-start(f32[1,5,3,2048]{3,2,1,0:T(4,128)} %get-tuple-element.9), channel_id=1, source_target_pairs={{0,28},{4,0},{8,4},{12,8},{16,12},{20,16},{24,20},{28,24},{1,29},{... | collective-permute-start | bytes 368648 | tf_op jit(solution)/shard_map/ppermute | solution.py:167
  9.0 0.0 collective-permute-start.3
  9.0 1.1 %collective-permute-start.1 = (f32[1,5,1,2048]{3,2,1,0:T(1,128)}, f32[1,5,1,2048]{3,2,1,0:T(1,128)S(1)}, u32[]{:S(2)}, u32[]{:S(2)}) collective-permute-start(f32[1,5,1,2048]{3,2,1,0:T(1,128)} %get-tuple-element.10), channel_id=1, source_target_pairs={{0,24},{4,28},{8,0},{12,4},{16,8},{20,12},{24,16},{28,20},{1,25},{... | collective-permute-start | bytes 122888 | tf_op jit(solution)/shard_map/ppermute | solution.py:167
  10.0 1.0 %collective-permute-start.2 = (f32[1,5,1,2048]{3,2,1,0:T(1,128)}, f32[1,5,1,2048]{3,2,1,0:T(1,128)S(1)}, u32[]{:S(2)}, u32[]{:S(2)}) collective-permute-start(f32[1,5,1,2048]{3,2,1,0:T(1,128)} %get-tuple-element.11), channel_id=1, source_target_pairs={{0,8},{4,12},{8,16},{12,20},{16,24},{20,28},{24,0},{28,4},{1,9},{5... | collective-permute-start | bytes 122888 | tf_op jit(solution)/shard_map/ppermute | solution.py:167
  11.0 3.1 %collective-permute-done.1.r_7_ = f32[1,5,1,2048]{3,2,1,0:T(1,128)S(1)} collective-permute-done((f32[1,5,1,2048]{3,2,1,0:T(1,128)}, f32[1,5,1,2048]{3,2,1,0:T(1,128)S(1)}, u32[]{:S(2)}, u32[]{:S(2)}) %collective-permute-start.1) | collective-permute-done | bytes 40992 | tf_op jit(solution)/shard_map/ppermute | solution.py:167
  14.1 0.0 copy-start.2
  14.1 1.9 %collective-permute-done.2.r_8_ = f32[1,5,1,2048]{3,2,1,0:T(1,128)S(1)} collective-permute-done((f32[1,5,1,2048]{3,2,1,0:T(1,128)}, f32[1,5,1,2048]{3,2,1,0:T(1,128)S(1)}, u32[]{:S(2)}, u32[]{:S(2)}) %collective-permute-start.2) | collective-permute-done | bytes 40992 | tf_op jit(solution)/shard_map/ppermute | solution.py:167
  16.0 0.0 copy-start.3
  16.0 0.0 collective-permute-done.r_6_
  16.1 0.0 copy-start
  16.1 2.4 %collective-permute-done.3.r_9_ = f32[1,5,3,2048]{3,2,1,0:T(4,128)S(1)} collective-permute-done((f32[1,5,3,2048]{3,2,1,0:T(4,128)}, f32[1,5,3,2048]{3,2,1,0:T(4,128)S(1)}, u32[]{:S(2)}, u32[]{:S(2)}) %collective-permute-start.3) | collective-permute-done | bytes 122912 | tf_op jit(solution)/shard_map/ppermute | solution.py:167
  18.4 0.0 copy-done.2
  18.4 0.0 copy-done.3
  18.4 0.0 copy-done
  18.4 0.0 copy-start.1
  18.4 0.6 %copy-done.1 = f32[1,5,3,2048]{3,2,1,0:T(4,128)} copy-done((f32[1,5,3,2048]{3,2,1,0:T(4,128)}, f32[1,5,3,2048]{3,2,1,0:T(4,128)S(1)}, u32[]{:S(2)}) %copy-start.1) | copy-done | bytes 122904
  19.1 7.8 %shard_map.74 = f32[5,1,32,2048]{3,2,1,0:T(8,128)} custom-call(f32[128,384]{1,0:T(8,128)} %constant.9.clone.r_0_, f32[32,32]{1,0:T(8,128)} %constant.10.clone.r_1_, f32[32,8]{1,0:T(8,128)} %constant.11.clone.r_2_, f32[1,32,2048]{2,1,0:T(8,128)} %r_3_.3, f32[3,1,32,2048]{3,2,1,0:T(8,128)} %r_4_.1, f32[1,32,2048]{2,1,0:T(8,128)} %r_5_.1, ...), custom_call_target="tpu_custom_call" | custom-call | tf_op jit(solution)/shard_map/pallas_call | solution.py:171
Async XLA Ops:
  3.0 13.1 %collective-permute-start = (f32[1,5,3,2048]{3,2,1,0:T(4,128)}, f32[1,5,3,2048]{3,2,1,0:T(4,128)S(1)}, u32[]{:S(2)}, u32[]{:S(2)}) collective-permute-start(f32[1,5,3,2048]{3,2,1,0:T(4,128)} %get-tuple-element.9), channel_id=1, source_target_pairs={{0,28},{4,0},{8,4},{12,8},{16,12},{20,16},{24,20},{28,24},{1,29},{... | collective-permute-start | bytes 368648 | tf_op jit(solution)/shard_map/ppermute | solution.py:167
  9.0 9.4 %collective-permute-start.3 = (f32[1,5,3,2048]{3,2,1,0:T(4,128)}, f32[1,5,3,2048]{3,2,1,0:T(4,128)S(1)}, u32[]{:S(2)}, u32[]{:S(2)}) collective-permute-start(f32[1,5,3,2048]{3,2,1,0:T(4,128)} %get-tuple-element.12), channel_id=1, source_target_pairs={{0,4},{4,8},{8,12},{12,16},{16,20},{20,24},{24,28},{28,0},{1,5},{5... | collective-permute-start | bytes 368648 | tf_op jit(solution)/shard_map/ppermute | solution.py:167
  9.0 5.1 %collective-permute-start.1 = (f32[1,5,1,2048]{3,2,1,0:T(1,128)}, f32[1,5,1,2048]{3,2,1,0:T(1,128)S(1)}, u32[]{:S(2)}, u32[]{:S(2)}) collective-permute-start(f32[1,5,1,2048]{3,2,1,0:T(1,128)} %get-tuple-element.10), channel_id=1, source_target_pairs={{0,24},{4,28},{8,0},{12,4},{16,8},{20,12},{24,16},{28,20},{1,25},{... | collective-permute-start | bytes 122888 | tf_op jit(solution)/shard_map/ppermute | solution.py:167
  10.0 6.0 %collective-permute-start.2 = (f32[1,5,1,2048]{3,2,1,0:T(1,128)}, f32[1,5,1,2048]{3,2,1,0:T(1,128)S(1)}, u32[]{:S(2)}, u32[]{:S(2)}) collective-permute-start(f32[1,5,1,2048]{3,2,1,0:T(1,128)} %get-tuple-element.11), channel_id=1, source_target_pairs={{0,8},{4,12},{8,16},{12,20},{16,24},{20,28},{24,0},{28,4},{1,9},{5... | collective-permute-start | bytes 122888 | tf_op jit(solution)/shard_map/ppermute | solution.py:167
  14.1 4.3 %copy-start.2 = (f32[1,5,1,2048]{3,2,1,0:T(1,128)}, f32[1,5,1,2048]{3,2,1,0:T(1,128)S(1)}, u32[]{:S(2)}) copy-start(f32[1,5,1,2048]{3,2,1,0:T(1,128)S(1)} %collective-permute-done.1.r_7_) | copy-start | bytes 122884
  16.0 2.4 %copy-start.3 = (f32[1,5,1,2048]{3,2,1,0:T(1,128)}, f32[1,5,1,2048]{3,2,1,0:T(1,128)S(1)}, u32[]{:S(2)}) copy-start(f32[1,5,1,2048]{3,2,1,0:T(1,128)S(1)} %collective-permute-done.2.r_8_) | copy-start | bytes 122884
  16.1 2.4 %copy-start = (f32[1,5,3,2048]{3,2,1,0:T(4,128)}, f32[1,5,3,2048]{3,2,1,0:T(4,128)S(1)}, u32[]{:S(2)}) copy-start(f32[1,5,3,2048]{3,2,1,0:T(4,128)S(1)} %collective-permute-done.r_6_) | copy-start | bytes 368644
  18.4 0.7 %copy-start.1 = (f32[1,5,3,2048]{3,2,1,0:T(4,128)}, f32[1,5,3,2048]{3,2,1,0:T(4,128)S(1)}, u32[]{:S(2)}) copy-start(f32[1,5,3,2048]{3,2,1,0:T(4,128)S(1)} %collective-permute-done.3.r_9_) | copy-start | bytes 368644

commit v3 on v2

--- a/solution.py
+++ b/solution.py
@@ -105,16 +105,13 @@
             out_ref[0, f] = moments[lo:hi]
 
 
-def tendency_kernel(count, wx_ref, own_ref, spread_ref, rho_ref, mom_ref, energy_ref, *refs):
-    recv_refs, out_ref = refs[:-1], refs[-1]
+def local_kernel(count, wx_ref, own_ref, rho_ref, mom_ref, energy_ref, out_ref):
     flux_x, flux_y = plane_fluxes(rho_ref, mom_ref, energy_ref)
     wx = wx_ref[...]
     own = own_ref[...]
-    spread = spread_ref[...]
     nb = count // WIDTH
     for f in range(5):
-        received = jnp.concatenate([r[0, f] for r in recv_refs], axis=0)
-        d_y = dot(own, flux_y[f]) + dot(spread, received)
+        d_y = dot(own, flux_y[f])
         fx = flux_x[f]
         rows = fx.shape[0]
         stacked = jnp.concatenate([fx[:, b * WIDTH : (b + 1) * WIDTH] for b in range(nb)], axis=0)
@@ -128,6 +125,14 @@
                 + parts[bn * rows : (bn + 1) * rows, 2 * WIDTH :]
             )
             out_ref[f, 0, :, b * WIDTH : (b + 1) * WIDTH] = -(d_x + d_y[:, b * WIDTH : (b + 1) * WIDTH])
+
+
+def correct_kernel(spread_ref, partial_ref, *refs):
+    recv_refs, out_ref = refs[:-1], refs[-1]
+    spread = spread_ref[...]
+    for f in range(5):
+        received = jnp.concatenate([r[0, f] for r in recv_refs], axis=0)
+        out_ref[f, 0] = partial_ref[f, 0] - dot(spread, received)
 
 
 def full_spec(shape):
@@ -168,15 +173,23 @@
             for (e, _, _), part in zip(shifts, moments)
         ]
         wx = block_weights(count)
+        out_spec = pl.BlockSpec((5, 1, rows, count), lambda z: (0, z, 0, 0))
+        out_shape = jax.ShapeDtypeStruct((5, planes, rows, count), jnp.float32)
+        partial = pl.pallas_call(
+            lambda *r: local_kernel(count, *r),
+            grid=(planes,),
+            in_specs=[full_spec(wx.shape), full_spec(own.shape)] + plane_specs,
+            out_specs=out_spec,
+            out_shape=out_shape,
+        )(wx, jnp.asarray(own), density, momentum, energy)
         return pl.pallas_call(
-            lambda *r: tendency_kernel(count, *r),
+            correct_kernel,
             grid=(planes,),
-            in_specs=[full_spec(wx.shape), full_spec(own.shape), full_spec(spread.shape)]
-            + plane_specs
-            + moment_specs,
-            out_specs=pl.BlockSpec((5, 1, rows, count), lambda z: (0, z, 0, 0)),
-            out_shape=jax.ShapeDtypeStruct((5, planes, rows, count), jnp.float32),
-        )(wx, jnp.asarray(own), jnp.asarray(spread), density, momentum, energy, *received)
+            in_specs=[full_spec(spread.shape), out_spec] + moment_specs,
+            out_specs=out_spec,
+            out_shape=out_shape,
+            input_output_aliases={1: 0},
+        )(jnp.asarray(spread), partial, *received)
 
     return local
 

time: 27.1 us -> 23.4 us (0.86)
  the two profiles are of different devices: /device:TPU:0 before, /device:TPU:30 now
where the time goes in v3:
time: 23.4 us; the launch traced here: 23.2 us
  Pallas kernels  13.3 us (57%)
  starting transfers between devices  8.55 us (37%)
  local copies, waits for them, and re-layouts  1.3 us (6%)
    ppermute x4, starting transfers between devices, local(): lax.ppermute(part, 'row', [(j, (j - e) % groups) for j in range(groups)])  8.55 us
    pallas_call x1, Pallas kernels, local(): pl.pallas_call(lambda *r: local_kernel(count, *r), grid=(planes,), in_spe...  6.69 us
    pallas_call x1, Pallas kernels, local(): pl.pallas_call(correct_kernel, grid=(planes,), in_specs=[full_spec(spread...  3.63 us
    pallas_call x1, Pallas kernels, local(): pl.pallas_call(lambda *r: moments_kernel(splits, *r), grid=(planes,), in_...  2.97 us
    unnamed x8, local copies, waits for them, and re-layouts  1.3 us
  transfers between devices with their start and end apart: 4, of which 0 were waited for; matrix products, arithmetic and copies ran while one was open for 0% of the time, Pallas kernels for 29%

profile of v3, /device:TPU:30, one launch (start us, length us, event | category | flops | bytes accessed | tf_op | source)
XLA Modules:
  0.0 23.2 jit_solution(2423063966907019934)
XLA Ops:
  0.0 3.0 %shard_map.74 = (f32[1,5,3,2048]{3,2,1,0:T(4,128)}, f32[1,5,1,2048]{3,2,1,0:T(1,128)}, f32[1,5,1,2048]{3,2,1,0:T(1,128)}, f32[1,5,3,2048]{3,2,1,0:T(4,128)}) custom-call(f32[8,32]{1,0:T(8,128)} %constant.8.clone.r_0_, f32[1,32,2048]{2,1,0:T(8,128)} %r_1_.2, f32[3,1,32,2048]{3,2,1,0:T(8,128)} %r_2_.3, f32[1,32,2048]{2,1,0:T(8,128)} %r_3_.3), custom_call_target="tpu_custom_call" | custom-call | tf_op jit(solution)/shard_map/pallas_call | solution.py:164
  3.0 0.5 %collective-permute-start = (f32[1,5,3,2048]{3,2,1,0:T(4,128)}, f32[1,5,3,2048]{3,2,1,0:T(4,128)S(1)}, u32[]{:S(2)}, u32[]{:S(2)}) collective-permute-start(f32[1,5,3,2048]{3,2,1,0:T(4,128)} %get-tuple-element.9), channel_id=1, source_target_pairs={{0,28},{4,0},{8,4},{12,8},{16,12},{20,16},{24,20},{28,24},{1,29},{... | collective-permute-start | bytes 368648 | tf_op jit(solution)/shard_map/ppermute | solution.py:172
  3.5 4.2 %collective-permute-start.3 = (f32[1,5,3,2048]{3,2,1,0:T(4,128)}, f32[1,5,3,2048]{3,2,1,0:T(4,128)S(1)}, u32[]{:S(2)}, u32[]{:S(2)}) collective-permute-start(f32[1,5,3,2048]{3,2,1,0:T(4,128)} %get-tuple-element.12), channel_id=1, source_target_pairs={{0,4},{4,8},{8,12},{12,16},{16,20},{20,24},{24,28},{28,0},{1,5},{5... | collective-permute-start | bytes 368648 | tf_op jit(solution)/shard_map/ppermute | solution.py:172
  7.7 0.0 collective-permute-start.1
  7.7 3.8 %collective-permute-start.2 = (f32[1,5,1,2048]{3,2,1,0:T(1,128)}, f32[1,5,1,2048]{3,2,1,0:T(1,128)S(1)}, u32[]{:S(2)}, u32[]{:S(2)}) collective-permute-start(f32[1,5,1,2048]{3,2,1,0:T(1,128)} %get-tuple-element.11), channel_id=1, source_target_pairs={{0,8},{4,12},{8,16},{12,20},{16,24},{20,28},{24,0},{28,4},{1,9},{5... | collective-permute-start | bytes 122888 | tf_op jit(solution)/shard_map/ppermute | solution.py:172
  11.5 6.7 %shard_map.73.partial_ref = f32[5,1,32,2048]{3,2,1,0:T(8,128)} custom-call(f32[128,384]{1,0:T(8,128)} %constant.9.clone.r_0_, f32[32,32]{1,0:T(8,128)} %constant.10.clone.r_1_, f32[1,32,2048]{2,1,0:T(8,128)} %r_1_.2, f32[3,1,32,2048]{3,2,1,0:T(8,128)} %r_2_.3, f32[1,32,2048]{2,1,0:T(8,128)} %r_3_.3), custom_call_target="tpu_custom_call" | custom-call | tf_op jit(solution)/shard_map/pallas_call | solution.py:178
  18.2 0.0 collective-permute-done.1.refs_1_
  18.2 0.0 copy-start.2
  18.2 0.0 collective-permute-done.2.refs_2_
  18.2 0.0 copy-start.3
  18.2 0.0 collective-permute-done.refs_0_
  18.2 0.0 copy-start
  18.2 0.0 collective-permute-done.3.refs_3_
  18.3 0.6 %copy-done.2 = f32[1,5,1,2048]{3,2,1,0:T(1,128)} copy-done((f32[1,5,1,2048]{3,2,1,0:T(1,128)}, f32[1,5,1,2048]{3,2,1,0:T(1,128)S(1)}, u32[]{:S(2)}) %copy-start.2) | copy-done | bytes 40984
  18.8 0.0 copy-done.3
  18.9 0.1 copy-done
  18.9 0.0 copy-start.1
  18.9 0.6 %copy-done.1 = f32[1,5,3,2048]{3,2,1,0:T(4,128)} copy-done((f32[1,5,3,2048]{3,2,1,0:T(4,128)}, f32[1,5,3,2048]{3,2,1,0:T(4,128)S(1)}, u32[]{:S(2)}) %copy-start.1) | copy-done | bytes 122904
  19.6 3.6 %shard_map.75 = f32[5,1,32,2048]{3,2,1,0:T(8,128)} custom-call(f32[32,8]{1,0:T(8,128)} %constant.11.clone.spread_ref, f32[5,1,32,2048]{3,2,1,0:T(8,128)} %shard_map.73.partial_ref, f32[1,5,3,2048]{3,2,1,0:T(4,128)} %copy-done, f32[1,5,1,2048]{3,2,1,0:T(1,128)} %copy-done.2, f32[1,5,1,2048]{3,2,1,0:T(1,128)} %copy-done.3, ...), custom_call_target="tpu_custom_call", output_to_operand_aliasing={{}: (1, {})} | custom-call | tf_op jit(solution)/shard_map/pallas_call | solution.py:185
Async XLA Ops:
  3.0 15.3 %collective-permute-start = (f32[1,5,3,2048]{3,2,1,0:T(4,128)}, f32[1,5,3,2048]{3,2,1,0:T(4,128)S(1)}, u32[]{:S(2)}, u32[]{:S(2)}) collective-permute-start(f32[1,5,3,2048]{3,2,1,0:T(4,128)} %get-tuple-element.9), channel_id=1, source_target_pairs={{0,28},{4,0},{8,4},{12,8},{16,12},{20,16},{24,20},{28,24},{1,29},{... | collective-permute-start | bytes 368648 | tf_op jit(solution)/shard_map/ppermute | solution.py:172
  3.5 14.8 %collective-permute-start.3 = (f32[1,5,3,2048]{3,2,1,0:T(4,128)}, f32[1,5,3,2048]{3,2,1,0:T(4,128)S(1)}, u32[]{:S(2)}, u32[]{:S(2)}) collective-permute-start(f32[1,5,3,2048]{3,2,1,0:T(4,128)} %get-tuple-element.12), channel_id=1, source_target_pairs={{0,4},{4,8},{8,12},{12,16},{16,20},{20,24},{24,28},{28,0},{1,5},{5... | collective-permute-start | bytes 368648 | tf_op jit(solution)/shard_map/ppermute | solution.py:172
  7.7 10.5 %collective-permute-start.1 = (f32[1,5,1,2048]{3,2,1,0:T(1,128)}, f32[1,5,1,2048]{3,2,1,0:T(1,128)S(1)}, u32[]{:S(2)}, u32[]{:S(2)}) collective-permute-start(f32[1,5,1,2048]{3,2,1,0:T(1,128)} %get-tuple-element.10), channel_id=1, source_target_pairs={{0,24},{4,28},{8,0},{12,4},{16,8},{20,12},{24,16},{28,20},{1,25},{... | collective-permute-start | bytes 122888 | tf_op jit(solution)/shard_map/ppermute | solution.py:172
  7.7 10.5 %collective-permute-start.2 = (f32[1,5,1,2048]{3,2,1,0:T(1,128)}, f32[1,5,1,2048]{3,2,1,0:T(1,128)S(1)}, u32[]{:S(2)}, u32[]{:S(2)}) collective-permute-start(f32[1,5,1,2048]{3,2,1,0:T(1,128)} %get-tuple-element.11), channel_id=1, source_target_pairs={{0,8},{4,12},{8,16},{12,20},{16,24},{20,28},{24,0},{28,4},{1,9},{5... | collective-permute-start | bytes 122888 | tf_op jit(solution)/shard_map/ppermute | solution.py:172
  18.2 0.6 %copy-start.2 = (f32[1,5,1,2048]{3,2,1,0:T(1,128)}, f32[1,5,1,2048]{3,2,1,0:T(1,128)S(1)}, u32[]{:S(2)}) copy-start(f32[1,5,1,2048]{3,2,1,0:T(1,128)S(1)} %collective-permute-done.1.refs_1_) | copy-start | bytes 122884
  18.2 0.6 %copy-start.3 = (f32[1,5,1,2048]{3,2,1,0:T(1,128)}, f32[1,5,1,2048]{3,2,1,0:T(1,128)S(1)}, u32[]{:S(2)}) copy-start(f32[1,5,1,2048]{3,2,1,0:T(1,128)S(1)} %collective-permute-done.2.refs_2_) | copy-start | bytes 122884
  18.2 0.7 %copy-start = (f32[1,5,3,2048]{3,2,1,0:T(4,128)}, f32[1,5,3,2048]{3,2,1,0:T(4,128)S(1)}, u32[]{:S(2)}) copy-start(f32[1,5,3,2048]{3,2,1,0:T(4,128)S(1)} %collective-permute-done.refs_0_) | copy-start | bytes 368644
  18.9 0.6 %copy-start.1 = (f32[1,5,3,2048]{3,2,1,0:T(4,128)}, f32[1,5,3,2048]{3,2,1,0:T(4,128)S(1)}, u32[]{:S(2)}) copy-start(f32[1,5,3,2048]{3,2,1,0:T(4,128)S(1)} %collective-permute-done.3.refs_3_) | copy-start | bytes 368644

commit v4 on v3

--- a/solution.py
+++ b/solution.py
@@ -127,12 +127,15 @@
             out_ref[f, 0, :, b * WIDTH : (b + 1) * WIDTH] = -(d_x + d_y[:, b * WIDTH : (b + 1) * WIDTH])
 
 
-def correct_kernel(spread_ref, partial_ref, *refs):
-    recv_refs, out_ref = refs[:-1], refs[-1]
-    spread = spread_ref[...]
-    for f in range(5):
-        received = jnp.concatenate([r[0, f] for r in recv_refs], axis=0)
-        out_ref[f, 0] = partial_ref[f, 0] - dot(spread, received)
+def correct_kernel(nrecv, partial_ref, *refs):
+    spread_refs, recv_refs, out_ref = refs[:nrecv], refs[nrecv:-1], refs[-1]
+    acc = partial_ref[0, 0]
+    for spread_ref, recv_ref in zip(spread_refs, recv_refs):
+        spread = spread_ref[...]
+        received = recv_ref[0, 0]
+        for r in range(received.shape[0]):
+            acc = acc - spread[:, r : r + 1] * received[r : r + 1, :]
+    out_ref[0, 0] = acc
 
 
 def full_spec(shape):
@@ -144,7 +147,6 @@
         planes, rows, count = density.shape
         own, shifts = y_operator(rows, groups)
         weights = np.concatenate([w for _, _, w in shifts], axis=0)
-        spread = np.concatenate([q for _, q, _ in shifts], axis=1)
         splits = []
         lo = 0
         for _, _, w in shifts:
@@ -155,17 +157,22 @@
             pl.BlockSpec((3, 1, rows, count), lambda z: (0, z, 0, 0)),
             pl.BlockSpec((1, rows, count), lambda z: (z, 0, 0)),
         ]
+        chunk = 512 if count % 512 == 0 else count
+        chunk_specs = [
+            pl.BlockSpec((1, rows, chunk), lambda z, c: (z, 0, c)),
+            pl.BlockSpec((3, 1, rows, chunk), lambda z, c: (0, z, 0, c)),
+            pl.BlockSpec((1, rows, chunk), lambda z, c: (z, 0, c)),
+        ]
         moment_shapes = [
             jax.ShapeDtypeStruct((planes, 5, hi - lo, count), jnp.float32) for lo, hi in splits
         ]
-        moment_specs = [
-            pl.BlockSpec((1, 5, hi - lo, count), lambda z: (z, 0, 0, 0)) for lo, hi in splits
-        ]
         moments = pl.pallas_call(
             lambda *r: moments_kernel(splits, *r),
-            grid=(planes,),
-            in_specs=[full_spec(weights.shape)] + plane_specs,
-            out_specs=moment_specs,
+            grid=(planes, count // chunk),
+            in_specs=[pl.BlockSpec(weights.shape, lambda z, c: (0, 0))] + chunk_specs,
+            out_specs=[
+                pl.BlockSpec((1, 5, hi - lo, chunk), lambda z, c: (z, 0, 0, c)) for lo, hi in splits
+            ],
             out_shape=moment_shapes,
         )(jnp.asarray(weights), density, momentum, energy)
         received = [
@@ -182,14 +189,21 @@
             out_specs=out_spec,
             out_shape=out_shape,
         )(wx, jnp.asarray(own), density, momentum, energy)
+        field_spec = pl.BlockSpec((1, 1, rows, count), lambda z, f: (f, z, 0, 0))
+        spreads = [jnp.asarray(q) for _, q, _ in shifts]
         return pl.pallas_call(
-            correct_kernel,
-            grid=(planes,),
-            in_specs=[full_spec(spread.shape), out_spec] + moment_specs,
-            out_specs=out_spec,
+            lambda *r: correct_kernel(len(shifts), *r),
+            grid=(planes, 5),
+            in_specs=[field_spec]
+            + [pl.BlockSpec(q.shape, lambda z, f: (0, 0)) for q in spreads]
+            + [
+                pl.BlockSpec((1, 1, hi - lo, count), lambda z, f: (z, f, 0, 0))
+                for lo, hi in splits
+            ],
+            out_specs=field_spec,
             out_shape=out_shape,
-            input_output_aliases={1: 0},
-        )(jnp.asarray(spread), partial, *received)
+            input_output_aliases={0: 0},
+        )(partial, *spreads, *received)
 
     return local
 

time: 23.4 us -> 25.7 us (1.098)
  the two profiles are of different devices: /device:TPU:30 before, /device:TPU:28 now
where the time goes in v4:
time: 25.7 us; the launch traced here: 25.4 us
  Pallas kernels  15.4 us (60%)
  starting transfers between devices  8.58 us (33%)
  local copies, waits for them, and re-layouts  1.3 us (5%)
    ppermute x4, starting transfers between devices, local(): lax.ppermute(part, 'row', [(j, (j - e) % groups) for j in range(groups)])  8.58 us
    pallas_call x1, Pallas kernels, local(): pl.pallas_call(lambda *r: local_kernel(count, *r), grid=(planes,), in_spe...  6.69 us
    pallas_call x1, Pallas kernels, local(): pl.pallas_call(lambda *r: correct_kernel(len(shifts), *r), grid=(planes,...  4.83 us
    pallas_call x1, Pallas kernels, local(): pl.pallas_call(lambda *r: moments_kernel(splits, *r), grid=(planes, count...  3.93 us
    unnamed x8, local copies, waits for them, and re-layouts  1.3 us
  transfers between devices with their start and end apart: 4, of which 0 were waited for; matrix products, arithmetic and copies ran while one was open for 0% of the time, Pallas kernels for 26%

profile of v4, /device:TPU:28, one launch (start us, length us, event | category | flops | bytes accessed | tf_op | source)
XLA Modules:
  0.0 25.4 jit_solution(871018080681785964)
XLA Ops:
  0.0 3.9 %shard_map.101 = (f32[1,5,3,2048]{3,2,1,0:T(4,128)}, f32[1,5,1,2048]{3,2,1,0:T(1,128)}, f32[1,5,1,2048]{3,2,1,0:T(1,128)}, f32[1,5,3,2048]{3,2,1,0:T(4,128)}) custom-call(f32[8,32]{1,0:T(8,128)} %constant.14.clone.r_0_, f32[1,32,2048]{2,1,0:T(8,128)} %r_1_.3, f32[3,1,32,2048]{3,2,1,0:T(8,128)} %r_2_.4, f32[1,32,2048]{2,1,0:T(8,128)} %r_3_.4), custom_call_target="tpu_custom_call" | custom-call | tf_op jit(solution)/shard_map/pallas_call | solution.py:169
  3.9 0.5 %collective-permute-start = (f32[1,5,3,2048]{3,2,1,0:T(4,128)}, f32[1,5,3,2048]{3,2,1,0:T(4,128)S(1)}, u32[]{:S(2)}, u32[]{:S(2)}) collective-permute-start(f32[1,5,3,2048]{3,2,1,0:T(4,128)} %get-tuple-element.9), channel_id=1, source_target_pairs={{0,28},{4,0},{8,4},{12,8},{16,12},{20,16},{24,20},{28,24},{1,29},{... | collective-permute-start | bytes 368648 | tf_op jit(solution)/shard_map/ppermute | solution.py:179
  4.5 4.2 %collective-permute-start.3 = (f32[1,5,3,2048]{3,2,1,0:T(4,128)}, f32[1,5,3,2048]{3,2,1,0:T(4,128)S(1)}, u32[]{:S(2)}, u32[]{:S(2)}) collective-permute-start(f32[1,5,3,2048]{3,2,1,0:T(4,128)} %get-tuple-element.12), channel_id=1, source_target_pairs={{0,4},{4,8},{8,12},{12,16},{16,20},{20,24},{24,28},{28,0},{1,5},{5... | collective-permute-start | bytes 368648 | tf_op jit(solution)/shard_map/ppermute | solution.py:179
  8.7 0.0 collective-permute-start.1
  8.7 3.8 %collective-permute-start.2 = (f32[1,5,1,2048]{3,2,1,0:T(1,128)}, f32[1,5,1,2048]{3,2,1,0:T(1,128)S(1)}, u32[]{:S(2)}, u32[]{:S(2)}) collective-permute-start(f32[1,5,1,2048]{3,2,1,0:T(1,128)} %get-tuple-element.11), channel_id=1, source_target_pairs={{0,8},{4,12},{8,16},{12,20},{16,24},{20,28},{24,0},{28,4},{1,9},{5... | collective-permute-start | bytes 122888 | tf_op jit(solution)/shard_map/ppermute | solution.py:179
  12.5 6.7 %shard_map.100.r_0_ = f32[5,1,32,2048]{3,2,1,0:T(8,128)} custom-call(f32[128,384]{1,0:T(8,128)} %constant.15.clone.r_0_, f32[32,32]{1,0:T(8,128)} %constant.16.clone.r_1_, f32[1,32,2048]{2,1,0:T(8,128)} %r_1_.3, f32[3,1,32,2048]{3,2,1,0:T(8,128)} %r_2_.4, f32[1,32,2048]{2,1,0:T(8,128)} %r_3_.4), custom_call_target="tpu_custom_call" | custom-call | tf_op jit(solution)/shard_map/pallas_call | solution.py:185
  19.2 0.0 collective-permute-done.1.r_6_
  19.2 0.0 copy-start.2
  19.2 0.0 collective-permute-done.2.r_7_
  19.2 0.0 copy-start.3
  19.2 0.0 collective-permute-done.r_5_
  19.2 0.0 copy-start
  19.2 0.0 collective-permute-done.3.r_8_
  19.3 0.6 %copy-done.2 = f32[1,5,1,2048]{3,2,1,0:T(1,128)} copy-done((f32[1,5,1,2048]{3,2,1,0:T(1,128)}, f32[1,5,1,2048]{3,2,1,0:T(1,128)S(1)}, u32[]{:S(2)}) %copy-start.2) | copy-done | bytes 40984
  19.8 0.0 copy-done.3
  19.9 0.1 copy-done
  19.9 0.0 copy-start.1
  19.9 0.6 %copy-done.1 = f32[1,5,3,2048]{3,2,1,0:T(4,128)} copy-done((f32[1,5,3,2048]{3,2,1,0:T(4,128)}, f32[1,5,3,2048]{3,2,1,0:T(4,128)S(1)}, u32[]{:S(2)}) %copy-start.1) | copy-done | bytes 122904
  20.6 4.8 %shard_map.102 = f32[5,1,32,2048]{3,2,1,0:T(8,128)} custom-call(f32[5,1,32,2048]{3,2,1,0:T(8,128)} %shard_map.100.r_0_, f32[32,3]{1,0:T(8,128)} %constant.17.clone.r_1_, f32[32,1]{1,0:T(8,128)} %constant.18.clone.r_2_, f32[32,1]{1,0:T(8,128)} %constant.19.clone.r_3_, f32[32,3]{1,0:T(8,128)} %constant.20.clone.r_4_, ...), custom_call_target="tpu_custom_call", output_to_operand_aliasing={{}: (0, {})} | custom-call | tf_op jit(solution)/shard_map/pallas_call | solution.py:194
Async XLA Ops:
  3.9 15.3 %collective-permute-start = (f32[1,5,3,2048]{3,2,1,0:T(4,128)}, f32[1,5,3,2048]{3,2,1,0:T(4,128)S(1)}, u32[]{:S(2)}, u32[]{:S(2)}) collective-permute-start(f32[1,5,3,2048]{3,2,1,0:T(4,128)} %get-tuple-element.9), channel_id=1, source_target_pairs={{0,28},{4,0},{8,4},{12,8},{16,12},{20,16},{24,20},{28,24},{1,29},{... | collective-permute-start | bytes 368648 | tf_op jit(solution)/shard_map/ppermute | solution.py:179
  4.5 14.8 %collective-permute-start.3 = (f32[1,5,3,2048]{3,2,1,0:T(4,128)}, f32[1,5,3,2048]{3,2,1,0:T(4,128)S(1)}, u32[]{:S(2)}, u32[]{:S(2)}) collective-permute-start(f32[1,5,3,2048]{3,2,1,0:T(4,128)} %get-tuple-element.12), channel_id=1, source_target_pairs={{0,4},{4,8},{8,12},{12,16},{16,20},{20,24},{24,28},{28,0},{1,5},{5... | collective-permute-start | bytes 368648 | tf_op jit(solution)/shard_map/ppermute | solution.py:179
  8.7 10.5 %collective-permute-start.1 = (f32[1,5,1,2048]{3,2,1,0:T(1,128)}, f32[1,5,1,2048]{3,2,1,0:T(1,128)S(1)}, u32[]{:S(2)}, u32[]{:S(2)}) collective-permute-start(f32[1,5,1,2048]{3,2,1,0:T(1,128)} %get-tuple-element.10), channel_id=1, source_target_pairs={{0,24},{4,28},{8,0},{12,4},{16,8},{20,12},{24,16},{28,20},{1,25},{... | collective-permute-start | bytes 122888 | tf_op jit(solution)/shard_map/ppermute | solution.py:179
  8.7 10.5 %collective-permute-start.2 = (f32[1,5,1,2048]{3,2,1,0:T(1,128)}, f32[1,5,1,2048]{3,2,1,0:T(1,128)S(1)}, u32[]{:S(2)}, u32[]{:S(2)}) collective-permute-start(f32[1,5,1,2048]{3,2,1,0:T(1,128)} %get-tuple-element.11), channel_id=1, source_target_pairs={{0,8},{4,12},{8,16},{12,20},{16,24},{20,28},{24,0},{28,4},{1,9},{5... | collective-permute-start | bytes 122888 | tf_op jit(solution)/shard_map/ppermute | solution.py:179
  19.2 0.6 %copy-start.2 = (f32[1,5,1,2048]{3,2,1,0:T(1,128)}, f32[1,5,1,2048]{3,2,1,0:T(1,128)S(1)}, u32[]{:S(2)}) copy-start(f32[1,5,1,2048]{3,2,1,0:T(1,128)S(1)} %collective-permute-done.1.r_6_) | copy-start | bytes 122884
  19.2 0.6 %copy-start.3 = (f32[1,5,1,2048]{3,2,1,0:T(1,128)}, f32[1,5,1,2048]{3,2,1,0:T(1,128)S(1)}, u32[]{:S(2)}) copy-start(f32[1,5,1,2048]{3,2,1,0:T(1,128)S(1)} %collective-permute-done.2.r_7_) | copy-start | bytes 122884
  19.2 0.7 %copy-start = (f32[1,5,3,2048]{3,2,1,0:T(4,128)}, f32[1,5,3,2048]{3,2,1,0:T(4,128)S(1)}, u32[]{:S(2)}) copy-start(f32[1,5,3,2048]{3,2,1,0:T(4,128)S(1)} %collective-permute-done.r_5_) | copy-start | bytes 368644
  19.9 0.6 %copy-start.1 = (f32[1,5,3,2048]{3,2,1,0:T(4,128)}, f32[1,5,3,2048]{3,2,1,0:T(4,128)S(1)}, u32[]{:S(2)}) copy-start(f32[1,5,3,2048]{3,2,1,0:T(4,128)S(1)} %collective-permute-done.3.r_8_) | copy-start | bytes 368644

commit v5 on v3

--- a/solution.py
+++ b/solution.py
@@ -127,14 +127,6 @@
             out_ref[f, 0, :, b * WIDTH : (b + 1) * WIDTH] = -(d_x + d_y[:, b * WIDTH : (b + 1) * WIDTH])
 
 
-def correct_kernel(spread_ref, partial_ref, *refs):
-    recv_refs, out_ref = refs[:-1], refs[-1]
-    spread = spread_ref[...]
-    for f in range(5):
-        received = jnp.concatenate([r[0, f] for r in recv_refs], axis=0)
-        out_ref[f, 0] = partial_ref[f, 0] - dot(spread, received)
-
-
 def full_spec(shape):
     return pl.BlockSpec(shape, lambda z: (0,) * len(shape))
 
@@ -182,14 +174,10 @@
             out_specs=out_spec,
             out_shape=out_shape,
         )(wx, jnp.asarray(own), density, momentum, energy)
-        return pl.pallas_call(
-            correct_kernel,
-            grid=(planes,),
-            in_specs=[full_spec(spread.shape), out_spec] + moment_specs,
-            out_specs=out_spec,
-            out_shape=out_shape,
-            input_output_aliases={1: 0},
-        )(jnp.asarray(spread), partial, *received)
+        received = jnp.concatenate(received, axis=2)
+        return partial - jnp.einsum(
+            "pr,zfrx->fzpx", jnp.asarray(spread), received, precision=HI
+        )
 
     return local
 

time: 23.4 us -> 22.3 us (0.953)
  the two profiles are of different devices: /device:TPU:30 before, /device:TPU:0 now
where the time goes in v5:
time: 22.3 us; the launch traced here: 22.1 us
  Pallas kernels  9.66 us (43%)
  starting transfers between devices  8.03 us (36%)
  matrix products  3.66 us (16%)
  waiting for transfers between devices  0.72 us (3%)
    ppermute x4, starting transfers between devices, local(): lax.ppermute(part, 'row', [(j, (j - e) % groups) for j in range(groups)])  8.03 us
    pallas_call x1, Pallas kernels, local(): pl.pallas_call(lambda *r: local_kernel(count, *r), grid=(planes,), in_spe...  6.69 us
    dot_general x1, matrix products, local(): jnp.einsum('pr,zfrx->fzpx', jnp.asarray(spread), received, precision=HI)  3.66 us
    pallas_call x1, Pallas kernels, local(): pl.pallas_call(lambda *r: moments_kernel(splits, *r), grid=(planes,), in_...  2.97 us
    ppermute x4, waiting for transfers between devices, local(): lax.ppermute(part, 'row', [(j, (j - e) % groups) for j in range(groups)])  0.72 us
  transfers between devices with their start and end apart: 4, of which 1 were waited for; matrix products, arithmetic and copies ran while one was open for 0% of the time, Pallas kernels for 30%

profile of v5, /device:TPU:0, one launch (start us, length us, event | category | flops | bytes accessed | tf_op | source)
XLA Modules:
  0.0 22.1 jit_solution(9843986623602545297)
XLA Ops:
  0.0 3.0 %shard_map.74 = (f32[1,5,3,2048]{3,2,1,0:T(4,128)}, f32[1,5,1,2048]{3,2,1,0:T(1,128)}, f32[1,5,1,2048]{3,2,1,0:T(1,128)}, f32[1,5,3,2048]{3,2,1,0:T(4,128)}) custom-call(f32[8,32]{1,0:T(8,128)} %constant.8.clone.r_0_, f32[1,32,2048]{2,1,0:T(8,128)} %r_1_.2, f32[3,1,32,2048]{3,2,1,0:T(8,128)} %r_2_.3, f32[1,32,2048]{2,1,0:T(8,128)} %r_3_.3), custom_call_target="tpu_custom_call" | custom-call | tf_op jit(solution)/shard_map/pallas_call | solution.py:156
  3.0 6.0 %collective-permute-start = (f32[1,5,3,2048]{3,2,1,0:T(4,128)}, f32[1,5,3,2048]{3,2,1,0:T(4,128)S(1)}, u32[]{:S(2)}, u32[]{:S(2)}) collective-permute-start(f32[1,5,3,2048]{3,2,1,0:T(4,128)} %get-tuple-element.9), channel_id=1, source_target_pairs={{0,28},{4,0},{8,4},{12,8},{16,12},{20,16},{24,20},{28,24},{1,29},{... | collective-permute-start | bytes 368648 | tf_op jit(solution)/shard_map/ppermute | solution.py:164
  9.0 0.0 collective-permute-start.3
  9.0 1.1 %collective-permute-start.1 = (f32[1,5,1,2048]{3,2,1,0:T(1,128)}, f32[1,5,1,2048]{3,2,1,0:T(1,128)S(1)}, u32[]{:S(2)}, u32[]{:S(2)}) collective-permute-start(f32[1,5,1,2048]{3,2,1,0:T(1,128)} %get-tuple-element.10), channel_id=1, source_target_pairs={{0,24},{4,28},{8,0},{12,4},{16,8},{20,12},{24,16},{28,20},{1,25},{... | collective-permute-start | bytes 122888 | tf_op jit(solution)/shard_map/ppermute | solution.py:164
  10.0 0.0 copy-start
  10.0 1.0 %collective-permute-start.2 = (f32[1,5,1,2048]{3,2,1,0:T(1,128)}, f32[1,5,1,2048]{3,2,1,0:T(1,128)S(1)}, u32[]{:S(2)}, u32[]{:S(2)}) collective-permute-start(f32[1,5,1,2048]{3,2,1,0:T(1,128)} %get-tuple-element.11), channel_id=1, source_target_pairs={{0,8},{4,12},{8,16},{12,20},{16,24},{20,28},{24,0},{28,4},{1,9},{5... | collective-permute-start | bytes 122888 | tf_op jit(solution)/shard_map/ppermute | solution.py:164
  11.0 6.7 %shard_map.73 = f32[5,1,32,2048]{3,2,1,0:T(8,128)} custom-call(f32[128,384]{1,0:T(8,128)} %constant.9.clone.r_0_, f32[32,32]{1,0:T(8,128)} %constant.10.clone.r_1_, f32[1,32,2048]{2,1,0:T(8,128)} %r_1_.2, f32[3,1,32,2048]{3,2,1,0:T(8,128)} %r_2_.3, f32[1,32,2048]{2,1,0:T(8,128)} %r_3_.3), custom_call_target="tpu_custom_call" | custom-call | tf_op jit(solution)/shard_map/pallas_call | solution.py:170
  17.7 0.0 collective-permute-done.1
  17.7 0.0 collective-permute-done.2
  17.7 0.0 collective-permute-done
  17.7 0.7 %collective-permute-done.3 = f32[1,5,3,2048]{3,2,1,0:T(4,128)S(1)} collective-permute-done((f32[1,5,3,2048]{3,2,1,0:T(4,128)}, f32[1,5,3,2048]{3,2,1,0:T(4,128)S(1)}, u32[]{:S(2)}, u32[]{:S(2)}) %collective-permute-start.3) | collective-permute-done | bytes 122912 | tf_op jit(solution)/shard_map/ppermute | solution.py:164
  18.4 0.0 copy-done
  18.4 3.7 %fusion = f32[5,1,32,2048]{3,2,1,0:T(8,128)} fusion(f32[5,1,32,2048]{3,2,1,0:T(8,128)} %shard_map.73, f32[32,8,1]{0,1,2:T(8,128)S(1)} %copy-done, f32[1,5,3,2048]{3,2,1,0:T(4,128)S(1)} %collective-permute-done.3, f32[1,5,1,2048]{3,2,1,0:T(1,128)S(1)} %collective-permute-done.2, f32[1,5,1,2048]{3,2,1,0:T(1,128)S(1)} %collective-permute-done.1, ...), kind=kOutput, calls=%fused_computation.1 | convolution fusion | flops 32030720 | bytes 2950144 | tf_op jit(solution)/shard_map/pr,zfrx->fzpx/dot_general | solution.py:178
Async XLA Ops:
  3.0 14.7 %collective-permute-start = (f32[1,5,3,2048]{3,2,1,0:T(4,128)}, f32[1,5,3,2048]{3,2,1,0:T(4,128)S(1)}, u32[]{:S(2)}, u32[]{:S(2)}) collective-permute-start(f32[1,5,3,2048]{3,2,1,0:T(4,128)} %get-tuple-element.9), channel_id=1, source_target_pairs={{0,28},{4,0},{8,4},{12,8},{16,12},{20,16},{24,20},{28,24},{1,29},{... | collective-permute-start | bytes 368648 | tf_op jit(solution)/shard_map/ppermute | solution.py:164
  9.0 9.4 %collective-permute-start.3 = (f32[1,5,3,2048]{3,2,1,0:T(4,128)}, f32[1,5,3,2048]{3,2,1,0:T(4,128)S(1)}, u32[]{:S(2)}, u32[]{:S(2)}) collective-permute-start(f32[1,5,3,2048]{3,2,1,0:T(4,128)} %get-tuple-element.12), channel_id=1, source_target_pairs={{0,4},{4,8},{8,12},{12,16},{16,20},{20,24},{24,28},{28,0},{1,5},{5... | collective-permute-start | bytes 368648 | tf_op jit(solution)/shard_map/ppermute | solution.py:164
  9.0 8.7 %collective-permute-start.1 = (f32[1,5,1,2048]{3,2,1,0:T(1,128)}, f32[1,5,1,2048]{3,2,1,0:T(1,128)S(1)}, u32[]{:S(2)}, u32[]{:S(2)}) collective-permute-start(f32[1,5,1,2048]{3,2,1,0:T(1,128)} %get-tuple-element.10), channel_id=1, source_target_pairs={{0,24},{4,28},{8,0},{12,4},{16,8},{20,12},{24,16},{28,20},{1,25},{... | collective-permute-start | bytes 122888 | tf_op jit(solution)/shard_map/ppermute | solution.py:164
  10.0 8.4 %copy-start = (f32[32,8,1]{0,1,2:T(8,128)S(1)}, f32[32,8,1]{0,1,2:T(8,128)}, u32[]{:S(2)}) copy-start(f32[32,8,1]{0,1,2:T(8,128)} %constant.15) | copy-start | bytes 3076
  10.0 7.7 %collective-permute-start.2 = (f32[1,5,1,2048]{3,2,1,0:T(1,128)}, f32[1,5,1,2048]{3,2,1,0:T(1,128)S(1)}, u32[]{:S(2)}, u32[]{:S(2)}) collective-permute-start(f32[1,5,1,2048]{3,2,1,0:T(1,128)} %get-tuple-element.11), channel_id=1, source_target_pairs={{0,8},{4,12},{8,16},{12,20},{16,24},{20,28},{24,0},{28,4},{1,9},{5... | collective-permute-start | bytes 122888 | tf_op jit(solution)/shard_map/ppermute | solution.py:164

commit v6 on v5

--- a/solution.py
+++ b/solution.py
@@ -127,6 +127,24 @@
             out_ref[f, 0, :, b * WIDTH : (b + 1) * WIDTH] = -(d_x + d_y[:, b * WIDTH : (b + 1) * WIDTH])
 
 
+def exchange_plan(groups, shift_list):
+    if groups % 4 or sorted(shift_list) != sorted({1, 2, groups - 2, groups - 1}) or groups < 8:
+        return None
+    plans = []
+    for step, phase in ((1, 0), (1, 1), (2, 0), (2, 1)):
+        perm = []
+        sends_first = np.zeros(groups, bool)
+        takes_first = np.zeros(groups, bool)
+        for r in range(groups):
+            if (r // step) % 2 == phase:
+                up = (r + step) % groups
+                perm += [(r, up), (up, r)]
+                sends_first[up] = True
+                takes_first[r] = True
+        plans.append((perm, sends_first, takes_first, step, groups - step))
+    return plans
+
+
 def full_spec(shape):
     return pl.BlockSpec(shape, lambda z: (0,) * len(shape))
 
@@ -136,7 +154,6 @@
         planes, rows, count = density.shape
         own, shifts = y_operator(rows, groups)
         weights = np.concatenate([w for _, _, w in shifts], axis=0)
-        spread = np.concatenate([q for _, q, _ in shifts], axis=1)
         splits = []
         lo = 0
         for _, _, w in shifts:
@@ -160,10 +177,27 @@
             out_specs=moment_specs,
             out_shape=moment_shapes,
         )(jnp.asarray(weights), density, momentum, energy)
-        received = [
-            lax.ppermute(part, "row", [(j, (j - e) % groups) for j in range(groups)])
-            for (e, _, _), part in zip(shifts, moments)
-        ]
+        by_shift = {e: (q, part) for (e, q, _), part in zip(shifts, moments)}
+        pairs = exchange_plan(groups, [e for e, _, _ in shifts])
+        if pairs is None:
+            received = [
+                lax.ppermute(part, "row", [(j, (j - e) % groups) for j in range(groups)])
+                for (e, _, _), part in zip(shifts, moments)
+            ]
+            spread = jnp.asarray(np.concatenate([q for _, q, _ in shifts], axis=1))
+        else:
+            index = lax.axis_index("row")
+            received = []
+            spreads = []
+            for perm, sends_first, takes_first, first, second in pairs:
+                send = jnp.asarray(sends_first)[index]
+                take = jnp.asarray(takes_first)[index]
+                message = jnp.where(send, by_shift[first][1], by_shift[second][1])
+                received.append(lax.ppermute(message, "row", perm))
+                spreads.append(
+                    jnp.where(take, jnp.asarray(by_shift[first][0]), jnp.asarray(by_shift[second][0]))
+                )
+            spread = jnp.concatenate(spreads, axis=1)
         wx = block_weights(count)
         out_spec = pl.BlockSpec((5, 1, rows, count), lambda z: (0, z, 0, 0))
         out_shape = jax.ShapeDtypeStruct((5, planes, rows, count), jnp.float32)
@@ -176,7 +210,7 @@
         )(wx, jnp.asarray(own), density, momentum, energy)
         received = jnp.concatenate(received, axis=2)
         return partial - jnp.einsum(
-            "pr,zfrx->fzpx", jnp.asarray(spread), received, precision=HI
+            "pr,zfrx->fzpx", spread, received, precision=HI
         )
 
     return local

time: 22.3 us -> 33.3 us (1.49)
  other arithmetic: 0 us -> 7.14 us
  local copies, waits for them, and re-layouts: 0.01 us -> 3.94 us
  waiting for transfers between devices: 0.72 us -> 0.01 us
  starting transfers between devices: 8.03 us -> 8.44 us
    select_n x0 -> x4, other arithmetic: none -> 7.14 us  [the longest x2 4.52 us: local(): message = jnp.where(send, by_shift[first][1], by_shift[second][1])]
    dynamic_slice x0 -> x4, local copies, waits for them, and re-layouts: none -> 3.92 us  [local(): send = jnp.asarray(sends_first)[index]]
    ppermute x4, waiting for transfers between devices: 0.72 us -> 0.01 us  [local(): received.append(lax.ppermute(message, 'row', perm))]
    ppermute x4, starting transfers between devices: 8.03 us -> 8.44 us  [local(): received.append(lax.ppermute(message, 'row', perm))]
  transfers between devices with their start and end apart: 4 -> 4, of which waited for: 1 -> 0; matrix products, arithmetic and copies ran while one was open for 0% -> 19% of each run, Pallas kernels for 30% -> 20%
where the time goes in v6:
time: 33.3 us; the launch traced here: 32.9 us
  Pallas kernels  9.64 us (29%)
  starting transfers between devices  8.44 us (25%)
  other arithmetic  7.14 us (21%)
  local copies, waits for them, and re-layouts  3.94 us (12%)
  matrix products  3.68 us (11%)
    ppermute x4, starting transfers between devices, local(): received.append(lax.ppermute(message, 'row', perm))  8.44 us
    pallas_call x1, Pallas kernels, local(): pl.pallas_call(lambda *r: local_kernel(count, *r), grid=(planes,), in_spe...  6.7 us
    select_n x2, other arithmetic, local(): message = jnp.where(send, by_shift[first][1], by_shift[second][1])  4.52 us
    dynamic_slice x4, local copies, waits for them, and re-layouts, local(): send = jnp.asarray(sends_first)[index]  3.92 us
    dot_general x1, matrix products, local(): return partial - jnp.einsum('pr,zfrx->fzpx', spread, received, precision=HI)  3.68 us
    pallas_call x1, Pallas kernels, local(): pl.pallas_call(lambda *r: moments_kernel(splits, *r), grid=(planes,), in_...  2.94 us
    select_n x2, other arithmetic, local(): jnp.where(take, jnp.asarray(by_shift[first][0]), jnp.asarray(by_shift[sec...  2.62 us
  transfers between devices with their start and end apart: 4, of which 0 were waited for; matrix products, arithmetic and copies ran while one was open for 19% of the time, Pallas kernels for 20%

profile of v6, /device:TPU:0, one launch (start us, length us, event | category | flops | bytes accessed | tf_op | source)
XLA Modules:
  0.0 32.9 jit_solution(6585596471362592054)
XLA Ops:
  0.0 0.0 copy-start.5
  0.0 0.0 copy-start.4
  0.0 0.0 copy-start
  0.0 0.0 copy-start.1
  0.0 0.0 copy-start.2
  0.0 0.0 copy-start.3
  0.0 1.4 %dynamic_slice.27 = pred[1]{0:T(512)(128)(4,1)} dynamic-slice(pred[8]{0:T(512)(128)(4,1)} %constant.38.clone, s32[]{:T(128)S(6)} %select_n.66), dynamic_slice_sizes={1} | dynamic-slice | bytes 6 | tf_op jit(solution)/shard_map/dynamic_slice | solution.py:193
  1.4 1.3 %dynamic_slice.26 = pred[1]{0:T(512)(128)(4,1)} dynamic-slice(pred[8]{0:T(512)(128)(4,1)} %constant.37.clone, s32[]{:T(128)S(6)} %select_n.66), dynamic_slice_sizes={1} | dynamic-slice | bytes 6 | tf_op jit(solution)/shard_map/dynamic_slice | solution.py:193
  2.7 2.9 %shard_map.173 = (f32[1,5,3,2048]{3,2,1,0:T(4,128)}, f32[1,5,1,2048]{3,2,1,0:T(1,128)}, f32[1,5,1,2048]{3,2,1,0:T(1,128)}, f32[1,5,3,2048]{3,2,1,0:T(4,128)}) custom-call(f32[8,32]{1,0:T(8,128)} %constant.32.clone.r_0_, f32[1,32,2048]{2,1,0:T(8,128)} %r_1_.2, f32[3,1,32,2048]{3,2,1,0:T(8,128)} %r_2_.3, f32[1,32,2048]{2,1,0:T(8,128)} %r_3_.3), custom_call_target="tpu_custom_call" | custom-call | tf_op jit(solution)/shard_map/pallas_call | solution.py:173
  5.6 2.2 %broadcast_select_fusion.1 = (f32[1,5,1,2048]{3,2,1,0:T(1,128)S(1)}, f32[1,5,1,2048]{3,2,1,0:T(1,128)S(1)}) fusion(f32[1,5,1,2048]{3,2,1,0:T(1,128)} %get-tuple-element.11, f32[1,5,1,2048]{3,2,1,0:T(1,128)} %get-tuple-element.12, pred[]{:T(512)} %bitcast.2, pred[]{:T(512)} %bitcast.3), kind=kLoop, calls=%fused_computation.10 | loop fusion | flops 20480 | bytes 163842 | tf_op jit(solution)/shard_map/jit(_where)/select_n | solution.py:195
  7.8 3.1 %collective-permute-start.2 = (f32[1,5,1,2048]{3,2,1,0:T(1,128)S(1)}, f32[1,5,1,2048]{3,2,1,0:T(1,128)S(1)}, u32[]{:S(2)}, u32[]{:S(2)}) collective-permute-start(f32[1,5,1,2048]{3,2,1,0:T(1,128)S(1)} %get-tuple-element.15), channel_id=1, source_target_pairs={{0,8},{8,0},{4,12},{12,4},{16,24},{24,16},{20,28},{28,20},{1,9},{9... | collective-permute-start | bytes 122888 | tf_op jit(solution)/shard_map/ppermute | solution.py:196
  10.9 2.5 %collective-permute-start.3 = (f32[1,5,1,2048]{3,2,1,0:T(1,128)S(1)}, f32[1,5,1,2048]{3,2,1,0:T(1,128)S(1)}, u32[]{:S(2)}, u32[]{:S(2)}) collective-permute-start(f32[1,5,1,2048]{3,2,1,0:T(1,128)S(1)} %get-tuple-element.16), channel_id=1, source_target_pairs={{8,16},{16,8},{12,20},{20,12},{24,0},{0,24},{28,4},{4,28},{9,17},{... | collective-permute-start | bytes 122888 | tf_op jit(solution)/shard_map/ppermute | solution.py:196
  13.4 0.0 copy-done.5
  13.4 0.7 %dynamic_slice.25 = pred[1]{0:T(512)(128)(4,1)} dynamic-slice(pred[8]{0:T(512)(128)(4,1)S(1)} %copy-done.5, s32[]{:T(128)S(6)} %select_n.66), dynamic_slice_sizes={1} | dynamic-slice | bytes 6 | tf_op jit(solution)/shard_map/dynamic_slice | solution.py:193
  14.0 0.0 copy-done.4
  14.0 0.6 %dynamic_slice.24 = pred[1]{0:T(512)(128)(4,1)} dynamic-slice(pred[8]{0:T(512)(128)(4,1)S(1)} %copy-done.4, s32[]{:T(128)S(6)} %select_n.66), dynamic_slice_sizes={1} | dynamic-slice | bytes 6 | tf_op jit(solution)/shard_map/dynamic_slice | solution.py:193
  14.6 2.4 %broadcast_select_fusion.3 = (f32[1,5,3,2048]{3,2,1,0:T(4,128)S(1)}, f32[1,5,3,2048]{3,2,1,0:T(4,128)S(1)}) fusion(f32[1,5,3,2048]{3,2,1,0:T(4,128)} %get-tuple-element.9, f32[1,5,3,2048]{3,2,1,0:T(4,128)} %get-tuple-element.10, pred[]{:T(512)} %bitcast, pred[]{:T(512)} %bitcast.1), kind=kLoop, calls=%fused_computation.12 | loop fusion | flops 61440 | bytes 491522 | tf_op jit(solution)/shard_map/jit(_where)/select_n | solution.py:195
  17.0 1.6 %collective-permute-start = (f32[1,5,3,2048]{3,2,1,0:T(4,128)S(1)}, f32[1,5,3,2048]{3,2,1,0:T(4,128)S(1)}, u32[]{:S(2)}, u32[]{:S(2)}) collective-permute-start(f32[1,5,3,2048]{3,2,1,0:T(4,128)S(1)} %get-tuple-element.13), channel_id=1, source_target_pairs={{0,4},{4,0},{8,12},{12,8},{16,20},{20,16},{24,28},{28,24},{1,5},{5... | collective-permute-start | bytes 368648 | tf_op jit(solution)/shard_map/ppermute | solution.py:196
  18.6 1.3 %collective-permute-start.1 = (f32[1,5,3,2048]{3,2,1,0:T(4,128)S(1)}, f32[1,5,3,2048]{3,2,1,0:T(4,128)S(1)}, u32[]{:S(2)}, u32[]{:S(2)}) collective-permute-start(f32[1,5,3,2048]{3,2,1,0:T(4,128)S(1)} %get-tuple-element.14), channel_id=1, source_target_pairs={{4,8},{8,4},{12,16},{16,12},{20,24},{24,20},{28,0},{0,28},{5,9},{9... | collective-permute-start | bytes 368648 | tf_op jit(solution)/shard_map/ppermute | solution.py:196
  19.9 0.0 copy-done
  19.9 0.0 copy-done.1
  19.9 1.3 %broadcast_select_fusion.7 = (f32[32,3]{0,1:T(4,128)S(1)}, f32[32,3]{0,1:T(4,128)S(1)}) fusion(f32[32,3]{0,1:T(4,128)S(1)} %copy-done.1, f32[32,3]{0,1:T(4,128)S(1)} %copy-done, pred[]{:T(512)} %bitcast.1, pred[]{:T(512)} %bitcast), kind=kLoop, calls=%fused_computation.23 | loop fusion | flops 192 | bytes 1538 | tf_op jit(solution)/shard_map/jit(_where)/select_n | solution.py:198
  21.2 0.0 copy-done.2
  21.2 0.0 copy-done.3
  21.2 1.3 %broadcast_select_fusion.5 = (f32[32,1]{0,1:T(1,128)S(1)}, f32[32,1]{0,1:T(1,128)S(1)}) fusion(f32[32,1]{0,1:T(1,128)S(1)} %copy-done.3, f32[32,1]{0,1:T(1,128)S(1)} %copy-done.2, pred[]{:T(512)} %bitcast.3, pred[]{:T(512)} %bitcast.2), kind=kLoop, calls=%fused_computation.21 | loop fusion | flops 64 | bytes 514 | tf_op jit(solution)/shard_map/jit(_where)/select_n | solution.py:198
  22.5 6.7 %shard_map.172 = f32[5,1,32,2048]{3,2,1,0:T(8,128)} custom-call(f32[128,384]{1,0:T(8,128)} %constant.41.clone.r_0_, f32[32,32]{1,0:T(8,128)} %constant.42.clone.r_1_, f32[1,32,2048]{2,1,0:T(8,128)} %r_1_.2, f32[3,1,32,2048]{3,2,1,0:T(8,128)} %r_2_.3, f32[1,32,2048]{2,1,0:T(8,128)} %r_3_.3), custom_call_target="tpu_custom_call" | custom-call | tf_op jit(solution)/shard_map/pallas_call | solution.py:204
  29.2 0.0 collective-permute-done.2
  29.2 0.0 collective-permute-done.3
  29.2 0.0 collective-permute-done
  29.2 0.0 collective-permute-done.1
  29.2 3.7 %fusion = f32[5,1,32,2048]{3,2,1,0:T(8,128)} fusion(f32[5,1,32,2048]{3,2,1,0:T(8,128)} %shard_map.172, f32[1,5,1,2048]{3,2,1,0:T(1,128)S(1)} %collective-permute-done.3, f32[1,5,1,2048]{3,2,1,0:T(1,128)S(1)} %collective-permute-done.2, f32[1,5,3,2048]{3,2,1,0:T(4,128)S(1)} %collective-permute-done.1, f32[1,5,3,2048]{3,2,1,0:T(4,128)S(1)} %collective-permute-done, ...), kind=kOutput, calls=%fused_computation.1 | convolution fusion | flops 32031488 | bytes 2950144 | tf_op jit(solution)/shard_map/pr,zfrx->fzpx/dot_general | solution.py:212
Async XLA Ops:
  0.0 13.4 %copy-start.5 = (pred[8]{0:T(512)(128)(4,1)S(1)}, pred[8]{0:T(512)(128)(4,1)}, u32[]{:S(2)}) copy-start(pred[8]{0:T(512)(128)(4,1)} %constant.34.clone) | copy-start | bytes 28
  0.0 14.0 %copy-start.4 = (pred[8]{0:T(512)(128)(4,1)S(1)}, pred[8]{0:T(512)(128)(4,1)}, u32[]{:S(2)}) copy-start(pred[8]{0:T(512)(128)(4,1)} %constant.33.clone) | copy-start | bytes 28
  0.0 19.9 %copy-start = (f32[32,3]{0,1:T(4,128)S(1)}, f32[32,3]{0,1:T(4,128)}, u32[]{:S(2)}) copy-start(f32[32,3]{0,1:T(4,128)} %constant.36.clone) | copy-start | bytes 1156
  0.0 19.9 %copy-start.1 = (f32[32,3]{0,1:T(4,128)S(1)}, f32[32,3]{0,1:T(4,128)}, u32[]{:S(2)}) copy-start(f32[32,3]{0,1:T(4,128)} %constant.35.clone) | copy-start | bytes 1156
  0.0 21.2 %copy-start.2 = (f32[32,1]{0,1:T(1,128)S(1)}, f32[32,1]{0,1:T(1,128)}, u32[]{:S(2)}) copy-start(f32[32,1]{0,1:T(1,128)} %constant.40.clone) | copy-start | bytes 388
  0.0 21.2 %copy-start.3 = (f32[32,1]{0,1:T(1,128)S(1)}, f32[32,1]{0,1:T(1,128)}, u32[]{:S(2)}) copy-start(f32[32,1]{0,1:T(1,128)} %constant.39.clone) | copy-start | bytes 388
  7.8 21.4 %collective-permute-start.2 = (f32[1,5,1,2048]{3,2,1,0:T(1,128)S(1)}, f32[1,5,1,2048]{3,2,1,0:T(1,128)S(1)}, u32[]{:S(2)}, u32[]{:S(2)}) collective-permute-start(f32[1,5,1,2048]{3,2,1,0:T(1,128)S(1)} %get-tuple-element.15), channel_id=1, source_target_pairs={{0,8},{8,0},{4,12},{12,4},{16,24},{24,16},{20,28},{28,20},{1,9},{9... | collective-permute-start | bytes 122888 | tf_op jit(solution)/shard_map/ppermute | solution.py:196
  10.9 18.3 %collective-permute-start.3 = (f32[1,5,1,2048]{3,2,1,0:T(1,128)S(1)}, f32[1,5,1,2048]{3,2,1,0:T(1,128)S(1)}, u32[]{:S(2)}, u32[]{:S(2)}) collective-permute-start(f32[1,5,1,2048]{3,2,1,0:T(1,128)S(1)} %get-tuple-element.16), channel_id=1, source_target_pairs={{8,16},{16,8},{12,20},{20,12},{24,0},{0,24},{28,4},{4,28},{9,17},{... | collective-permute-start | bytes 122888 | tf_op jit(solution)/shard_map/ppermute | solution.py:196
  17.0 12.2 %collective-permute-start = (f32[1,5,3,2048]{3,2,1,0:T(4,128)S(1)}, f32[1,5,3,2048]{3,2,1,0:T(4,128)S(1)}, u32[]{:S(2)}, u32[]{:S(2)}) collective-permute-start(f32[1,5,3,2048]{3,2,1,0:T(4,128)S(1)} %get-tuple-element.13), channel_id=1, source_target_pairs={{0,4},{4,0},{8,12},{12,8},{16,20},{20,16},{24,28},{28,24},{1,5},{5... | collective-permute-start | bytes 368648 | tf_op jit(solution)/shard_map/ppermute | solution.py:196
  18.6 10.7 %collective-permute-start.1 = (f32[1,5,3,2048]{3,2,1,0:T(4,128)S(1)}, f32[1,5,3,2048]{3,2,1,0:T(4,128)S(1)}, u32[]{:S(2)}, u32[]{:S(2)}) collective-permute-start(f32[1,5,3,2048]{3,2,1,0:T(4,128)S(1)} %get-tuple-element.14), channel_id=1, source_target_pairs={{4,8},{8,4},{12,16},{16,12},{20,24},{24,20},{28,0},{0,28},{5,9},{9... | collective-permute-start | bytes 368648 | tf_op jit(solution)/shard_map/ppermute | solution.py:196

commit v7 on v5

--- a/solution.py
+++ b/solution.py
@@ -96,13 +96,17 @@
     return flux_x, flux_y
 
 
-def moments_kernel(splits, weights_ref, rho_ref, mom_ref, energy_ref, *out_refs):
+def moments_kernel(splits, choices, index_ref, weights_ref, rho_ref, mom_ref, energy_ref, *out_refs):
     _, flux_y = plane_fluxes(rho_ref, mom_ref, energy_ref)
     weights = weights_ref[...]
+    index = index_ref[0]
     for f in range(5):
         moments = dot(weights, flux_y[f])
-        for (lo, hi), out_ref in zip(splits, out_refs):
-            out_ref[0, f] = moments[lo:hi]
+        for (step, phase, first, second), out_ref in zip(choices, out_refs):
+            pick = (index // step) % 2 != phase
+            lo, hi = splits[first]
+            lo2, hi2 = splits[second]
+            out_ref[0, f] = jnp.where(pick, moments[lo:hi], moments[lo2:hi2])
 
 
 def local_kernel(count, wx_ref, own_ref, rho_ref, mom_ref, energy_ref, out_ref):
@@ -127,6 +131,21 @@
             out_ref[f, 0, :, b * WIDTH : (b + 1) * WIDTH] = -(d_x + d_y[:, b * WIDTH : (b + 1) * WIDTH])
 
 
+def exchange_plan(groups, shift_list):
+    assert groups % 4 == 0 and groups >= 8
+    assert sorted(shift_list) == sorted({1, 2, groups - 2, groups - 1})
+    plans = []
+    for step, phase in ((1, 0), (1, 1), (2, 0), (2, 1)):
+        perm = []
+        for r in range(groups):
+            if (r // step) % 2 == phase:
+                up = (r + step) % groups
+                assert (up // step) % 2 != phase
+                perm += [(r, up), (up, r)]
+        plans.append((step, phase, step, groups - step, perm))
+    return plans
+
+
 def full_spec(shape):
     return pl.BlockSpec(shape, lambda z: (0,) * len(shape))
 
@@ -136,7 +155,6 @@
         planes, rows, count = density.shape
         own, shifts = y_operator(rows, groups)
         weights = np.concatenate([w for _, _, w in shifts], axis=0)
-        spread = np.concatenate([q for _, q, _ in shifts], axis=1)
         splits = []
         lo = 0
         for _, _, w in shifts:
@@ -147,23 +165,38 @@
             pl.BlockSpec((3, 1, rows, count), lambda z: (0, z, 0, 0)),
             pl.BlockSpec((1, rows, count), lambda z: (z, 0, 0)),
         ]
+        by_shift = {e: (q, split) for (e, q, _), split in zip(shifts, splits)}
+        plan = exchange_plan(groups, [e for e, _, _ in shifts])
+        index = lax.axis_index("row")
+        choices = [(step, phase, first, second) for step, phase, first, second, _ in plan]
         moment_shapes = [
-            jax.ShapeDtypeStruct((planes, 5, hi - lo, count), jnp.float32) for lo, hi in splits
+            jax.ShapeDtypeStruct(
+                (planes, 5, by_shift[first][1][1] - by_shift[first][1][0], count), jnp.float32
+            )
+            for _, _, first, _ in choices
         ]
         moment_specs = [
-            pl.BlockSpec((1, 5, hi - lo, count), lambda z: (z, 0, 0, 0)) for lo, hi in splits
+            pl.BlockSpec((1,) + s.shape[1:], lambda z: (z, 0, 0, 0)) for s in moment_shapes
         ]
-        moments = pl.pallas_call(
-            lambda *r: moments_kernel(splits, *r),
+        split_of = {e: by_shift[e][1] for e in by_shift}
+        messages = pl.pallas_call(
+            lambda *r: moments_kernel(split_of, choices, *r),
             grid=(planes,),
-            in_specs=[full_spec(weights.shape)] + plane_specs,
+            in_specs=[pl.BlockSpec(memory_space=pltpu.SMEM), full_spec(weights.shape)]
+            + plane_specs,
             out_specs=moment_specs,
             out_shape=moment_shapes,
-        )(jnp.asarray(weights), density, momentum, energy)
-        received = [
-            lax.ppermute(part, "row", [(j, (j - e) % groups) for j in range(groups)])
-            for (e, _, _), part in zip(shifts, moments)
-        ]
+        )(index.reshape(1).astype(jnp.int32), jnp.asarray(weights), density, momentum, energy)
+        received = []
+        spreads = []
+        for (step, phase, first, second, perm), message in zip(plan, messages):
+            received.append(lax.ppermute(message, "row", perm))
+            take = ((index // step) % 2 == phase).astype(jnp.float32)
+            spreads.append(
+                take * jnp.asarray(by_shift[first][0])
+                + (1.0 - take) * jnp.asarray(by_shift[second][0])
+            )
+        spread = jnp.concatenate(spreads, axis=1)
         wx = block_weights(count)
         out_spec = pl.BlockSpec((5, 1, rows, count), lambda z: (0, z, 0, 0))
         out_shape = jax.ShapeDtypeStruct((5, planes, rows, count), jnp.float32)
@@ -176,7 +209,7 @@
         )(wx, jnp.asarray(own), density, momentum, energy)
         received = jnp.concatenate(received, axis=2)
         return partial - jnp.einsum(
-            "pr,zfrx->fzpx", jnp.asarray(spread), received, precision=HI
+            "pr,zfrx->fzpx", spread, received, precision=HI
         )
 
     return local

time: 22.3 us -> 22.1 us (level)
  waiting for transfers between devices: 0.72 us -> 0.18 us
  starting transfers between devices: 8.03 us -> 8.31 us
    ppermute x4, waiting for transfers between devices: 0.72 us -> 0.18 us  [local(): received.append(lax.ppermute(message, 'row', perm))]
    ppermute x4, starting transfers between devices: 8.03 us -> 8.31 us  [local(): received.append(lax.ppermute(message, 'row', perm))]
  transfers between devices with their start and end apart: 4 -> 4, of which waited for: 1 -> 1; matrix products, arithmetic and copies ran while one was open for 0% -> 0% of each run, Pallas kernels for 30% -> 31%
where the time goes in v7:
time: 22.1 us; the launch traced here: 21.9 us
  Pallas kernels  9.7 us (44%)
  starting transfers between devices  8.31 us (38%)
  matrix products  3.66 us (17%)
    ppermute x4, starting transfers between devices, local(): received.append(lax.ppermute(message, 'row', perm))  8.31 us
    pallas_call x1, Pallas kernels, local(): pl.pallas_call(lambda *r: local_kernel(count, *r), grid=(planes,), in_spe...  6.7 us
    dot_general x1, matrix products, local(): return partial - jnp.einsum('pr,zfrx->fzpx', spread, received, precision=HI)  3.66 us
    pallas_call x1, Pallas kernels, local(): pl.pallas_call(lambda *r: moments_kernel(split_of, choices, *r), grid=(pl...  3.01 us
  transfers between devices with their start and end apart: 4, of which 1 were waited for; matrix products, arithmetic and copies ran while one was open for 0% of the time, Pallas kernels for 31%

profile of v7, /device:TPU:0, one launch (start us, length us, event | category | flops | bytes accessed | tf_op | source)
XLA Modules:
  0.0 21.9 jit_solution(3104662582057016465)
XLA Ops:
  0.0 0.0 copy-start
  0.0 0.0 copy-start.1
  0.0 0.0 copy-start.2
  0.0 0.0 copy-start.3
  0.0 3.0 %shard_map.101 = (f32[1,5,3,2048]{3,2,1,0:T(4,128)}, f32[1,5,3,2048]{3,2,1,0:T(4,128)}, f32[1,5,1,2048]{3,2,1,0:T(1,128)}, f32[1,5,1,2048]{3,2,1,0:T(1,128)}) custom-call(s32[1]{0:T(128)} %bitcast.r_0_, f32[8,32]{1,0:T(8,128)} %constant.68.clone.r_1_, f32[1,32,2048]{2,1,0:T(8,128)} %r_2_.3, f32[3,1,32,2048]{3,2,1,0:T(8,128)} %r_3_.3, f32[1,32,2048]{2,1,0:T(8,128)} %r_4_.3), custom_call_target="tpu_custom_call" | custom-call | tf_op jit(solution)/shard_map/pallas_call | solution.py:182
  3.0 3.0 %collective-permute-start.2 = (f32[1,5,1,2048]{3,2,1,0:T(1,128)}, f32[1,5,1,2048]{3,2,1,0:T(1,128)S(1)}, u32[]{:S(2)}, u32[]{:S(2)}) collective-permute-start(f32[1,5,1,2048]{3,2,1,0:T(1,128)} %get-tuple-element.11), channel_id=1, source_target_pairs={{0,8},{8,0},{4,12},{12,4},{16,24},{24,16},{20,28},{28,20},{1,9},{9... | collective-permute-start | bytes 122888 | tf_op jit(solution)/shard_map/ppermute | solution.py:193
  6.0 2.5 %collective-permute-start.3 = (f32[1,5,1,2048]{3,2,1,0:T(1,128)}, f32[1,5,1,2048]{3,2,1,0:T(1,128)S(1)}, u32[]{:S(2)}, u32[]{:S(2)}) collective-permute-start(f32[1,5,1,2048]{3,2,1,0:T(1,128)} %get-tuple-element.12), channel_id=1, source_target_pairs={{8,16},{16,8},{12,20},{20,12},{24,0},{0,24},{28,4},{4,28},{9,17},{... | collective-permute-start | bytes 122888 | tf_op jit(solution)/shard_map/ppermute | solution.py:193
  8.5 1.5 %collective-permute-start = (f32[1,5,3,2048]{3,2,1,0:T(4,128)}, f32[1,5,3,2048]{3,2,1,0:T(4,128)S(1)}, u32[]{:S(2)}, u32[]{:S(2)}) collective-permute-start(f32[1,5,3,2048]{3,2,1,0:T(4,128)} %get-tuple-element.9), channel_id=1, source_target_pairs={{0,4},{4,0},{8,12},{12,8},{16,20},{20,16},{24,28},{28,24},{1,5},{5... | collective-permute-start | bytes 368648 | tf_op jit(solution)/shard_map/ppermute | solution.py:193
  10.0 1.3 %collective-permute-start.1 = (f32[1,5,3,2048]{3,2,1,0:T(4,128)}, f32[1,5,3,2048]{3,2,1,0:T(4,128)S(1)}, u32[]{:S(2)}, u32[]{:S(2)}) collective-permute-start(f32[1,5,3,2048]{3,2,1,0:T(4,128)} %get-tuple-element.10), channel_id=1, source_target_pairs={{4,8},{8,4},{12,16},{16,12},{20,24},{24,20},{28,0},{0,28},{5,9},{9... | collective-permute-start | bytes 368648 | tf_op jit(solution)/shard_map/ppermute | solution.py:193
  11.3 0.0 copy-done
  11.3 0.0 copy-done.1
  11.3 0.0 copy-done.2
  11.4 0.0 copy-done.3
  11.4 6.7 %shard_map.100 = f32[5,1,32,2048]{3,2,1,0:T(8,128)} custom-call(f32[128,384]{1,0:T(8,128)} %constant.73.clone.r_0_, f32[32,32]{1,0:T(8,128)} %constant.74.clone.r_1_, f32[1,32,2048]{2,1,0:T(8,128)} %r_2_.3, f32[3,1,32,2048]{3,2,1,0:T(8,128)} %r_3_.3, f32[1,32,2048]{2,1,0:T(8,128)} %r_4_.3), custom_call_target="tpu_custom_call" | custom-call | tf_op jit(solution)/shard_map/pallas_call | solution.py:203
  18.1 0.0 collective-permute-done.2
  18.1 0.0 collective-permute-done.3
  18.1 0.0 collective-permute-done
  18.1 0.2 collective-permute-done.1
  18.3 3.7 %fusion = f32[5,1,32,2048]{3,2,1,0:T(8,128)} fusion(f32[5,1,32,2048]{3,2,1,0:T(8,128)} %shard_map.100, f32[1,5,1,2048]{3,2,1,0:T(1,128)S(1)} %collective-permute-done.3, f32[1,5,1,2048]{3,2,1,0:T(1,128)S(1)} %collective-permute-done.2, f32[1,5,3,2048]{3,2,1,0:T(4,128)S(1)} %collective-permute-done.1, f32[1,5,3,2048]{3,2,1,0:T(4,128)S(1)} %collective-permute-done, ...), kind=kOutput, calls=%fused_computation.1 | convolution fusion | flops 32031488 | bytes 2950144 | tf_op jit(solution)/shard_map/pr,zfrx->fzpx/dot_general | solution.py:211
  (2 shorter events, 0.0 us)
Async XLA Ops:
  0.0 11.3 %copy-start = (f32[32,3]{0,1:T(4,128)S(1)}, f32[32,3]{0,1:T(4,128)}, u32[]{:S(2)}) copy-start(f32[32,3]{0,1:T(4,128)} %constant.70.clone) | copy-start | bytes 1156
  0.0 11.3 %copy-start.1 = (f32[32,3]{0,1:T(4,128)S(1)}, f32[32,3]{0,1:T(4,128)}, u32[]{:S(2)}) copy-start(f32[32,3]{0,1:T(4,128)} %constant.69.clone) | copy-start | bytes 1156
  0.0 11.3 %copy-start.2 = (f32[32,1]{0,1:T(1,128)S(1)}, f32[32,1]{0,1:T(1,128)}, u32[]{:S(2)}) copy-start(f32[32,1]{0,1:T(1,128)} %constant.72.clone) | copy-start | bytes 388
  0.0 11.3 %copy-start.3 = (f32[32,1]{0,1:T(1,128)S(1)}, f32[32,1]{0,1:T(1,128)}, u32[]{:S(2)}) copy-start(f32[32,1]{0,1:T(1,128)} %constant.71.clone) | copy-start | bytes 388
  3.0 15.1 %collective-permute-start.2 = (f32[1,5,1,2048]{3,2,1,0:T(1,128)}, f32[1,5,1,2048]{3,2,1,0:T(1,128)S(1)}, u32[]{:S(2)}, u32[]{:S(2)}) collective-permute-start(f32[1,5,1,2048]{3,2,1,0:T(1,128)} %get-tuple-element.11), channel_id=1, source_target_pairs={{0,8},{8,0},{4,12},{12,4},{16,24},{24,16},{20,28},{28,20},{1,9},{9... | collective-permute-start | bytes 122888 | tf_op jit(solution)/shard_map/ppermute | solution.py:193
  6.0 12.0 %collective-permute-start.3 = (f32[1,5,1,2048]{3,2,1,0:T(1,128)}, f32[1,5,1,2048]{3,2,1,0:T(1,128)S(1)}, u32[]{:S(2)}, u32[]{:S(2)}) collective-permute-start(f32[1,5,1,2048]{3,2,1,0:T(1,128)} %get-tuple-element.12), channel_id=1, source_target_pairs={{8,16},{16,8},{12,20},{20,12},{24,0},{0,24},{28,4},{4,28},{9,17},{... | collective-permute-start | bytes 122888 | tf_op jit(solution)/shard_map/ppermute | solution.py:193
  8.5 9.6 %collective-permute-start = (f32[1,5,3,2048]{3,2,1,0:T(4,128)}, f32[1,5,3,2048]{3,2,1,0:T(4,128)S(1)}, u32[]{:S(2)}, u32[]{:S(2)}) collective-permute-start(f32[1,5,3,2048]{3,2,1,0:T(4,128)} %get-tuple-element.9), channel_id=1, source_target_pairs={{0,4},{4,0},{8,12},{12,8},{16,20},{20,16},{24,28},{28,24},{1,5},{5... | collective-permute-start | bytes 368648 | tf_op jit(solution)/shard_map/ppermute | solution.py:193
  10.0 8.2 %collective-permute-start.1 = (f32[1,5,3,2048]{3,2,1,0:T(4,128)}, f32[1,5,3,2048]{3,2,1,0:T(4,128)S(1)}, u32[]{:S(2)}, u32[]{:S(2)}) collective-permute-start(f32[1,5,3,2048]{3,2,1,0:T(4,128)} %get-tuple-element.10), channel_id=1, source_target_pairs={{4,8},{8,4},{12,16},{16,12},{20,24},{24,20},{28,0},{0,28},{5,9},{9... | collective-permute-start | bytes 368648 | tf_op jit(solution)/shard_map/ppermute | solution.py:193

commit v8 on v7

--- a/solution.py
+++ b/solution.py
@@ -144,6 +144,12 @@
                 perm += [(r, up), (up, r)]
         plans.append((step, phase, step, groups - step, perm))
     return plans
+
+
+def correct_kernel(spread_ref, partial_ref, *refs):
+    recv_refs, out_ref = refs[:-1], refs[-1]
+    received = jnp.concatenate([r[0, 0] for r in recv_refs], axis=0)
+    out_ref[0, 0] = partial_ref[0, 0] - dot(spread_ref[...], received)
 
 
 def full_spec(shape):
@@ -207,10 +213,16 @@
             out_specs=out_spec,
             out_shape=out_shape,
         )(wx, jnp.asarray(own), density, momentum, energy)
-        received = jnp.concatenate(received, axis=2)
-        return partial - jnp.einsum(
-            "pr,zfrx->fzpx", spread, received, precision=HI
-        )
+        field_spec = pl.BlockSpec((1, 1, rows, count), lambda z, f: (f, z, 0, 0))
+        return pl.pallas_call(
+            correct_kernel,
+            grid=(planes, 5),
+            in_specs=[pl.BlockSpec(spread.shape, lambda z, f: (0, 0)), field_spec]
+            + [pl.BlockSpec((1, 1) + r.shape[2:], lambda z, f: (z, f, 0, 0)) for r in received],
+            out_specs=field_spec,
+            out_shape=out_shape,
+            input_output_aliases={1: 0},
+        )(spread, partial, *received)
 
     return local
 

time: 22.1 us -> 25.3 us (1.14)
  Pallas kernels: 9.7 us -> 14.7 us
  matrix products: 3.66 us -> 0 us
  local copies, waits for them, and re-layouts: 0.01 us -> 2.01 us
    pallas_call x0 -> x1, Pallas kernels: none -> 4.96 us  [local(): pl.pallas_call(correct_kernel, grid=(planes, 5), in_specs=[pl.BlockSpec(s...]
    dot_general x1 -> x0, matrix products: 3.66 us -> none  [local(): return partial - jnp.einsum('pr,zfrx->fzpx', spread, received, precision=HI)]
    unnamed x8 -> x16, local copies, waits for them, and re-layouts: 0.01 us -> 1.33 us
    concatenate x0 -> x1, local copies, waits for them, and re-layouts: none -> 0.67 us  [local(): spread = jnp.concatenate(spreads, axis=1)]
  transfers between devices with their start and end apart: 4 -> 4, of which waited for: 1 -> 0; matrix products, arithmetic and copies ran while one was open for 0% -> 3% of each run, Pallas kernels for 31% -> 27%
where the time goes in v8:
time: 25.3 us; the launch traced here: 25.1 us
  Pallas kernels  14.7 us (58%)
  starting transfers between devices  8.31 us (33%)
  local copies, waits for them, and re-layouts  2.01 us (8%)
    ppermute x4, starting transfers between devices, local(): received.append(lax.ppermute(message, 'row', perm))  8.31 us
    pallas_call x1, Pallas kernels, local(): pl.pallas_call(lambda *r: local_kernel(count, *r), grid=(planes,), in_spe...  6.7 us
    pallas_call x1, Pallas kernels, local(): pl.pallas_call(correct_kernel, grid=(planes, 5), in_specs=[pl.BlockSpec(s...  4.96 us
    pallas_call x1, Pallas kernels, local(): pl.pallas_call(lambda *r: moments_kernel(split_of, choices, *r), grid=(pl...  3.02 us
    unnamed x16, local copies, waits for them, and re-layouts  1.33 us
    concatenate x1, local copies, waits for them, and re-layouts, local(): spread = jnp.concatenate(spreads, axis=1)  0.67 us
  transfers between devices with their start and end apart: 4, of which 0 were waited for; matrix products, arithmetic and copies ran while one was open for 3% of the time, Pallas kernels for 27%

profile of v8, /device:TPU:0, one launch (start us, length us, event | category | flops | bytes accessed | tf_op | source)
XLA Modules:
  0.0 25.1 jit_solution(3849092660083412907)
XLA Ops:
  0.0 0.0 copy-start.4
  0.0 0.0 copy-start.5
  0.0 0.0 copy-start.6
  0.0 0.0 copy-start.7
  0.0 3.0 %shard_map.101 = (f32[1,5,3,2048]{3,2,1,0:T(4,128)}, f32[1,5,3,2048]{3,2,1,0:T(4,128)}, f32[1,5,1,2048]{3,2,1,0:T(1,128)}, f32[1,5,1,2048]{3,2,1,0:T(1,128)}) custom-call(s32[1]{0:T(128)} %bitcast.r_0_, f32[8,32]{1,0:T(8,128)} %constant.68.clone.r_1_, f32[1,32,2048]{2,1,0:T(8,128)} %r_2_.3, f32[3,1,32,2048]{3,2,1,0:T(8,128)} %r_3_.3, f32[1,32,2048]{2,1,0:T(8,128)} %r_4_.3), custom_call_target="tpu_custom_call" | custom-call | tf_op jit(solution)/shard_map/pallas_call | solution.py:188
  3.0 3.0 %collective-permute-start.2 = (f32[1,5,1,2048]{3,2,1,0:T(1,128)}, f32[1,5,1,2048]{3,2,1,0:T(1,128)S(1)}, u32[]{:S(2)}, u32[]{:S(2)}) collective-permute-start(f32[1,5,1,2048]{3,2,1,0:T(1,128)} %get-tuple-element.11), channel_id=1, source_target_pairs={{0,8},{8,0},{4,12},{12,4},{16,24},{24,16},{20,28},{28,20},{1,9},{9... | collective-permute-start | bytes 122888 | tf_op jit(solution)/shard_map/ppermute | solution.py:199
  6.1 2.5 %collective-permute-start.3 = (f32[1,5,1,2048]{3,2,1,0:T(1,128)}, f32[1,5,1,2048]{3,2,1,0:T(1,128)S(1)}, u32[]{:S(2)}, u32[]{:S(2)}) collective-permute-start(f32[1,5,1,2048]{3,2,1,0:T(1,128)} %get-tuple-element.12), channel_id=1, source_target_pairs={{8,16},{16,8},{12,20},{20,12},{24,0},{0,24},{28,4},{4,28},{9,17},{... | collective-permute-start | bytes 122888 | tf_op jit(solution)/shard_map/ppermute | solution.py:199
  8.5 1.5 %collective-permute-start = (f32[1,5,3,2048]{3,2,1,0:T(4,128)}, f32[1,5,3,2048]{3,2,1,0:T(4,128)S(1)}, u32[]{:S(2)}, u32[]{:S(2)}) collective-permute-start(f32[1,5,3,2048]{3,2,1,0:T(4,128)} %get-tuple-element.9), channel_id=1, source_target_pairs={{0,4},{4,0},{8,12},{12,8},{16,20},{20,16},{24,28},{28,24},{1,5},{5... | collective-permute-start | bytes 368648 | tf_op jit(solution)/shard_map/ppermute | solution.py:199
  10.0 1.3 %collective-permute-start.1 = (f32[1,5,3,2048]{3,2,1,0:T(4,128)}, f32[1,5,3,2048]{3,2,1,0:T(4,128)S(1)}, u32[]{:S(2)}, u32[]{:S(2)}) collective-permute-start(f32[1,5,3,2048]{3,2,1,0:T(4,128)} %get-tuple-element.10), channel_id=1, source_target_pairs={{4,8},{8,4},{12,16},{16,12},{20,24},{24,20},{28,0},{0,28},{5,9},{9... | collective-permute-start | bytes 368648 | tf_op jit(solution)/shard_map/ppermute | solution.py:199
  11.3 0.0 copy-done.4
  11.3 0.0 copy-done.5
  11.4 0.0 copy-done.6
  11.4 0.0 copy-done.7
  11.4 0.7 %copy.12.spread_ref = f32[32,8]{1,0:T(8,128)} copy(f32[32,8]{0,1:T(8,128)S(1)} %pad_maximum_fusion) | data formatting | bytes 2048 | tf_op jit(solution)/shard_map/concatenate | solution.py:205
  12.1 6.7 %shard_map.100.partial_ref = f32[5,1,32,2048]{3,2,1,0:T(8,128)} custom-call(f32[128,384]{1,0:T(8,128)} %constant.73.clone.r_0_, f32[32,32]{1,0:T(8,128)} %constant.74.clone.r_1_, f32[1,32,2048]{2,1,0:T(8,128)} %r_2_.3, f32[3,1,32,2048]{3,2,1,0:T(8,128)} %r_3_.3, f32[1,32,2048]{2,1,0:T(8,128)} %r_4_.3), custom_call_target="tpu_custom_call" | custom-call | tf_op jit(solution)/shard_map/pallas_call | solution.py:209
  18.8 0.0 collective-permute-done.2.refs_2_
  18.8 0.0 copy-start.2
  18.8 0.0 collective-permute-done.3.refs_3_
  18.8 0.0 copy-start.3
  18.8 0.0 collective-permute-done.refs_0_
  18.8 0.0 copy-start
  18.8 0.0 collective-permute-done.1.refs_1_
  18.8 0.6 %copy-done.2 = f32[1,5,1,2048]{3,2,1,0:T(1,128)} copy-done((f32[1,5,1,2048]{3,2,1,0:T(1,128)}, f32[1,5,1,2048]{3,2,1,0:T(1,128)S(1)}, u32[]{:S(2)}) %copy-start.2) | copy-done | bytes 40984
  19.4 0.0 copy-done.3
  19.4 0.0 copy-done
  19.5 0.0 copy-start.1
  19.5 0.7 %copy-done.1 = f32[1,5,3,2048]{3,2,1,0:T(4,128)} copy-done((f32[1,5,3,2048]{3,2,1,0:T(4,128)}, f32[1,5,3,2048]{3,2,1,0:T(4,128)S(1)}, u32[]{:S(2)}) %copy-start.1) | copy-done | bytes 122904
  20.1 5.0 %shard_map.102 = f32[5,1,32,2048]{3,2,1,0:T(8,128)} custom-call(f32[32,8]{1,0:T(8,128)} %copy.12.spread_ref, f32[5,1,32,2048]{3,2,1,0:T(8,128)} %shard_map.100.partial_ref, f32[1,5,3,2048]{3,2,1,0:T(4,128)} %copy-done, f32[1,5,3,2048]{3,2,1,0:T(4,128)} %copy-done.1, f32[1,5,1,2048]{3,2,1,0:T(1,128)} %copy-done.2, ...), custom_call_target="tpu_custom_call", output_to_operand_aliasing={{}: (1, {})} | custom-call | tf_op jit(solution)/shard_map/pallas_call | solution.py:217
  (3 shorter events, 0.0 us)
Async XLA Ops:
  0.0 11.3 %copy-start.4 = (f32[32,3]{0,1:T(4,128)S(1)}, f32[32,3]{0,1:T(4,128)}, u32[]{:S(2)}) copy-start(f32[32,3]{0,1:T(4,128)} %constant.70.clone) | copy-start | bytes 1156
  0.0 11.3 %copy-start.5 = (f32[32,3]{0,1:T(4,128)S(1)}, f32[32,3]{0,1:T(4,128)}, u32[]{:S(2)}) copy-start(f32[32,3]{0,1:T(4,128)} %constant.69.clone) | copy-start | bytes 1156
  0.0 11.3 %copy-start.6 = (f32[32,1]{0,1:T(1,128)S(1)}, f32[32,1]{0,1:T(1,128)}, u32[]{:S(2)}) copy-start(f32[32,1]{0,1:T(1,128)} %constant.72.clone) | copy-start | bytes 388
  0.0 11.4 %copy-start.7 = (f32[32,1]{0,1:T(1,128)S(1)}, f32[32,1]{0,1:T(1,128)}, u32[]{:S(2)}) copy-start(f32[32,1]{0,1:T(1,128)} %constant.71.clone) | copy-start | bytes 388
  3.0 15.8 %collective-permute-start.2 = (f32[1,5,1,2048]{3,2,1,0:T(1,128)}, f32[1,5,1,2048]{3,2,1,0:T(1,128)S(1)}, u32[]{:S(2)}, u32[]{:S(2)}) collective-permute-start(f32[1,5,1,2048]{3,2,1,0:T(1,128)} %get-tuple-element.11), channel_id=1, source_target_pairs={{0,8},{8,0},{4,12},{12,4},{16,24},{24,16},{20,28},{28,20},{1,9},{9... | collective-permute-start | bytes 122888 | tf_op jit(solution)/shard_map/ppermute | solution.py:199
  6.1 12.7 %collective-permute-start.3 = (f32[1,5,1,2048]{3,2,1,0:T(1,128)}, f32[1,5,1,2048]{3,2,1,0:T(1,128)S(1)}, u32[]{:S(2)}, u32[]{:S(2)}) collective-permute-start(f32[1,5,1,2048]{3,2,1,0:T(1,128)} %get-tuple-element.12), channel_id=1, source_target_pairs={{8,16},{16,8},{12,20},{20,12},{24,0},{0,24},{28,4},{4,28},{9,17},{... | collective-permute-start | bytes 122888 | tf_op jit(solution)/shard_map/ppermute | solution.py:199
  8.5 10.3 %collective-permute-start = (f32[1,5,3,2048]{3,2,1,0:T(4,128)}, f32[1,5,3,2048]{3,2,1,0:T(4,128)S(1)}, u32[]{:S(2)}, u32[]{:S(2)}) collective-permute-start(f32[1,5,3,2048]{3,2,1,0:T(4,128)} %get-tuple-element.9), channel_id=1, source_target_pairs={{0,4},{4,0},{8,12},{12,8},{16,20},{20,16},{24,28},{28,24},{1,5},{5... | collective-permute-start | bytes 368648 | tf_op jit(solution)/shard_map/ppermute | solution.py:199
  10.0 8.8 %collective-permute-start.1 = (f32[1,5,3,2048]{3,2,1,0:T(4,128)}, f32[1,5,3,2048]{3,2,1,0:T(4,128)S(1)}, u32[]{:S(2)}, u32[]{:S(2)}) collective-permute-start(f32[1,5,3,2048]{3,2,1,0:T(4,128)} %get-tuple-element.10), channel_id=1, source_target_pairs={{4,8},{8,4},{12,16},{16,12},{20,24},{24,20},{28,0},{0,28},{5,9},{9... | collective-permute-start | bytes 368648 | tf_op jit(solution)/shard_map/ppermute | solution.py:199
  18.8 0.6 %copy-start.2 = (f32[1,5,1,2048]{3,2,1,0:T(1,128)}, f32[1,5,1,2048]{3,2,1,0:T(1,128)S(1)}, u32[]{:S(2)}) copy-start(f32[1,5,1,2048]{3,2,1,0:T(1,128)S(1)} %collective-permute-done.2.refs_2_) | copy-start | bytes 122884
  18.8 0.6 %copy-start.3 = (f32[1,5,1,2048]{3,2,1,0:T(1,128)}, f32[1,5,1,2048]{3,2,1,0:T(1,128)S(1)}, u32[]{:S(2)}) copy-start(f32[1,5,1,2048]{3,2,1,0:T(1,128)S(1)} %collective-permute-done.3.refs_3_) | copy-start | bytes 122884
  18.8 0.7 %copy-start = (f32[1,5,3,2048]{3,2,1,0:T(4,128)}, f32[1,5,3,2048]{3,2,1,0:T(4,128)S(1)}, u32[]{:S(2)}) copy-start(f32[1,5,3,2048]{3,2,1,0:T(4,128)S(1)} %collective-permute-done.refs_0_) | copy-start | bytes 368644
  19.5 0.7 %copy-start.1 = (f32[1,5,3,2048]{3,2,1,0:T(4,128)}, f32[1,5,3,2048]{3,2,1,0:T(4,128)S(1)}, u32[]{:S(2)}) copy-start(f32[1,5,3,2048]{3,2,1,0:T(4,128)S(1)} %collective-permute-done.1.refs_1_) | copy-start | bytes 368644

commit v9 on v7

--- a/solution.py
+++ b/solution.py
@@ -114,8 +114,9 @@
     wx = wx_ref[...]
     own = own_ref[...]
     nb = count // WIDTH
+    d_all = dot(own, jnp.concatenate(flux_y, axis=1))
     for f in range(5):
-        d_y = dot(own, flux_y[f])
+        d_y = d_all[:, f * count : (f + 1) * count]
         fx = flux_x[f]
         rows = fx.shape[0]
         stacked = jnp.concatenate([fx[:, b * WIDTH : (b + 1) * WIDTH] for b in range(nb)], axis=0)

time: 22.1 us -> 22.1 us (level)
  transfers between devices with their start and end apart: 4 -> 4, of which waited for: 1 -> 1; matrix products, arithmetic and copies ran while one was open for 0% -> 0% of each run, Pallas kernels for 31% -> 30%
where the time goes in v9:
time: 22.1 us; the launch traced here: 21.9 us
  Pallas kernels  9.66 us (44%)
  starting transfers between devices  8.31 us (38%)
  matrix products  3.66 us (17%)
  waiting for transfers between devices  0.23 us (1%)
    ppermute x4, starting transfers between devices, local(): received.append(lax.ppermute(message, 'row', perm))  8.31 us
    pallas_call x1, Pallas kernels, local(): pl.pallas_call(lambda *r: local_kernel(count, *r), grid=(planes,), in_spe...  6.65 us
    dot_general x1, matrix products, local(): return partial - jnp.einsum('pr,zfrx->fzpx', spread, received, precision=HI)  3.66 us
    pallas_call x1, Pallas kernels, local(): pl.pallas_call(lambda *r: moments_kernel(split_of, choices, *r), grid=(pl...  3.01 us
  transfers between devices with their start and end apart: 4, of which 1 were waited for; matrix products, arithmetic and copies ran while one was open for 0% of the time, Pallas kernels for 30%

profile of v9, /device:TPU:0, one launch (start us, length us, event | category | flops | bytes accessed | tf_op | source)
XLA Modules:
  0.0 21.9 jit_solution(2328948215148020963)
XLA Ops:
  0.0 0.0 copy-start
  0.0 0.0 copy-start.1
  0.0 0.0 copy-start.2
  0.0 0.0 copy-start.3
  0.0 3.0 %shard_map.101 = (f32[1,5,3,2048]{3,2,1,0:T(4,128)}, f32[1,5,3,2048]{3,2,1,0:T(4,128)}, f32[1,5,1,2048]{3,2,1,0:T(1,128)}, f32[1,5,1,2048]{3,2,1,0:T(1,128)}) custom-call(s32[1]{0:T(128)} %bitcast.r_0_, f32[8,32]{1,0:T(8,128)} %constant.68.clone.r_1_, f32[1,32,2048]{2,1,0:T(8,128)} %r_2_.3, f32[3,1,32,2048]{3,2,1,0:T(8,128)} %r_3_.3, f32[1,32,2048]{2,1,0:T(8,128)} %r_4_.3), custom_call_target="tpu_custom_call" | custom-call | tf_op jit(solution)/shard_map/pallas_call | solution.py:183
  3.0 3.0 %collective-permute-start.2 = (f32[1,5,1,2048]{3,2,1,0:T(1,128)}, f32[1,5,1,2048]{3,2,1,0:T(1,128)S(1)}, u32[]{:S(2)}, u32[]{:S(2)}) collective-permute-start(f32[1,5,1,2048]{3,2,1,0:T(1,128)} %get-tuple-element.11), channel_id=1, source_target_pairs={{0,8},{8,0},{4,12},{12,4},{16,24},{24,16},{20,28},{28,20},{1,9},{9... | collective-permute-start | bytes 122888 | tf_op jit(solution)/shard_map/ppermute | solution.py:194
  6.0 2.5 %collective-permute-start.3 = (f32[1,5,1,2048]{3,2,1,0:T(1,128)}, f32[1,5,1,2048]{3,2,1,0:T(1,128)S(1)}, u32[]{:S(2)}, u32[]{:S(2)}) collective-permute-start(f32[1,5,1,2048]{3,2,1,0:T(1,128)} %get-tuple-element.12), channel_id=1, source_target_pairs={{8,16},{16,8},{12,20},{20,12},{24,0},{0,24},{28,4},{4,28},{9,17},{... | collective-permute-start | bytes 122888 | tf_op jit(solution)/shard_map/ppermute | solution.py:194
  8.5 1.5 %collective-permute-start = (f32[1,5,3,2048]{3,2,1,0:T(4,128)}, f32[1,5,3,2048]{3,2,1,0:T(4,128)S(1)}, u32[]{:S(2)}, u32[]{:S(2)}) collective-permute-start(f32[1,5,3,2048]{3,2,1,0:T(4,128)} %get-tuple-element.9), channel_id=1, source_target_pairs={{0,4},{4,0},{8,12},{12,8},{16,20},{20,16},{24,28},{28,24},{1,5},{5... | collective-permute-start | bytes 368648 | tf_op jit(solution)/shard_map/ppermute | solution.py:194
  10.0 1.3 %collective-permute-start.1 = (f32[1,5,3,2048]{3,2,1,0:T(4,128)}, f32[1,5,3,2048]{3,2,1,0:T(4,128)S(1)}, u32[]{:S(2)}, u32[]{:S(2)}) collective-permute-start(f32[1,5,3,2048]{3,2,1,0:T(4,128)} %get-tuple-element.10), channel_id=1, source_target_pairs={{4,8},{8,4},{12,16},{16,12},{20,24},{24,20},{28,0},{0,28},{5,9},{9... | collective-permute-start | bytes 368648 | tf_op jit(solution)/shard_map/ppermute | solution.py:194
  11.3 0.0 copy-done
  11.3 0.0 copy-done.1
  11.3 0.0 copy-done.2
  11.4 0.0 copy-done.3
  11.4 6.7 %shard_map.100 = f32[5,1,32,2048]{3,2,1,0:T(8,128)} custom-call(f32[128,384]{1,0:T(8,128)} %constant.73.clone.r_0_, f32[32,32]{1,0:T(8,128)} %constant.74.clone.r_1_, f32[1,32,2048]{2,1,0:T(8,128)} %r_2_.3, f32[3,1,32,2048]{3,2,1,0:T(8,128)} %r_3_.3, f32[1,32,2048]{2,1,0:T(8,128)} %r_4_.3), custom_call_target="tpu_custom_call" | custom-call | tf_op jit(solution)/shard_map/pallas_call | solution.py:204
  18.0 0.0 collective-permute-done.2
  18.0 0.0 collective-permute-done.3
  18.0 0.0 collective-permute-done
  18.0 0.2 collective-permute-done.1
  18.3 3.7 %fusion = f32[5,1,32,2048]{3,2,1,0:T(8,128)} fusion(f32[5,1,32,2048]{3,2,1,0:T(8,128)} %shard_map.100, f32[1,5,1,2048]{3,2,1,0:T(1,128)S(1)} %collective-permute-done.3, f32[1,5,1,2048]{3,2,1,0:T(1,128)S(1)} %collective-permute-done.2, f32[1,5,3,2048]{3,2,1,0:T(4,128)S(1)} %collective-permute-done.1, f32[1,5,3,2048]{3,2,1,0:T(4,128)S(1)} %collective-permute-done, ...), kind=kOutput, calls=%fused_computation.1 | convolution fusion | flops 32031488 | bytes 2950144 | tf_op jit(solution)/shard_map/pr,zfrx->fzpx/dot_general | solution.py:212
  (2 shorter events, 0.0 us)
Async XLA Ops:
  0.0 11.3 %copy-start = (f32[32,3]{0,1:T(4,128)S(1)}, f32[32,3]{0,1:T(4,128)}, u32[]{:S(2)}) copy-start(f32[32,3]{0,1:T(4,128)} %constant.70.clone) | copy-start | bytes 1156
  0.0 11.3 %copy-start.1 = (f32[32,3]{0,1:T(4,128)S(1)}, f32[32,3]{0,1:T(4,128)}, u32[]{:S(2)}) copy-start(f32[32,3]{0,1:T(4,128)} %constant.69.clone) | copy-start | bytes 1156
  0.0 11.3 %copy-start.2 = (f32[32,1]{0,1:T(1,128)S(1)}, f32[32,1]{0,1:T(1,128)}, u32[]{:S(2)}) copy-start(f32[32,1]{0,1:T(1,128)} %constant.72.clone) | copy-start | bytes 388
  0.0 11.3 %copy-start.3 = (f32[32,1]{0,1:T(1,128)S(1)}, f32[32,1]{0,1:T(1,128)}, u32[]{:S(2)}) copy-start(f32[32,1]{0,1:T(1,128)} %constant.71.clone) | copy-start | bytes 388
  3.0 15.0 %collective-permute-start.2 = (f32[1,5,1,2048]{3,2,1,0:T(1,128)}, f32[1,5,1,2048]{3,2,1,0:T(1,128)S(1)}, u32[]{:S(2)}, u32[]{:S(2)}) collective-permute-start(f32[1,5,1,2048]{3,2,1,0:T(1,128)} %get-tuple-element.11), channel_id=1, source_target_pairs={{0,8},{8,0},{4,12},{12,4},{16,24},{24,16},{20,28},{28,20},{1,9},{9... | collective-permute-start | bytes 122888 | tf_op jit(solution)/shard_map/ppermute | solution.py:194
  6.0 12.0 %collective-permute-start.3 = (f32[1,5,1,2048]{3,2,1,0:T(1,128)}, f32[1,5,1,2048]{3,2,1,0:T(1,128)S(1)}, u32[]{:S(2)}, u32[]{:S(2)}) collective-permute-start(f32[1,5,1,2048]{3,2,1,0:T(1,128)} %get-tuple-element.12), channel_id=1, source_target_pairs={{8,16},{16,8},{12,20},{20,12},{24,0},{0,24},{28,4},{4,28},{9,17},{... | collective-permute-start | bytes 122888 | tf_op jit(solution)/shard_map/ppermute | solution.py:194
  8.5 9.5 %collective-permute-start = (f32[1,5,3,2048]{3,2,1,0:T(4,128)}, f32[1,5,3,2048]{3,2,1,0:T(4,128)S(1)}, u32[]{:S(2)}, u32[]{:S(2)}) collective-permute-start(f32[1,5,3,2048]{3,2,1,0:T(4,128)} %get-tuple-element.9), channel_id=1, source_target_pairs={{0,4},{4,0},{8,12},{12,8},{16,20},{20,16},{24,28},{28,24},{1,5},{5... | collective-permute-start | bytes 368648 | tf_op jit(solution)/shard_map/ppermute | solution.py:194
  10.0 8.2 %collective-permute-start.1 = (f32[1,5,3,2048]{3,2,1,0:T(4,128)}, f32[1,5,3,2048]{3,2,1,0:T(4,128)S(1)}, u32[]{:S(2)}, u32[]{:S(2)}) collective-permute-start(f32[1,5,3,2048]{3,2,1,0:T(4,128)} %get-tuple-element.10), channel_id=1, source_target_pairs={{4,8},{8,4},{12,16},{16,12},{20,24},{24,20},{28,0},{0,28},{5,9},{9... | collective-permute-start | bytes 368648 | tf_op jit(solution)/shard_map/ppermute | solution.py:194

commit v10 on v7

--- a/solution.py
+++ b/solution.py
@@ -109,14 +109,28 @@
             out_ref[0, f] = jnp.where(pick, moments[lo:hi], moments[lo2:hi2])
 
 
-def local_kernel(count, wx_ref, own_ref, rho_ref, mom_ref, energy_ref, out_ref):
-    flux_x, flux_y = plane_fluxes(rho_ref, mom_ref, energy_ref)
+def local_kernel(
+    count, wx_ref, own_ref, rho_hbm, mom_hbm, energy_hbm, out_hbm,
+    rho_v, mom_v, energy_v, out_v, in_sem, out_sem,
+):
+    z = pl.program_id(0)
+    plane = pl.ds(z, 1)
+    loads = [
+        pltpu.make_async_copy(mom_hbm.at[0, plane], mom_v.at[0], in_sem.at[0]),
+        pltpu.make_async_copy(mom_hbm.at[1, plane], mom_v.at[1], in_sem.at[1]),
+        pltpu.make_async_copy(rho_hbm.at[plane], rho_v, in_sem.at[2]),
+        pltpu.make_async_copy(mom_hbm.at[2, plane], mom_v.at[2], in_sem.at[3]),
+        pltpu.make_async_copy(energy_hbm.at[plane], energy_v, in_sem.at[4]),
+    ]
+    for copy in loads:
+        copy.start()
     wx = wx_ref[...]
     own = own_ref[...]
     nb = count // WIDTH
-    for f in range(5):
-        d_y = dot(own, flux_y[f])
-        fx = flux_x[f]
+    stores = []
+
+    def emit(f, fx, fy):
+        d_y = dot(own, fy)
         rows = fx.shape[0]
         stacked = jnp.concatenate([fx[:, b * WIDTH : (b + 1) * WIDTH] for b in range(nb)], axis=0)
         parts = dot(stacked, wx)
@@ -128,7 +142,21 @@
                 + parts[b * rows : (b + 1) * rows, WIDTH : 2 * WIDTH]
                 + parts[bn * rows : (bn + 1) * rows, 2 * WIDTH :]
             )
-            out_ref[f, 0, :, b * WIDTH : (b + 1) * WIDTH] = -(d_x + d_y[:, b * WIDTH : (b + 1) * WIDTH])
+            out_v[f, 0, :, b * WIDTH : (b + 1) * WIDTH] = -(d_x + d_y[:, b * WIDTH : (b + 1) * WIDTH])
+        store = pltpu.make_async_copy(out_v.at[f], out_hbm.at[f, plane], out_sem.at[f])
+        store.start()
+        stores.append(store)
+
+    loads[0].wait()
+    loads[1].wait()
+    emit(0, mom_v[0, 0], mom_v[1, 0])
+    for copy in loads[2:]:
+        copy.wait()
+    flux_x, flux_y = plane_fluxes(rho_v, mom_v, energy_v)
+    for f in range(1, 5):
+        emit(f, flux_x[f], flux_y[f])
+    for store in stores:
+        store.wait()
 
 
 def exchange_plan(groups, shift_list):
@@ -200,12 +228,21 @@
         wx = block_weights(count)
         out_spec = pl.BlockSpec((5, 1, rows, count), lambda z: (0, z, 0, 0))
         out_shape = jax.ShapeDtypeStruct((5, planes, rows, count), jnp.float32)
+        hbm = pl.BlockSpec(memory_space=pl.ANY)
         partial = pl.pallas_call(
             lambda *r: local_kernel(count, *r),
             grid=(planes,),
-            in_specs=[full_spec(wx.shape), full_spec(own.shape)] + plane_specs,
-            out_specs=out_spec,
+            in_specs=[full_spec(wx.shape), full_spec(own.shape), hbm, hbm, hbm],
+            out_specs=hbm,
             out_shape=out_shape,
+            scratch_shapes=[
+                pltpu.VMEM((1, rows, count), jnp.float32),
+                pltpu.VMEM((3, 1, rows, count), jnp.float32),
+                pltpu.VMEM((1, rows, count), jnp.float32),
+                pltpu.VMEM((5, 1, rows, count), jnp.float32),
+                pltpu.SemaphoreType.DMA((5,)),
+                pltpu.SemaphoreType.DMA((5,)),
+            ],
         )(wx, jnp.asarray(own), density, momentum, energy)
         received = jnp.concatenate(received, axis=2)
         return partial - jnp.einsum(

time: 22.1 us -> 22.6 us (1.023)
  Pallas kernels: 9.7 us -> 10.3 us
    pallas_call x1, Pallas kernels: 6.7 us -> 7.26 us  [local(): pl.pallas_call(lambda *r: local_kernel(count, *r), grid=(planes,), in_spe...]
  transfers between devices with their start and end apart: 4 -> 4, of which waited for: 1 -> 0; matrix products, arithmetic and copies ran while one was open for 0% -> 0% of each run, Pallas kernels for 31% -> 32%
where the time goes in v10:
time: 22.6 us; the launch traced here: 22.4 us
  Pallas kernels  10.3 us (46%)
  starting transfers between devices  8.31 us (37%)
  matrix products  3.68 us (16%)
    ppermute x4, starting transfers between devices, local(): received.append(lax.ppermute(message, 'row', perm))  8.31 us
    pallas_call x1, Pallas kernels, local(): pl.pallas_call(lambda *r: local_kernel(count, *r), grid=(planes,), in_spe...  7.26 us
    dot_general x1, matrix products, local(): return partial - jnp.einsum('pr,zfrx->fzpx', spread, received, precision=HI)  3.68 us
    pallas_call x1, Pallas kernels, local(): pl.pallas_call(lambda *r: moments_kernel(split_of, choices, *r), grid=(pl...  3.01 us
  transfers between devices with their start and end apart: 4, of which 0 were waited for; matrix products, arithmetic and copies ran while one was open for 0% of the time, Pallas kernels for 32%

profile of v10, /device:TPU:0, one launch (start us, length us, event | category | flops | bytes accessed | tf_op | source)
XLA Modules:
  0.0 22.4 jit_solution(5209525611205496066)
XLA Ops:
  0.0 0.0 copy-start
  0.0 0.0 copy-start.1
  0.0 0.0 copy-start.2
  0.0 0.0 copy-start.3
  0.0 3.0 %shard_map.101 = (f32[1,5,3,2048]{3,2,1,0:T(4,128)}, f32[1,5,3,2048]{3,2,1,0:T(4,128)}, f32[1,5,1,2048]{3,2,1,0:T(1,128)}, f32[1,5,1,2048]{3,2,1,0:T(1,128)}) custom-call(s32[1]{0:T(128)} %bitcast.r_0_, f32[8,32]{1,0:T(8,128)} %constant.68.clone.r_1_, f32[1,32,2048]{2,1,0:T(8,128)} %r_2_.3, f32[3,1,32,2048]{3,2,1,0:T(8,128)} %r_3_.3, f32[1,32,2048]{2,1,0:T(8,128)} %r_4_.3), custom_call_target="tpu_custom_call" | custom-call | tf_op jit(solution)/shard_map/pallas_call | solution.py:210
  3.0 3.0 %collective-permute-start.2 = (f32[1,5,1,2048]{3,2,1,0:T(1,128)}, f32[1,5,1,2048]{3,2,1,0:T(1,128)S(1)}, u32[]{:S(2)}, u32[]{:S(2)}) collective-permute-start(f32[1,5,1,2048]{3,2,1,0:T(1,128)} %get-tuple-element.11), channel_id=1, source_target_pairs={{0,8},{8,0},{4,12},{12,4},{16,24},{24,16},{20,28},{28,20},{1,9},{9... | collective-permute-start | bytes 122888 | tf_op jit(solution)/shard_map/ppermute | solution.py:221
  6.0 2.5 %collective-permute-start.3 = (f32[1,5,1,2048]{3,2,1,0:T(1,128)}, f32[1,5,1,2048]{3,2,1,0:T(1,128)S(1)}, u32[]{:S(2)}, u32[]{:S(2)}) collective-permute-start(f32[1,5,1,2048]{3,2,1,0:T(1,128)} %get-tuple-element.12), channel_id=1, source_target_pairs={{8,16},{16,8},{12,20},{20,12},{24,0},{0,24},{28,4},{4,28},{9,17},{... | collective-permute-start | bytes 122888 | tf_op jit(solution)/shard_map/ppermute | solution.py:221
  8.5 1.5 %collective-permute-start = (f32[1,5,3,2048]{3,2,1,0:T(4,128)}, f32[1,5,3,2048]{3,2,1,0:T(4,128)S(1)}, u32[]{:S(2)}, u32[]{:S(2)}) collective-permute-start(f32[1,5,3,2048]{3,2,1,0:T(4,128)} %get-tuple-element.9), channel_id=1, source_target_pairs={{0,4},{4,0},{8,12},{12,8},{16,20},{20,16},{24,28},{28,24},{1,5},{5... | collective-permute-start | bytes 368648 | tf_op jit(solution)/shard_map/ppermute | solution.py:221
  10.0 1.3 %collective-permute-start.1 = (f32[1,5,3,2048]{3,2,1,0:T(4,128)}, f32[1,5,3,2048]{3,2,1,0:T(4,128)S(1)}, u32[]{:S(2)}, u32[]{:S(2)}) collective-permute-start(f32[1,5,3,2048]{3,2,1,0:T(4,128)} %get-tuple-element.10), channel_id=1, source_target_pairs={{4,8},{8,4},{12,16},{16,12},{20,24},{24,20},{28,0},{0,28},{5,9},{9... | collective-permute-start | bytes 368648 | tf_op jit(solution)/shard_map/ppermute | solution.py:221
  11.3 0.0 copy-done
  11.3 0.0 copy-done.1
  11.3 0.0 copy-done.2
  11.4 0.0 copy-done.3
  11.4 7.3 %shard_map.100 = f32[5,1,32,2048]{3,2,1,0:T(8,128)} custom-call(f32[128,384]{1,0:T(8,128)} %constant.73.clone.r_0_, f32[32,32]{1,0:T(8,128)} %constant.74.clone.r_1_, f32[1,32,2048]{2,1,0:T(8,128)} %r_2_.3, f32[3,1,32,2048]{3,2,1,0:T(8,128)} %r_3_.3, f32[1,32,2048]{2,1,0:T(8,128)} %r_4_.3), custom_call_target="tpu_custom_call" | custom-call | tf_op jit(solution)/shard_map/pallas_call | solution.py:232
  18.6 0.0 collective-permute-done.2
  18.7 0.0 collective-permute-done.3
  18.7 0.0 collective-permute-done
  18.7 0.0 collective-permute-done.1
  18.7 3.7 %fusion = f32[5,1,32,2048]{3,2,1,0:T(8,128)} fusion(f32[5,1,32,2048]{3,2,1,0:T(8,128)} %shard_map.100, f32[1,5,1,2048]{3,2,1,0:T(1,128)S(1)} %collective-permute-done.3, f32[1,5,1,2048]{3,2,1,0:T(1,128)S(1)} %collective-permute-done.2, f32[1,5,3,2048]{3,2,1,0:T(4,128)S(1)} %collective-permute-done.1, f32[1,5,3,2048]{3,2,1,0:T(4,128)S(1)} %collective-permute-done, ...), kind=kOutput, calls=%fused_computation.1 | convolution fusion | flops 32031488 | bytes 2950144 | tf_op jit(solution)/shard_map/pr,zfrx->fzpx/dot_general | solution.py:248
  (2 shorter events, 0.0 us)
Async XLA Ops:
  0.0 11.3 %copy-start = (f32[32,3]{0,1:T(4,128)S(1)}, f32[32,3]{0,1:T(4,128)}, u32[]{:S(2)}) copy-start(f32[32,3]{0,1:T(4,128)} %constant.70.clone) | copy-start | bytes 1156
  0.0 11.3 %copy-start.1 = (f32[32,3]{0,1:T(4,128)S(1)}, f32[32,3]{0,1:T(4,128)}, u32[]{:S(2)}) copy-start(f32[32,3]{0,1:T(4,128)} %constant.69.clone) | copy-start | bytes 1156
  0.0 11.3 %copy-start.2 = (f32[32,1]{0,1:T(1,128)S(1)}, f32[32,1]{0,1:T(1,128)}, u32[]{:S(2)}) copy-start(f32[32,1]{0,1:T(1,128)} %constant.72.clone) | copy-start | bytes 388
  0.0 11.3 %copy-start.3 = (f32[32,1]{0,1:T(1,128)S(1)}, f32[32,1]{0,1:T(1,128)}, u32[]{:S(2)}) copy-start(f32[32,1]{0,1:T(1,128)} %constant.71.clone) | copy-start | bytes 388
  3.0 15.6 %collective-permute-start.2 = (f32[1,5,1,2048]{3,2,1,0:T(1,128)}, f32[1,5,1,2048]{3,2,1,0:T(1,128)S(1)}, u32[]{:S(2)}, u32[]{:S(2)}) collective-permute-start(f32[1,5,1,2048]{3,2,1,0:T(1,128)} %get-tuple-element.11), channel_id=1, source_target_pairs={{0,8},{8,0},{4,12},{12,4},{16,24},{24,16},{20,28},{28,20},{1,9},{9... | collective-permute-start | bytes 122888 | tf_op jit(solution)/shard_map/ppermute | solution.py:221
  6.0 12.6 %collective-permute-start.3 = (f32[1,5,1,2048]{3,2,1,0:T(1,128)}, f32[1,5,1,2048]{3,2,1,0:T(1,128)S(1)}, u32[]{:S(2)}, u32[]{:S(2)}) collective-permute-start(f32[1,5,1,2048]{3,2,1,0:T(1,128)} %get-tuple-element.12), channel_id=1, source_target_pairs={{8,16},{16,8},{12,20},{20,12},{24,0},{0,24},{28,4},{4,28},{9,17},{... | collective-permute-start | bytes 122888 | tf_op jit(solution)/shard_map/ppermute | solution.py:221
  8.5 10.2 %collective-permute-start = (f32[1,5,3,2048]{3,2,1,0:T(4,128)}, f32[1,5,3,2048]{3,2,1,0:T(4,128)S(1)}, u32[]{:S(2)}, u32[]{:S(2)}) collective-permute-start(f32[1,5,3,2048]{3,2,1,0:T(4,128)} %get-tuple-element.9), channel_id=1, source_target_pairs={{0,4},{4,0},{8,12},{12,8},{16,20},{20,16},{24,28},{28,24},{1,5},{5... | collective-permute-start | bytes 368648 | tf_op jit(solution)/shard_map/ppermute | solution.py:221
  10.0 8.6 %collective-permute-start.1 = (f32[1,5,3,2048]{3,2,1,0:T(4,128)}, f32[1,5,3,2048]{3,2,1,0:T(4,128)S(1)}, u32[]{:S(2)}, u32[]{:S(2)}) collective-permute-start(f32[1,5,3,2048]{3,2,1,0:T(4,128)} %get-tuple-element.10), channel_id=1, source_target_pairs={{4,8},{8,4},{12,16},{16,12},{20,24},{24,20},{28,0},{0,28},{5,9},{9... | collective-permute-start | bytes 368648 | tf_op jit(solution)/shard_map/ppermute | solution.py:221

commit v11 on v9

--- a/solution.py
+++ b/solution.py
@@ -96,17 +96,47 @@
     return flux_x, flux_y
 
 
-def moments_kernel(splits, choices, index_ref, weights_ref, rho_ref, mom_ref, energy_ref, *out_refs):
-    _, flux_y = plane_fluxes(rho_ref, mom_ref, energy_ref)
+def moments_kernel(
+    splits, choices, index_ref, weights_ref, rho_hbm, mom_hbm, energy_hbm, *refs
+):
+    out_refs = refs[: len(choices)]
+    rho_v, mom_v, energy_v, in_sem = refs[len(choices) :]
+    z = pl.program_id(0)
+    plane = pl.ds(z, 1)
+    loads = [
+        pltpu.make_async_copy(mom_hbm.at[1, plane], mom_v.at[1], in_sem.at[0]),
+        pltpu.make_async_copy(rho_hbm.at[plane], rho_v, in_sem.at[1]),
+        pltpu.make_async_copy(mom_hbm.at[0, plane], mom_v.at[0], in_sem.at[2]),
+        pltpu.make_async_copy(mom_hbm.at[2, plane], mom_v.at[2], in_sem.at[3]),
+        pltpu.make_async_copy(energy_hbm.at[plane], energy_v, in_sem.at[4]),
+    ]
+    for copy in loads:
+        copy.start()
     weights = weights_ref[...]
     index = index_ref[0]
-    for f in range(5):
-        moments = dot(weights, flux_y[f])
+
+    def emit(f, fy):
+        moments = dot(weights, fy)
         for (step, phase, first, second), out_ref in zip(choices, out_refs):
             pick = (index // step) % 2 != phase
             lo, hi = splits[first]
             lo2, hi2 = splits[second]
             out_ref[0, f] = jnp.where(pick, moments[lo:hi], moments[lo2:hi2])
+
+    loads[0].wait()
+    emit(0, mom_v[1, 0])
+    loads[1].wait()
+    loads[2].wait()
+    rho = rho_v[0]
+    m_x = mom_v[0, 0]
+    m_y = mom_v[1, 0]
+    vel_y = m_y / rho
+    emit(1, m_x * vel_y)
+    loads[3].wait()
+    loads[4].wait()
+    _, flux_y = plane_fluxes(rho_v, mom_v, energy_v)
+    for f in range(2, 5):
+        emit(f, flux_y[f])
 
 
 def local_kernel(count, wx_ref, own_ref, rho_ref, mom_ref, energy_ref, out_ref):
@@ -184,9 +214,15 @@
             lambda *r: moments_kernel(split_of, choices, *r),
             grid=(planes,),
             in_specs=[pl.BlockSpec(memory_space=pltpu.SMEM), full_spec(weights.shape)]
-            + plane_specs,
+            + [pl.BlockSpec(memory_space=pl.ANY)] * 3,
             out_specs=moment_specs,
             out_shape=moment_shapes,
+            scratch_shapes=[
+                pltpu.VMEM((1, rows, count), jnp.float32),
+                pltpu.VMEM((3, 1, rows, count), jnp.float32),
+                pltpu.VMEM((1, rows, count), jnp.float32),
+                pltpu.SemaphoreType.DMA((5,)),
+            ],
         )(index.reshape(1).astype(jnp.int32), jnp.asarray(weights), density, momentum, energy)
         received = []
         spreads = []

time: 22.1 us -> 22.9 us (1.036)
  Pallas kernels: 9.66 us -> 10.3 us
    pallas_call x1, Pallas kernels: 3.01 us -> 3.69 us  [local(): pl.pallas_call(lambda *r: moments_kernel(split_of, choices, *r), grid=(pl...]
  transfers between devices with their start and end apart: 4 -> 4, of which waited for: 1 -> 1; matrix products, arithmetic and copies ran while one was open for 0% -> 0% of each run, Pallas kernels for 30% -> 29%
where the time goes in v11:
time: 22.9 us; the launch traced here: 22.7 us
  Pallas kernels  10.3 us (45%)
  starting transfers between devices  8.37 us (37%)
  matrix products  3.67 us (16%)
    ppermute x4, starting transfers between devices, local(): received.append(lax.ppermute(message, 'row', perm))  8.37 us
    pallas_call x1, Pallas kernels, local(): pl.pallas_call(lambda *r: local_kernel(count, *r), grid=(planes,), in_spe...  6.66 us
    pallas_call x1, Pallas kernels, local(): pl.pallas_call(lambda *r: moments_kernel(split_of, choices, *r), grid=(pl...  3.69 us
    dot_general x1, matrix products, local(): return partial - jnp.einsum('pr,zfrx->fzpx', spread, received, precision=HI)  3.67 us
  transfers between devices with their start and end apart: 4, of which 1 were waited for; matrix products, arithmetic and copies ran while one was open for 0% of the time, Pallas kernels for 29%

profile of v11, /device:TPU:0, one launch (start us, length us, event | category | flops | bytes accessed | tf_op | source)
XLA Modules:
  0.0 22.7 jit_solution(9835491965872207187)
XLA Ops:
  0.0 0.0 copy-start
  0.0 0.0 copy-start.1
  0.0 0.0 copy-start.2
  0.0 0.0 copy-start.3
  0.0 3.7 %shard_map.101 = (f32[1,5,3,2048]{3,2,1,0:T(4,128)}, f32[1,5,3,2048]{3,2,1,0:T(4,128)}, f32[1,5,1,2048]{3,2,1,0:T(1,128)}, f32[1,5,1,2048]{3,2,1,0:T(1,128)}) custom-call(s32[1]{0:T(128)} %bitcast.r_0_, f32[8,32]{1,0:T(8,128)} %constant.68.clone.r_1_, f32[1,32,2048]{2,1,0:T(8,128)} %r_2_.3, f32[3,1,32,2048]{3,2,1,0:T(8,128)} %r_3_.3, f32[1,32,2048]{2,1,0:T(8,128)} %r_4_.3), custom_call_target="tpu_custom_call" | custom-call | tf_op jit(solution)/shard_map/pallas_call | solution.py:213
  3.7 3.1 %collective-permute-start.2 = (f32[1,5,1,2048]{3,2,1,0:T(1,128)}, f32[1,5,1,2048]{3,2,1,0:T(1,128)S(1)}, u32[]{:S(2)}, u32[]{:S(2)}) collective-permute-start(f32[1,5,1,2048]{3,2,1,0:T(1,128)} %get-tuple-element.11), channel_id=1, source_target_pairs={{0,8},{8,0},{4,12},{12,4},{16,24},{24,16},{20,28},{28,20},{1,9},{9... | collective-permute-start | bytes 122888 | tf_op jit(solution)/shard_map/ppermute | solution.py:230
  6.8 2.5 %collective-permute-start.3 = (f32[1,5,1,2048]{3,2,1,0:T(1,128)}, f32[1,5,1,2048]{3,2,1,0:T(1,128)S(1)}, u32[]{:S(2)}, u32[]{:S(2)}) collective-permute-start(f32[1,5,1,2048]{3,2,1,0:T(1,128)} %get-tuple-element.12), channel_id=1, source_target_pairs={{8,16},{16,8},{12,20},{20,12},{24,0},{0,24},{28,4},{4,28},{9,17},{... | collective-permute-start | bytes 122888 | tf_op jit(solution)/shard_map/ppermute | solution.py:230
  9.3 1.5 %collective-permute-start = (f32[1,5,3,2048]{3,2,1,0:T(4,128)}, f32[1,5,3,2048]{3,2,1,0:T(4,128)S(1)}, u32[]{:S(2)}, u32[]{:S(2)}) collective-permute-start(f32[1,5,3,2048]{3,2,1,0:T(4,128)} %get-tuple-element.9), channel_id=1, source_target_pairs={{0,4},{4,0},{8,12},{12,8},{16,20},{20,16},{24,28},{28,24},{1,5},{5... | collective-permute-start | bytes 368648 | tf_op jit(solution)/shard_map/ppermute | solution.py:230
  10.8 1.3 %collective-permute-start.1 = (f32[1,5,3,2048]{3,2,1,0:T(4,128)}, f32[1,5,3,2048]{3,2,1,0:T(4,128)S(1)}, u32[]{:S(2)}, u32[]{:S(2)}) collective-permute-start(f32[1,5,3,2048]{3,2,1,0:T(4,128)} %get-tuple-element.10), channel_id=1, source_target_pairs={{4,8},{8,4},{12,16},{16,12},{20,24},{24,20},{28,0},{0,28},{5,9},{9... | collective-permute-start | bytes 368648 | tf_op jit(solution)/shard_map/ppermute | solution.py:230
  12.1 0.0 copy-done
  12.1 0.0 copy-done.1
  12.1 0.0 copy-done.2
  12.1 0.0 copy-done.3
  12.1 6.7 %shard_map.100 = f32[5,1,32,2048]{3,2,1,0:T(8,128)} custom-call(f32[128,384]{1,0:T(8,128)} %constant.73.clone.r_0_, f32[32,32]{1,0:T(8,128)} %constant.74.clone.r_1_, f32[1,32,2048]{2,1,0:T(8,128)} %r_2_.3, f32[3,1,32,2048]{3,2,1,0:T(8,128)} %r_3_.3, f32[1,32,2048]{2,1,0:T(8,128)} %r_4_.3), custom_call_target="tpu_custom_call" | custom-call | tf_op jit(solution)/shard_map/pallas_call | solution.py:240
  18.8 0.0 collective-permute-done.2
  18.8 0.0 collective-permute-done.3
  18.8 0.0 collective-permute-done
  18.8 0.2 collective-permute-done.1
  19.0 3.7 %fusion = f32[5,1,32,2048]{3,2,1,0:T(8,128)} fusion(f32[5,1,32,2048]{3,2,1,0:T(8,128)} %shard_map.100, f32[1,5,1,2048]{3,2,1,0:T(1,128)S(1)} %collective-permute-done.3, f32[1,5,1,2048]{3,2,1,0:T(1,128)S(1)} %collective-permute-done.2, f32[1,5,3,2048]{3,2,1,0:T(4,128)S(1)} %collective-permute-done.1, f32[1,5,3,2048]{3,2,1,0:T(4,128)S(1)} %collective-permute-done, ...), kind=kOutput, calls=%fused_computation.1 | convolution fusion | flops 32031488 | bytes 2950144 | tf_op jit(solution)/shard_map/pr,zfrx->fzpx/dot_general | solution.py:248
  (2 shorter events, 0.0 us)
Async XLA Ops:
  0.0 12.1 %copy-start = (f32[32,3]{0,1:T(4,128)S(1)}, f32[32,3]{0,1:T(4,128)}, u32[]{:S(2)}) copy-start(f32[32,3]{0,1:T(4,128)} %constant.70.clone) | copy-start | bytes 1156
  0.0 12.1 %copy-start.1 = (f32[32,3]{0,1:T(4,128)S(1)}, f32[32,3]{0,1:T(4,128)}, u32[]{:S(2)}) copy-start(f32[32,3]{0,1:T(4,128)} %constant.69.clone) | copy-start | bytes 1156
  0.0 12.1 %copy-start.2 = (f32[32,1]{0,1:T(1,128)S(1)}, f32[32,1]{0,1:T(1,128)}, u32[]{:S(2)}) copy-start(f32[32,1]{0,1:T(1,128)} %constant.72.clone) | copy-start | bytes 388
  0.0 12.1 %copy-start.3 = (f32[32,1]{0,1:T(1,128)S(1)}, f32[32,1]{0,1:T(1,128)}, u32[]{:S(2)}) copy-start(f32[32,1]{0,1:T(1,128)} %constant.71.clone) | copy-start | bytes 388
  3.7 15.1 %collective-permute-start.2 = (f32[1,5,1,2048]{3,2,1,0:T(1,128)}, f32[1,5,1,2048]{3,2,1,0:T(1,128)S(1)}, u32[]{:S(2)}, u32[]{:S(2)}) collective-permute-start(f32[1,5,1,2048]{3,2,1,0:T(1,128)} %get-tuple-element.11), channel_id=1, source_target_pairs={{0,8},{8,0},{4,12},{12,4},{16,24},{24,16},{20,28},{28,20},{1,9},{9... | collective-permute-start | bytes 122888 | tf_op jit(solution)/shard_map/ppermute | solution.py:230
  6.8 12.0 %collective-permute-start.3 = (f32[1,5,1,2048]{3,2,1,0:T(1,128)}, f32[1,5,1,2048]{3,2,1,0:T(1,128)S(1)}, u32[]{:S(2)}, u32[]{:S(2)}) collective-permute-start(f32[1,5,1,2048]{3,2,1,0:T(1,128)} %get-tuple-element.12), channel_id=1, source_target_pairs={{8,16},{16,8},{12,20},{20,12},{24,0},{0,24},{28,4},{4,28},{9,17},{... | collective-permute-start | bytes 122888 | tf_op jit(solution)/shard_map/ppermute | solution.py:230
  9.3 9.5 %collective-permute-start = (f32[1,5,3,2048]{3,2,1,0:T(4,128)}, f32[1,5,3,2048]{3,2,1,0:T(4,128)S(1)}, u32[]{:S(2)}, u32[]{:S(2)}) collective-permute-start(f32[1,5,3,2048]{3,2,1,0:T(4,128)} %get-tuple-element.9), channel_id=1, source_target_pairs={{0,4},{4,0},{8,12},{12,8},{16,20},{20,16},{24,28},{28,24},{1,5},{5... | collective-permute-start | bytes 368648 | tf_op jit(solution)/shard_map/ppermute | solution.py:230
  10.8 8.2 %collective-permute-start.1 = (f32[1,5,3,2048]{3,2,1,0:T(4,128)}, f32[1,5,3,2048]{3,2,1,0:T(4,128)S(1)}, u32[]{:S(2)}, u32[]{:S(2)}) collective-permute-start(f32[1,5,3,2048]{3,2,1,0:T(4,128)} %get-tuple-element.10), channel_id=1, source_target_pairs={{4,8},{8,4},{12,16},{16,12},{20,24},{24,20},{28,0},{0,28},{5,9},{9... | collective-permute-start | bytes 368648 | tf_op jit(solution)/shard_map/ppermute | solution.py:230

commit v12 on v7

--- a/solution.py
+++ b/solution.py
@@ -109,17 +109,16 @@
             out_ref[0, f] = jnp.where(pick, moments[lo:hi], moments[lo2:hi2])
 
 
-def local_kernel(count, wx_ref, own_ref, rho_ref, mom_ref, energy_ref, out_ref):
-    flux_x, flux_y = plane_fluxes(rho_ref, mom_ref, energy_ref)
-    wx = wx_ref[...]
-    own = own_ref[...]
+def field_tendency(count, wx, own, flux_x, flux_y, fields):
     nb = count // WIDTH
-    for f in range(5):
-        d_y = dot(own, flux_y[f])
+    d_all = dot(own, jnp.concatenate([flux_y[f] for f in fields], axis=1))
+    results = []
+    for i, f in enumerate(fields):
         fx = flux_x[f]
         rows = fx.shape[0]
         stacked = jnp.concatenate([fx[:, b * WIDTH : (b + 1) * WIDTH] for b in range(nb)], axis=0)
         parts = dot(stacked, wx)
+        pieces = []
         for b in range(nb):
             bp = (b - 1) % nb
             bn = (b + 1) % nb
@@ -128,7 +127,36 @@
                 + parts[b * rows : (b + 1) * rows, WIDTH : 2 * WIDTH]
                 + parts[bn * rows : (bn + 1) * rows, 2 * WIDTH :]
             )
-            out_ref[f, 0, :, b * WIDTH : (b + 1) * WIDTH] = -(d_x + d_y[:, b * WIDTH : (b + 1) * WIDTH])
+            lo = i * count + b * WIDTH
+            pieces.append(-(d_x + d_all[:, lo : lo + WIDTH]))
+        results.append(pieces)
+    return results
+
+
+def local_kernel(count, fields, wx_ref, own_ref, rho_ref, mom_ref, energy_ref, out_ref):
+    flux_x, flux_y = plane_fluxes(rho_ref, mom_ref, energy_ref)
+    results = field_tendency(count, wx_ref[...], own_ref[...], flux_x, flux_y, fields)
+    for i, pieces in enumerate(results):
+        for b, piece in enumerate(pieces):
+            out_ref[i, 0, :, b * WIDTH : (b + 1) * WIDTH] = piece
+
+
+def final_kernel(count, early, late, wx_ref, own_ref, spread_ref, rho_ref, mom_ref, energy_ref, partial_ref, *refs):
+    recv_refs, out_ref = refs[:-1], refs[-1]
+    spread = spread_ref[...]
+
+    def correction(f):
+        received = jnp.concatenate([r[0, f] for r in recv_refs], axis=0)
+        return dot(spread, received)
+
+    for i, f in enumerate(early):
+        out_ref[f, 0] = partial_ref[i, 0] - correction(f)
+    flux_x, flux_y = plane_fluxes(rho_ref, mom_ref, energy_ref)
+    results = field_tendency(count, wx_ref[...], own_ref[...], flux_x, flux_y, late)
+    for f, pieces in zip(late, results):
+        corr = correction(f)
+        for b, piece in enumerate(pieces):
+            out_ref[f, 0, :, b * WIDTH : (b + 1) * WIDTH] = piece - corr[:, b * WIDTH : (b + 1) * WIDTH]
 
 
 def exchange_plan(groups, shift_list):
@@ -200,17 +228,24 @@
         wx = block_weights(count)
         out_spec = pl.BlockSpec((5, 1, rows, count), lambda z: (0, z, 0, 0))
         out_shape = jax.ShapeDtypeStruct((5, planes, rows, count), jnp.float32)
+        early, late = (0, 1, 2), (3, 4)
         partial = pl.pallas_call(
-            lambda *r: local_kernel(count, *r),
+            lambda *r: local_kernel(count, early, *r),
             grid=(planes,),
             in_specs=[full_spec(wx.shape), full_spec(own.shape)] + plane_specs,
+            out_specs=pl.BlockSpec((len(early), 1, rows, count), lambda z: (0, z, 0, 0)),
+            out_shape=jax.ShapeDtypeStruct((len(early), planes, rows, count), jnp.float32),
+        )(wx, jnp.asarray(own), density, momentum, energy)
+        return pl.pallas_call(
+            lambda *r: final_kernel(count, early, late, *r),
+            grid=(planes,),
+            in_specs=[full_spec(wx.shape), full_spec(own.shape), full_spec(spread.shape)]
+            + plane_specs
+            + [pl.BlockSpec((len(early), 1, rows, count), lambda z: (0, z, 0, 0))]
+            + [pl.BlockSpec((1,) + r.shape[1:], lambda z: (z, 0, 0, 0)) for r in received],
             out_specs=out_spec,
             out_shape=out_shape,
-        )(wx, jnp.asarray(own), density, momentum, energy)
-        received = jnp.concatenate(received, axis=2)
-        return partial - jnp.einsum(
-            "pr,zfrx->fzpx", spread, received, precision=HI
-        )
+        )(wx, jnp.asarray(own), spread, density, momentum, energy, partial, *received)
 
     return local
 

time: 22.1 us -> 24.7 us (1.12)
  Pallas kernels: 9.7 us -> 13.5 us
  matrix products: 3.66 us -> 0 us
  local copies, waits for them, and re-layouts: 0.01 us -> 1.36 us
  waiting for transfers between devices: 0.18 us -> 1.27 us
    pallas_call x1 -> x2, Pallas kernels: 6.7 us -> 10.5 us  [the longest x1 5.58 us: local(): pl.pallas_call(lambda *r: final_kernel(count, early, late, *r), grid=(pla...]
    dot_general x1 -> x0, matrix products: 3.66 us -> none  [local(): return partial - jnp.einsum('pr,zfrx->fzpx', spread, received, precision=HI)]
    ppermute x4, waiting for transfers between devices: 0.18 us -> 1.27 us  [local(): received.append(lax.ppermute(message, 'row', perm))]
    concatenate x0 -> x1, local copies, waits for them, and re-layouts: none -> 0.67 us  [local(): spread = jnp.concatenate(spreads, axis=1)]
    unnamed x8 -> x16, local copies, waits for them, and re-layouts: 0.01 us -> 0.69 us
  transfers between devices with their start and end apart: 4 -> 4, of which waited for: 1 -> 1; matrix products, arithmetic and copies ran while one was open for 0% -> 3% of each run, Pallas kernels for 31% -> 20%
where the time goes in v12:
time: 24.7 us; the launch traced here: 24.5 us
  Pallas kernels  13.5 us (55%)
  starting transfers between devices  8.31 us (34%)
  local copies, waits for them, and re-layouts  1.36 us (6%)
  waiting for transfers between devices  1.27 us (5%)
    ppermute x4, starting transfers between devices, local(): received.append(lax.ppermute(message, 'row', perm))  8.31 us
    pallas_call x1, Pallas kernels, local(): pl.pallas_call(lambda *r: final_kernel(count, early, late, *r), grid=(pla...  5.58 us
    pallas_call x1, Pallas kernels, local(): pl.pallas_call(lambda *r: local_kernel(count, early, *r), grid=(planes,),...  4.89 us
    pallas_call x1, Pallas kernels, local(): pl.pallas_call(lambda *r: moments_kernel(split_of, choices, *r), grid=(pl...  2.99 us
    ppermute x4, waiting for transfers between devices, local(): received.append(lax.ppermute(message, 'row', perm))  1.27 us
    unnamed x16, local copies, waits for them, and re-layouts  0.69 us
    concatenate x1, local copies, waits for them, and re-layouts, local(): spread = jnp.concatenate(spreads, axis=1)  0.67 us
  transfers between devices with their start and end apart: 4, of which 1 were waited for; matrix products, arithmetic and copies ran while one was open for 3% of the time, Pallas kernels for 20%

profile of v12, /device:TPU:0, one launch (start us, length us, event | category | flops | bytes accessed | tf_op | source)
XLA Modules:
  0.0 24.5 jit_solution(4240845292166060091)
XLA Ops:
  0.0 0.0 copy-start.4
  0.0 0.0 copy-start.5
  0.0 0.0 copy-start.6
  0.0 0.0 copy-start.7
  0.0 3.0 %shard_map.101 = (f32[1,5,3,2048]{3,2,1,0:T(4,128)}, f32[1,5,3,2048]{3,2,1,0:T(4,128)}, f32[1,5,1,2048]{3,2,1,0:T(1,128)}, f32[1,5,1,2048]{3,2,1,0:T(1,128)}) custom-call(s32[1]{0:T(128)} %bitcast.r_0_, f32[8,32]{1,0:T(8,128)} %constant.68.clone.r_1_, f32[1,32,2048]{2,1,0:T(8,128)} %r_3_.5, f32[3,1,32,2048]{3,2,1,0:T(8,128)} %r_4_.5, f32[1,32,2048]{2,1,0:T(8,128)} %r_5_.1), custom_call_target="tpu_custom_call" | custom-call | tf_op jit(solution)/shard_map/pallas_call | solution.py:210
  3.0 3.0 %collective-permute-start.2 = (f32[1,5,1,2048]{3,2,1,0:T(1,128)}, f32[1,5,1,2048]{3,2,1,0:T(1,128)S(1)}, u32[]{:S(2)}, u32[]{:S(2)}) collective-permute-start(f32[1,5,1,2048]{3,2,1,0:T(1,128)} %get-tuple-element.11), channel_id=1, source_target_pairs={{0,8},{8,0},{4,12},{12,4},{16,24},{24,16},{20,28},{28,20},{1,9},{9... | collective-permute-start | bytes 122888 | tf_op jit(solution)/shard_map/ppermute | solution.py:221
  6.0 2.5 %collective-permute-start.3 = (f32[1,5,1,2048]{3,2,1,0:T(1,128)}, f32[1,5,1,2048]{3,2,1,0:T(1,128)S(1)}, u32[]{:S(2)}, u32[]{:S(2)}) collective-permute-start(f32[1,5,1,2048]{3,2,1,0:T(1,128)} %get-tuple-element.12), channel_id=1, source_target_pairs={{8,16},{16,8},{12,20},{20,12},{24,0},{0,24},{28,4},{4,28},{9,17},{... | collective-permute-start | bytes 122888 | tf_op jit(solution)/shard_map/ppermute | solution.py:221
  8.5 1.5 %collective-permute-start = (f32[1,5,3,2048]{3,2,1,0:T(4,128)}, f32[1,5,3,2048]{3,2,1,0:T(4,128)S(1)}, u32[]{:S(2)}, u32[]{:S(2)}) collective-permute-start(f32[1,5,3,2048]{3,2,1,0:T(4,128)} %get-tuple-element.9), channel_id=1, source_target_pairs={{0,4},{4,0},{8,12},{12,8},{16,20},{20,16},{24,28},{28,24},{1,5},{5... | collective-permute-start | bytes 368648 | tf_op jit(solution)/shard_map/ppermute | solution.py:221
  10.0 1.3 %collective-permute-start.1 = (f32[1,5,3,2048]{3,2,1,0:T(4,128)}, f32[1,5,3,2048]{3,2,1,0:T(4,128)S(1)}, u32[]{:S(2)}, u32[]{:S(2)}) collective-permute-start(f32[1,5,3,2048]{3,2,1,0:T(4,128)} %get-tuple-element.10), channel_id=1, source_target_pairs={{4,8},{8,4},{12,16},{16,12},{20,24},{24,20},{28,0},{0,28},{5,9},{9... | collective-permute-start | bytes 368648 | tf_op jit(solution)/shard_map/ppermute | solution.py:221
  11.3 0.0 copy-done.4
  11.3 0.0 copy-done.5
  11.3 0.0 copy-done.6
  11.3 0.0 copy-done.7
  11.4 0.7 %copy.11.r_2_ = f32[32,8]{1,0:T(8,128)} copy(f32[32,8]{0,1:T(8,128)S(1)} %pad_maximum_fusion) | data formatting | bytes 2048 | tf_op jit(solution)/shard_map/concatenate | solution.py:227
  12.0 4.9 %shard_map.100.r_6_ = f32[3,1,32,2048]{3,2,1,0:T(8,128)} custom-call(f32[128,384]{1,0:T(8,128)} %constant.73.clone.r_0_, f32[32,32]{1,0:T(8,128)} %constant.74.clone.r_1_, f32[1,32,2048]{2,1,0:T(8,128)} %r_3_.5, f32[3,1,32,2048]{3,2,1,0:T(8,128)} %r_4_.5, f32[1,32,2048]{2,1,0:T(8,128)} %r_5_.1), custom_call_target="tpu_custom_call" | custom-call | tf_op jit(solution)/shard_map/pallas_call | solution.py:232
  16.9 0.0 collective-permute-done.2.r_9_
  16.9 0.0 copy-start.2
  16.9 0.0 collective-permute-done.3.r_10_
  16.9 0.0 copy-start.3
  17.0 0.0 collective-permute-done.r_7_
  17.0 0.0 copy-start
  17.0 1.3 %collective-permute-done.1.r_8_ = f32[1,5,3,2048]{3,2,1,0:T(4,128)S(1)} collective-permute-done((f32[1,5,3,2048]{3,2,1,0:T(4,128)}, f32[1,5,3,2048]{3,2,1,0:T(4,128)S(1)}, u32[]{:S(2)}, u32[]{:S(2)}) %collective-permute-start.1) | collective-permute-done | bytes 122912 | tf_op jit(solution)/shard_map/ppermute | solution.py:221
  18.2 0.0 copy-done.2
  18.2 0.0 copy-done.3
  18.2 0.0 copy-done
  18.3 0.0 copy-start.1
  18.3 0.7 %copy-done.1 = f32[1,5,3,2048]{3,2,1,0:T(4,128)} copy-done((f32[1,5,3,2048]{3,2,1,0:T(4,128)}, f32[1,5,3,2048]{3,2,1,0:T(4,128)S(1)}, u32[]{:S(2)}) %copy-start.1) | copy-done | bytes 122904
  18.9 5.6 %shard_map.102 = f32[5,1,32,2048]{3,2,1,0:T(8,128)} custom-call(f32[128,384]{1,0:T(8,128)} %constant.73.clone.r_0_, f32[32,32]{1,0:T(8,128)} %constant.74.clone.r_1_, f32[32,8]{1,0:T(8,128)} %copy.11.r_2_, f32[1,32,2048]{2,1,0:T(8,128)} %r_3_.5, f32[3,1,32,2048]{3,2,1,0:T(8,128)} %r_4_.5, f32[1,32,2048]{2,1,0:T(8,128)} %r_5_.1, ...), custom_call_target="tpu_custom_call" | custom-call | tf_op jit(solution)/shard_map/pallas_call | solution.py:239
  (3 shorter events, 0.0 us)
Async XLA Ops:
  0.0 11.3 %copy-start.4 = (f32[32,3]{0,1:T(4,128)S(1)}, f32[32,3]{0,1:T(4,128)}, u32[]{:S(2)}) copy-start(f32[32,3]{0,1:T(4,128)} %constant.70.clone) | copy-start | bytes 1156
  0.0 11.3 %copy-start.5 = (f32[32,3]{0,1:T(4,128)S(1)}, f32[32,3]{0,1:T(4,128)}, u32[]{:S(2)}) copy-start(f32[32,3]{0,1:T(4,128)} %constant.69.clone) | copy-start | bytes 1156
  0.0 11.3 %copy-start.6 = (f32[32,1]{0,1:T(1,128)S(1)}, f32[32,1]{0,1:T(1,128)}, u32[]{:S(2)}) copy-start(f32[32,1]{0,1:T(1,128)} %constant.72.clone) | copy-start | bytes 388
  0.0 11.3 %copy-start.7 = (f32[32,1]{0,1:T(1,128)S(1)}, f32[32,1]{0,1:T(1,128)}, u32[]{:S(2)}) copy-start(f32[32,1]{0,1:T(1,128)} %constant.71.clone) | copy-start | bytes 388
  3.0 13.9 %collective-permute-start.2 = (f32[1,5,1,2048]{3,2,1,0:T(1,128)}, f32[1,5,1,2048]{3,2,1,0:T(1,128)S(1)}, u32[]{:S(2)}, u32[]{:S(2)}) collective-permute-start(f32[1,5,1,2048]{3,2,1,0:T(1,128)} %get-tuple-element.11), channel_id=1, source_target_pairs={{0,8},{8,0},{4,12},{12,4},{16,24},{24,16},{20,28},{28,20},{1,9},{9... | collective-permute-start | bytes 122888 | tf_op jit(solution)/shard_map/ppermute | solution.py:221
  6.0 10.9 %collective-permute-start.3 = (f32[1,5,1,2048]{3,2,1,0:T(1,128)}, f32[1,5,1,2048]{3,2,1,0:T(1,128)S(1)}, u32[]{:S(2)}, u32[]{:S(2)}) collective-permute-start(f32[1,5,1,2048]{3,2,1,0:T(1,128)} %get-tuple-element.12), channel_id=1, source_target_pairs={{8,16},{16,8},{12,20},{20,12},{24,0},{0,24},{28,4},{4,28},{9,17},{... | collective-permute-start | bytes 122888 | tf_op jit(solution)/shard_map/ppermute | solution.py:221
  8.5 8.5 %collective-permute-start = (f32[1,5,3,2048]{3,2,1,0:T(4,128)}, f32[1,5,3,2048]{3,2,1,0:T(4,128)S(1)}, u32[]{:S(2)}, u32[]{:S(2)}) collective-permute-start(f32[1,5,3,2048]{3,2,1,0:T(4,128)} %get-tuple-element.9), channel_id=1, source_target_pairs={{0,4},{4,0},{8,12},{12,8},{16,20},{20,16},{24,28},{28,24},{1,5},{5... | collective-permute-start | bytes 368648 | tf_op jit(solution)/shard_map/ppermute | solution.py:221
  10.0 8.2 %collective-permute-start.1 = (f32[1,5,3,2048]{3,2,1,0:T(4,128)}, f32[1,5,3,2048]{3,2,1,0:T(4,128)S(1)}, u32[]{:S(2)}, u32[]{:S(2)}) collective-permute-start(f32[1,5,3,2048]{3,2,1,0:T(4,128)} %get-tuple-element.10), channel_id=1, source_target_pairs={{4,8},{8,4},{12,16},{16,12},{20,24},{24,20},{28,0},{0,28},{5,9},{9... | collective-permute-start | bytes 368648 | tf_op jit(solution)/shard_map/ppermute | solution.py:221
  16.9 1.3 %copy-start.2 = (f32[1,5,1,2048]{3,2,1,0:T(1,128)}, f32[1,5,1,2048]{3,2,1,0:T(1,128)S(1)}, u32[]{:S(2)}) copy-start(f32[1,5,1,2048]{3,2,1,0:T(1,128)S(1)} %collective-permute-done.2.r_9_) | copy-start | bytes 122884
  16.9 1.3 %copy-start.3 = (f32[1,5,1,2048]{3,2,1,0:T(1,128)}, f32[1,5,1,2048]{3,2,1,0:T(1,128)S(1)}, u32[]{:S(2)}) copy-start(f32[1,5,1,2048]{3,2,1,0:T(1,128)S(1)} %collective-permute-done.3.r_10_) | copy-start | bytes 122884
  17.0 1.3 %copy-start = (f32[1,5,3,2048]{3,2,1,0:T(4,128)}, f32[1,5,3,2048]{3,2,1,0:T(4,128)S(1)}, u32[]{:S(2)}) copy-start(f32[1,5,3,2048]{3,2,1,0:T(4,128)S(1)} %collective-permute-done.r_7_) | copy-start | bytes 368644
  18.3 0.7 %copy-start.1 = (f32[1,5,3,2048]{3,2,1,0:T(4,128)}, f32[1,5,3,2048]{3,2,1,0:T(4,128)S(1)}, u32[]{:S(2)}) copy-start(f32[1,5,3,2048]{3,2,1,0:T(4,128)S(1)} %collective-permute-done.1.r_8_) | copy-start | bytes 368644

commit v13 on v7

--- a/solution.py
+++ b/solution.py
@@ -109,13 +109,18 @@
             out_ref[0, f] = jnp.where(pick, moments[lo:hi], moments[lo2:hi2])
 
 
-def local_kernel(count, wx_ref, own_ref, rho_ref, mom_ref, energy_ref, out_ref):
-    flux_x, flux_y = plane_fluxes(rho_ref, mom_ref, energy_ref)
+def y_kernel(count, own_ref, rho_ref, mom_ref, energy_ref, out_ref):
+    _, flux_y = plane_fluxes(rho_ref, mom_ref, energy_ref)
+    d_all = dot(own_ref[...], jnp.concatenate(flux_y, axis=1))
+    for f in range(5):
+        out_ref[f, 0] = -d_all[:, f * count : (f + 1) * count]
+
+
+def x_kernel(count, wx_ref, rho_ref, mom_ref, energy_ref, out_ref):
+    flux_x, _ = plane_fluxes(rho_ref, mom_ref, energy_ref)
     wx = wx_ref[...]
-    own = own_ref[...]
     nb = count // WIDTH
     for f in range(5):
-        d_y = dot(own, flux_y[f])
         fx = flux_x[f]
         rows = fx.shape[0]
         stacked = jnp.concatenate([fx[:, b * WIDTH : (b + 1) * WIDTH] for b in range(nb)], axis=0)
@@ -128,7 +133,7 @@
                 + parts[b * rows : (b + 1) * rows, WIDTH : 2 * WIDTH]
                 + parts[bn * rows : (bn + 1) * rows, 2 * WIDTH :]
             )
-            out_ref[f, 0, :, b * WIDTH : (b + 1) * WIDTH] = -(d_x + d_y[:, b * WIDTH : (b + 1) * WIDTH])
+            out_ref[f, 0, :, b * WIDTH : (b + 1) * WIDTH] = -d_x
 
 
 def exchange_plan(groups, shift_list):
@@ -179,14 +184,29 @@
             pl.BlockSpec((1,) + s.shape[1:], lambda z: (z, 0, 0, 0)) for s in moment_shapes
         ]
         split_of = {e: by_shift[e][1] for e in by_shift}
-        messages = pl.pallas_call(
+        messages = list(pl.pallas_call(
             lambda *r: moments_kernel(split_of, choices, *r),
             grid=(planes,),
             in_specs=[pl.BlockSpec(memory_space=pltpu.SMEM), full_spec(weights.shape)]
             + plane_specs,
             out_specs=moment_specs,
             out_shape=moment_shapes,
-        )(index.reshape(1).astype(jnp.int32), jnp.asarray(weights), density, momentum, energy)
+        )(index.reshape(1).astype(jnp.int32), jnp.asarray(weights), density, momentum, energy))
+        wx = block_weights(count)
+        out_spec = pl.BlockSpec((5, 1, rows, count), lambda z: (0, z, 0, 0))
+        out_shape = jax.ShapeDtypeStruct((5, planes, rows, count), jnp.float32)
+        part_y = pl.pallas_call(
+            lambda *r: y_kernel(count, *r),
+            grid=(planes,),
+            in_specs=[full_spec(own.shape)] + plane_specs,
+            out_specs=out_spec,
+            out_shape=out_shape,
+        )(jnp.asarray(own), density, momentum, energy)
+        late = [k for k, (step, phase, _, _, _) in enumerate(plan) if phase == 1]
+        held = lax.optimization_barrier(([messages[k] for k in late], part_y, density))
+        for k, message in zip(late, held[0]):
+            messages[k] = message
+        part_y, density_late = held[1], held[2]
         received = []
         spreads = []
         for (step, phase, first, second, perm), message in zip(plan, messages):
@@ -197,18 +217,15 @@
                 + (1.0 - take) * jnp.asarray(by_shift[second][0])
             )
         spread = jnp.concatenate(spreads, axis=1)
-        wx = block_weights(count)
-        out_spec = pl.BlockSpec((5, 1, rows, count), lambda z: (0, z, 0, 0))
-        out_shape = jax.ShapeDtypeStruct((5, planes, rows, count), jnp.float32)
-        partial = pl.pallas_call(
-            lambda *r: local_kernel(count, *r),
+        part_x = pl.pallas_call(
+            lambda *r: x_kernel(count, *r),
             grid=(planes,),
-            in_specs=[full_spec(wx.shape), full_spec(own.shape)] + plane_specs,
+            in_specs=[full_spec(wx.shape)] + plane_specs,
             out_specs=out_spec,
             out_shape=out_shape,
-        )(wx, jnp.asarray(own), density, momentum, energy)
+        )(wx, density_late, momentum, energy)
         received = jnp.concatenate(received, axis=2)
-        return partial - jnp.einsum(
+        return part_x + part_y - jnp.einsum(
             "pr,zfrx->fzpx", spread, received, precision=HI
         )
 

time: 22.1 us -> 25.5 us (1.15)
  Pallas kernels: 9.7 us -> 12.3 us
  waiting for transfers between devices: 0.18 us -> 0.86 us
    pallas_call x1 -> x2, Pallas kernels: 6.7 us -> 9.33 us  [the longest x1 5.8 us: local(): pl.pallas_call(lambda *r: x_kernel(count, *r), grid=(planes,), in_specs=[...]
    ppermute x4, waiting for transfers between devices: 0.18 us -> 0.86 us  [local(): received.append(lax.ppermute(message, 'row', perm))]
  transfers between devices with their start and end apart: 4 -> 4, of which waited for: 1 -> 1; matrix products, arithmetic and copies ran while one was open for 0% -> 0% of each run, Pallas kernels for 31% -> 37%
where the time goes in v13:
time: 25.5 us; the launch traced here: 25.3 us
  Pallas kernels  12.3 us (48%)
  starting transfers between devices  8.37 us (33%)
  matrix products  3.72 us (15%)
  waiting for transfers between devices  0.86 us (3%)
    ppermute x4, starting transfers between devices, local(): received.append(lax.ppermute(message, 'row', perm))  8.37 us
    pallas_call x1, Pallas kernels, local(): pl.pallas_call(lambda *r: x_kernel(count, *r), grid=(planes,), in_specs=[...  5.8 us
    dot_general x1, matrix products, local(): jnp.einsum('pr,zfrx->fzpx', spread, received, precision=HI)  3.72 us
    pallas_call x1, Pallas kernels, local(): pl.pallas_call(lambda *r: y_kernel(count, *r), grid=(planes,), in_specs=[...  3.53 us
    pallas_call x1, Pallas kernels, local(): pl.pallas_call(lambda *r: moments_kernel(split_of, choices, *r), grid=(pl...  2.94 us
    ppermute x4, waiting for transfers between devices, local(): received.append(lax.ppermute(message, 'row', perm))  0.86 us
  transfers between devices with their start and end apart: 4, of which 1 were waited for; matrix products, arithmetic and copies ran while one was open for 0% of the time, Pallas kernels for 37%

profile of v13, /device:TPU:0, one launch (start us, length us, event | category | flops | bytes accessed | tf_op | source)
XLA Modules:
  0.0 25.3 jit_solution(8405503727699857432)
XLA Ops:
  0.0 2.9 %shard_map.100 = (f32[1,5,3,2048]{3,2,1,0:T(4,128)}, f32[1,5,3,2048]{3,2,1,0:T(4,128)}, f32[1,5,1,2048]{3,2,1,0:T(1,128)}, f32[1,5,1,2048]{3,2,1,0:T(1,128)}) custom-call(s32[1]{0:T(128)} %bitcast.r_0_, f32[8,32]{1,0:T(8,128)} %constant.68.clone.r_1_, f32[1,32,2048]{2,1,0:T(8,128)} %r_1_.3, f32[3,1,32,2048]{3,2,1,0:T(8,128)} %r_2_.5, f32[1,32,2048]{2,1,0:T(8,128)} %r_3_.5), custom_call_target="tpu_custom_call" | custom-call | tf_op jit(solution)/shard_map/pallas_call | solution.py:187
  2.9 3.0 %collective-permute-start.2 = (f32[1,5,1,2048]{3,2,1,0:T(1,128)}, f32[1,5,1,2048]{3,2,1,0:T(1,128)S(1)}, u32[]{:S(2)}, u32[]{:S(2)}) collective-permute-start(f32[1,5,1,2048]{3,2,1,0:T(1,128)} %get-tuple-element.19), channel_id=1, source_target_pairs={{0,8},{8,0},{4,12},{12,4},{16,24},{24,16},{20,28},{28,20},{1,9},{9... | collective-permute-start | bytes 122888 | tf_op jit(solution)/shard_map/ppermute | solution.py:213
  6.0 0.0 copy-start.6
  6.0 0.0 copy-start.5
  6.0 0.0 copy-start.1
  6.0 0.0 copy-start.2
  6.0 0.0 copy-start.3
  6.0 0.0 copy-start.4
  6.0 1.6 %collective-permute-start = (f32[1,5,3,2048]{3,2,1,0:T(4,128)}, f32[1,5,3,2048]{3,2,1,0:T(4,128)S(1)}, u32[]{:S(2)}, u32[]{:S(2)}) collective-permute-start(f32[1,5,3,2048]{3,2,1,0:T(4,128)} %get-tuple-element.17), channel_id=1, source_target_pairs={{0,4},{4,0},{8,12},{12,8},{16,20},{20,16},{24,28},{28,24},{1,5},{5... | collective-permute-start | bytes 368648 | tf_op jit(solution)/shard_map/ppermute | solution.py:213
  7.6 3.5 %shard_map.101 = f32[5,1,32,2048]{3,2,1,0:T(8,128)} custom-call(f32[32,32]{1,0:T(8,128)} %constant.70.clone.r_0_, f32[1,32,2048]{2,1,0:T(8,128)} %r_1_.3, f32[3,1,32,2048]{3,2,1,0:T(8,128)} %r_2_.5, f32[1,32,2048]{2,1,0:T(8,128)} %r_3_.5), custom_call_target="tpu_custom_call" | custom-call | tf_op jit(solution)/shard_map/pallas_call | solution.py:198
  11.1 0.0 copy-done.6
  11.1 2.5 %collective-permute-start.3 = (f32[1,5,1,2048]{3,2,1,0:T(1,128)S(1)}, f32[1,5,1,2048]{3,2,1,0:T(1,128)S(1)}, u32[]{:S(2)}, u32[]{:S(2)}) collective-permute-start(f32[1,5,1,2048]{3,2,1,0:T(1,128)S(1)} %copy-done.6), channel_id=1, source_target_pairs={{8,16},{16,8},{12,20},{20,12},{24,0},{0,24},{28,4},{4,28},{9,17},{... | collective-permute-start | bytes 122888 | tf_op jit(solution)/shard_map/ppermute | solution.py:213
  13.6 0.0 copy-done.5
  13.6 1.3 %collective-permute-start.1 = (f32[1,5,3,2048]{3,2,1,0:T(4,128)S(1)}, f32[1,5,3,2048]{3,2,1,0:T(4,128)S(1)}, u32[]{:S(2)}, u32[]{:S(2)}) collective-permute-start(f32[1,5,3,2048]{3,2,1,0:T(4,128)S(1)} %copy-done.5), channel_id=1, source_target_pairs={{4,8},{8,4},{12,16},{16,12},{20,24},{24,20},{28,0},{0,28},{5,9},{9... | collective-permute-start | bytes 368648 | tf_op jit(solution)/shard_map/ppermute | solution.py:213
  14.9 0.0 copy-done.1
  14.9 0.0 copy-done.2
  14.9 0.0 copy-done.3
  14.9 0.0 copy-done.4
  14.9 0.0 copy-start
  14.9 5.8 %shard_map.102 = f32[5,1,32,2048]{3,2,1,0:T(8,128)} custom-call(f32[128,384]{1,0:T(8,128)} %constant.69.clone.r_0_, f32[1,32,2048]{2,1,0:T(8,128)} %r_1_.3, f32[3,1,32,2048]{3,2,1,0:T(8,128)} %r_2_.5, f32[1,32,2048]{2,1,0:T(8,128)} %r_3_.5), custom_call_target="tpu_custom_call" | custom-call | tf_op jit(solution)/shard_map/pallas_call | solution.py:220
  20.7 0.0 collective-permute-done.2
  20.7 0.0 collective-permute-done.3
  20.8 0.0 collective-permute-done
  20.8 0.8 %collective-permute-done.1 = f32[1,5,3,2048]{3,2,1,0:T(4,128)S(1)} collective-permute-done((f32[1,5,3,2048]{3,2,1,0:T(4,128)S(1)}, f32[1,5,3,2048]{3,2,1,0:T(4,128)S(1)}, u32[]{:S(2)}, u32[]{:S(2)}) %collective-permute-start.1) | collective-permute-done | bytes 122912 | tf_op jit(solution)/shard_map/ppermute | solution.py:213
  21.6 0.0 copy-done
  21.6 3.7 %fusion = f32[5,1,32,2048]{3,2,1,0:T(8,128)} fusion(f32[5,1,32,2048]{3,2,1,0:T(8,128)} %shard_map.102, f32[5,1,32,2048]{3,2,1,0:T(8,128)S(1)} %copy-done, f32[1,5,1,2048]{3,2,1,0:T(1,128)S(1)} %collective-permute-done.3, f32[1,5,1,2048]{3,2,1,0:T(1,128)S(1)} %collective-permute-done.2, f32[1,5,3,2048]{3,2,1,0:T(4,128)S(1)} %collective-permute-done.1, ...), kind=kOutput, calls=%fused_computation.1 | convolution fusion | flops 32359168 | bytes 4260864 | tf_op jit(solution)/shard_map/pr,zfrx->fzpx/dot_general | solution.py:228
  (2 shorter events, 0.0 us)
Async XLA Ops:
  2.9 17.8 %collective-permute-start.2 = (f32[1,5,1,2048]{3,2,1,0:T(1,128)}, f32[1,5,1,2048]{3,2,1,0:T(1,128)S(1)}, u32[]{:S(2)}, u32[]{:S(2)}) collective-permute-start(f32[1,5,1,2048]{3,2,1,0:T(1,128)} %get-tuple-element.19), channel_id=1, source_target_pairs={{0,8},{8,0},{4,12},{12,4},{16,24},{24,16},{20,28},{28,20},{1,9},{9... | collective-permute-start | bytes 122888 | tf_op jit(solution)/shard_map/ppermute | solution.py:213
  6.0 5.2 %copy-start.6 = (f32[1,5,1,2048]{3,2,1,0:T(1,128)S(1)}, f32[1,5,1,2048]{3,2,1,0:T(1,128)}, u32[]{:S(2)}) copy-start(f32[1,5,1,2048]{3,2,1,0:T(1,128)} %get-tuple-element.20) | copy-start | bytes 122884
  6.0 7.6 %copy-start.5 = (f32[1,5,3,2048]{3,2,1,0:T(4,128)S(1)}, f32[1,5,3,2048]{3,2,1,0:T(4,128)}, u32[]{:S(2)}) copy-start(f32[1,5,3,2048]{3,2,1,0:T(4,128)} %get-tuple-element.18) | copy-start | bytes 368644
  6.0 8.9 %copy-start.1 = (f32[32,3]{0,1:T(4,128)S(1)}, f32[32,3]{0,1:T(4,128)}, u32[]{:S(2)}) copy-start(f32[32,3]{0,1:T(4,128)} %constant.72.clone) | copy-start | bytes 1156
  6.0 8.9 %copy-start.2 = (f32[32,3]{0,1:T(4,128)S(1)}, f32[32,3]{0,1:T(4,128)}, u32[]{:S(2)}) copy-start(f32[32,3]{0,1:T(4,128)} %constant.71.clone) | copy-start | bytes 1156
  6.0 8.9 %copy-start.3 = (f32[32,1]{0,1:T(1,128)S(1)}, f32[32,1]{0,1:T(1,128)}, u32[]{:S(2)}) copy-start(f32[32,1]{0,1:T(1,128)} %constant.74.clone) | copy-start | bytes 388
  6.0 8.9 %copy-start.4 = (f32[32,1]{0,1:T(1,128)S(1)}, f32[32,1]{0,1:T(1,128)}, u32[]{:S(2)}) copy-start(f32[32,1]{0,1:T(1,128)} %constant.73.clone) | copy-start | bytes 388
  6.0 14.8 %collective-permute-start = (f32[1,5,3,2048]{3,2,1,0:T(4,128)}, f32[1,5,3,2048]{3,2,1,0:T(4,128)S(1)}, u32[]{:S(2)}, u32[]{:S(2)}) collective-permute-start(f32[1,5,3,2048]{3,2,1,0:T(4,128)} %get-tuple-element.17), channel_id=1, source_target_pairs={{0,4},{4,0},{8,12},{12,8},{16,20},{20,16},{24,28},{28,24},{1,5},{5... | collective-permute-start | bytes 368648 | tf_op jit(solution)/shard_map/ppermute | solution.py:213
  11.1 9.6 %collective-permute-start.3 = (f32[1,5,1,2048]{3,2,1,0:T(1,128)S(1)}, f32[1,5,1,2048]{3,2,1,0:T(1,128)S(1)}, u32[]{:S(2)}, u32[]{:S(2)}) collective-permute-start(f32[1,5,1,2048]{3,2,1,0:T(1,128)S(1)} %copy-done.6), channel_id=1, source_target_pairs={{8,16},{16,8},{12,20},{20,12},{24,0},{0,24},{28,4},{4,28},{9,17},{... | collective-permute-start | bytes 122888 | tf_op jit(solution)/shard_map/ppermute | solution.py:213
  13.6 8.0 %collective-permute-start.1 = (f32[1,5,3,2048]{3,2,1,0:T(4,128)S(1)}, f32[1,5,3,2048]{3,2,1,0:T(4,128)S(1)}, u32[]{:S(2)}, u32[]{:S(2)}) collective-permute-start(f32[1,5,3,2048]{3,2,1,0:T(4,128)S(1)} %copy-done.5), channel_id=1, source_target_pairs={{4,8},{8,4},{12,16},{16,12},{20,24},{24,20},{28,0},{0,28},{5,9},{9... | collective-permute-start | bytes 368648 | tf_op jit(solution)/shard_map/ppermute | solution.py:213
  14.9 6.7 %copy-start = (f32[5,1,32,2048]{3,2,1,0:T(8,128)S(1)}, f32[5,1,32,2048]{3,2,1,0:T(8,128)}, u32[]{:S(2)}) copy-start(f32[5,1,32,2048]{3,2,1,0:T(8,128)} %shard_map.101) | copy-start | bytes 3932164

commit v14 on v8

--- a/solution.py
+++ b/solution.py
@@ -114,8 +114,9 @@
     wx = wx_ref[...]
     own = own_ref[...]
     nb = count // WIDTH
+    d_all = dot(own, jnp.concatenate(flux_y, axis=1))
     for f in range(5):
-        d_y = dot(own, flux_y[f])
+        d_y = d_all[:, f * count : (f + 1) * count]
         fx = flux_x[f]
         rows = fx.shape[0]
         stacked = jnp.concatenate([fx[:, b * WIDTH : (b + 1) * WIDTH] for b in range(nb)], axis=0)
@@ -148,8 +149,13 @@
 
 def correct_kernel(spread_ref, partial_ref, *refs):
     recv_refs, out_ref = refs[:-1], refs[-1]
-    received = jnp.concatenate([r[0, 0] for r in recv_refs], axis=0)
-    out_ref[0, 0] = partial_ref[0, 0] - dot(spread_ref[...], received)
+    count = partial_ref.shape[-1]
+    received = jnp.concatenate(
+        [jnp.concatenate([r[0, f] for r in recv_refs], axis=0) for f in range(5)], axis=1
+    )
+    correction = dot(spread_ref[...], received)
+    for f in range(5):
+        out_ref[f, 0] = partial_ref[f, 0] - correction[:, f * count : (f + 1) * count]
 
 
 def full_spec(shape):
@@ -213,13 +219,12 @@
             out_specs=out_spec,
             out_shape=out_shape,
         )(wx, jnp.asarray(own), density, momentum, energy)
-        field_spec = pl.BlockSpec((1, 1, rows, count), lambda z, f: (f, z, 0, 0))
         return pl.pallas_call(
             correct_kernel,
-            grid=(planes, 5),
-            in_specs=[pl.BlockSpec(spread.shape, lambda z, f: (0, 0)), field_spec]
-            + [pl.BlockSpec((1, 1) + r.shape[2:], lambda z, f: (z, f, 0, 0)) for r in received],
-            out_specs=field_spec,
+            grid=(planes,),
+            in_specs=[full_spec(spread.shape), out_spec]
+            + [pl.BlockSpec((1,) + r.shape[1:], lambda z: (z, 0, 0, 0)) for r in received],
+            out_specs=out_spec,
             out_shape=out_shape,
             input_output_aliases={1: 0},
         )(spread, partial, *received)

time: 25.3 us -> 23.9 us (0.945)
  Pallas kernels: 14.7 us -> 13.3 us
    pallas_call x1, Pallas kernels: 4.96 us -> 3.59 us  [local(): pl.pallas_call(correct_kernel, grid=(planes,), in_specs=[full_spec(spread...]
  transfers between devices with their start and end apart: 4 -> 4, of which waited for: 0 -> 0; matrix products, arithmetic and copies ran while one was open for 3% -> 3% of each run, Pallas kernels for 27% -> 28%
where the time goes in v14:
time: 23.9 us; the launch traced here: 23.7 us
  Pallas kernels  13.3 us (56%)
  starting transfers between devices  8.31 us (35%)
  local copies, waits for them, and re-layouts  2.01 us (8%)
    ppermute x4, starting transfers between devices, local(): received.append(lax.ppermute(message, 'row', perm))  8.31 us
    pallas_call x1, Pallas kernels, local(): pl.pallas_call(lambda *r: local_kernel(count, *r), grid=(planes,), in_spe...  6.65 us
    pallas_call x1, Pallas kernels, local(): pl.pallas_call(correct_kernel, grid=(planes,), in_specs=[full_spec(spread...  3.59 us
    pallas_call x1, Pallas kernels, local(): pl.pallas_call(lambda *r: moments_kernel(split_of, choices, *r), grid=(pl...  3.02 us
    unnamed x16, local copies, waits for them, and re-layouts  1.33 us
    concatenate x1, local copies, waits for them, and re-layouts, local(): spread = jnp.concatenate(spreads, axis=1)  0.67 us
  transfers between devices with their start and end apart: 4, of which 0 were waited for; matrix products, arithmetic and copies ran while one was open for 3% of the time, Pallas kernels for 28%

profile of v14, /device:TPU:0, one launch (start us, length us, event | category | flops | bytes accessed | tf_op | source)
XLA Modules:
  0.0 23.7 jit_solution(1970412425234985096)
XLA Ops:
  0.0 0.0 copy-start.4
  0.0 0.0 copy-start.5
  0.0 0.0 copy-start.6
  0.0 0.0 copy-start.7
  0.0 3.0 %shard_map.101 = (f32[1,5,3,2048]{3,2,1,0:T(4,128)}, f32[1,5,3,2048]{3,2,1,0:T(4,128)}, f32[1,5,1,2048]{3,2,1,0:T(1,128)}, f32[1,5,1,2048]{3,2,1,0:T(1,128)}) custom-call(s32[1]{0:T(128)} %bitcast.r_0_, f32[8,32]{1,0:T(8,128)} %constant.68.clone.r_1_, f32[1,32,2048]{2,1,0:T(8,128)} %r_2_.3, f32[3,1,32,2048]{3,2,1,0:T(8,128)} %r_3_.3, f32[1,32,2048]{2,1,0:T(8,128)} %r_4_.3), custom_call_target="tpu_custom_call" | custom-call | tf_op jit(solution)/shard_map/pallas_call | solution.py:194
  3.0 3.0 %collective-permute-start.2 = (f32[1,5,1,2048]{3,2,1,0:T(1,128)}, f32[1,5,1,2048]{3,2,1,0:T(1,128)S(1)}, u32[]{:S(2)}, u32[]{:S(2)}) collective-permute-start(f32[1,5,1,2048]{3,2,1,0:T(1,128)} %get-tuple-element.11), channel_id=1, source_target_pairs={{0,8},{8,0},{4,12},{12,4},{16,24},{24,16},{20,28},{28,20},{1,9},{9... | collective-permute-start | bytes 122888 | tf_op jit(solution)/shard_map/ppermute | solution.py:205
  6.1 2.5 %collective-permute-start.3 = (f32[1,5,1,2048]{3,2,1,0:T(1,128)}, f32[1,5,1,2048]{3,2,1,0:T(1,128)S(1)}, u32[]{:S(2)}, u32[]{:S(2)}) collective-permute-start(f32[1,5,1,2048]{3,2,1,0:T(1,128)} %get-tuple-element.12), channel_id=1, source_target_pairs={{8,16},{16,8},{12,20},{20,12},{24,0},{0,24},{28,4},{4,28},{9,17},{... | collective-permute-start | bytes 122888 | tf_op jit(solution)/shard_map/ppermute | solution.py:205
  8.5 1.5 %collective-permute-start = (f32[1,5,3,2048]{3,2,1,0:T(4,128)}, f32[1,5,3,2048]{3,2,1,0:T(4,128)S(1)}, u32[]{:S(2)}, u32[]{:S(2)}) collective-permute-start(f32[1,5,3,2048]{3,2,1,0:T(4,128)} %get-tuple-element.9), channel_id=1, source_target_pairs={{0,4},{4,0},{8,12},{12,8},{16,20},{20,16},{24,28},{28,24},{1,5},{5... | collective-permute-start | bytes 368648 | tf_op jit(solution)/shard_map/ppermute | solution.py:205
  10.0 1.3 %collective-permute-start.1 = (f32[1,5,3,2048]{3,2,1,0:T(4,128)}, f32[1,5,3,2048]{3,2,1,0:T(4,128)S(1)}, u32[]{:S(2)}, u32[]{:S(2)}) collective-permute-start(f32[1,5,3,2048]{3,2,1,0:T(4,128)} %get-tuple-element.10), channel_id=1, source_target_pairs={{4,8},{8,4},{12,16},{16,12},{20,24},{24,20},{28,0},{0,28},{5,9},{9... | collective-permute-start | bytes 368648 | tf_op jit(solution)/shard_map/ppermute | solution.py:205
  11.3 0.0 copy-done.4
  11.3 0.0 copy-done.5
  11.4 0.0 copy-done.6
  11.4 0.0 copy-done.7
  11.4 0.7 %copy.12.spread_ref = f32[32,8]{1,0:T(8,128)} copy(f32[32,8]{0,1:T(8,128)S(1)} %pad_maximum_fusion) | data formatting | bytes 2048 | tf_op jit(solution)/shard_map/concatenate | solution.py:211
  12.1 6.6 %shard_map.100.partial_ref = f32[5,1,32,2048]{3,2,1,0:T(8,128)} custom-call(f32[128,384]{1,0:T(8,128)} %constant.73.clone.r_0_, f32[32,32]{1,0:T(8,128)} %constant.74.clone.r_1_, f32[1,32,2048]{2,1,0:T(8,128)} %r_2_.3, f32[3,1,32,2048]{3,2,1,0:T(8,128)} %r_3_.3, f32[1,32,2048]{2,1,0:T(8,128)} %r_4_.3), custom_call_target="tpu_custom_call" | custom-call | tf_op jit(solution)/shard_map/pallas_call | solution.py:215
  18.7 0.0 collective-permute-done.2.refs_2_
  18.7 0.0 copy-start.2
  18.7 0.0 collective-permute-done.3.refs_3_
  18.7 0.0 copy-start.3
  18.7 0.0 collective-permute-done.refs_0_
  18.8 0.0 copy-start
  18.8 0.0 collective-permute-done.1.refs_1_
  18.8 0.6 %copy-done.2 = f32[1,5,1,2048]{3,2,1,0:T(1,128)} copy-done((f32[1,5,1,2048]{3,2,1,0:T(1,128)}, f32[1,5,1,2048]{3,2,1,0:T(1,128)S(1)}, u32[]{:S(2)}) %copy-start.2) | copy-done | bytes 40984
  19.3 0.0 copy-done.3
  19.4 0.0 copy-done
  19.4 0.0 copy-start.1
  19.4 0.7 %copy-done.1 = f32[1,5,3,2048]{3,2,1,0:T(4,128)} copy-done((f32[1,5,3,2048]{3,2,1,0:T(4,128)}, f32[1,5,3,2048]{3,2,1,0:T(4,128)S(1)}, u32[]{:S(2)}) %copy-start.1) | copy-done | bytes 122904
  20.1 3.6 %shard_map.102 = f32[5,1,32,2048]{3,2,1,0:T(8,128)} custom-call(f32[32,8]{1,0:T(8,128)} %copy.12.spread_ref, f32[5,1,32,2048]{3,2,1,0:T(8,128)} %shard_map.100.partial_ref, f32[1,5,3,2048]{3,2,1,0:T(4,128)} %copy-done, f32[1,5,3,2048]{3,2,1,0:T(4,128)} %copy-done.1, f32[1,5,1,2048]{3,2,1,0:T(1,128)} %copy-done.2, ...), custom_call_target="tpu_custom_call", output_to_operand_aliasing={{}: (1, {})} | custom-call | tf_op jit(solution)/shard_map/pallas_call | solution.py:222
  (3 shorter events, 0.0 us)
Async XLA Ops:
  0.0 11.3 %copy-start.4 = (f32[32,3]{0,1:T(4,128)S(1)}, f32[32,3]{0,1:T(4,128)}, u32[]{:S(2)}) copy-start(f32[32,3]{0,1:T(4,128)} %constant.70.clone) | copy-start | bytes 1156
  0.0 11.3 %copy-start.5 = (f32[32,3]{0,1:T(4,128)S(1)}, f32[32,3]{0,1:T(4,128)}, u32[]{:S(2)}) copy-start(f32[32,3]{0,1:T(4,128)} %constant.69.clone) | copy-start | bytes 1156
  0.0 11.3 %copy-start.6 = (f32[32,1]{0,1:T(1,128)S(1)}, f32[32,1]{0,1:T(1,128)}, u32[]{:S(2)}) copy-start(f32[32,1]{0,1:T(1,128)} %constant.72.clone) | copy-start | bytes 388
  0.0 11.4 %copy-start.7 = (f32[32,1]{0,1:T(1,128)S(1)}, f32[32,1]{0,1:T(1,128)}, u32[]{:S(2)}) copy-start(f32[32,1]{0,1:T(1,128)} %constant.71.clone) | copy-start | bytes 388
  3.0 15.7 %collective-permute-start.2 = (f32[1,5,1,2048]{3,2,1,0:T(1,128)}, f32[1,5,1,2048]{3,2,1,0:T(1,128)S(1)}, u32[]{:S(2)}, u32[]{:S(2)}) collective-permute-start(f32[1,5,1,2048]{3,2,1,0:T(1,128)} %get-tuple-element.11), channel_id=1, source_target_pairs={{0,8},{8,0},{4,12},{12,4},{16,24},{24,16},{20,28},{28,20},{1,9},{9... | collective-permute-start | bytes 122888 | tf_op jit(solution)/shard_map/ppermute | solution.py:205
  6.1 12.7 %collective-permute-start.3 = (f32[1,5,1,2048]{3,2,1,0:T(1,128)}, f32[1,5,1,2048]{3,2,1,0:T(1,128)S(1)}, u32[]{:S(2)}, u32[]{:S(2)}) collective-permute-start(f32[1,5,1,2048]{3,2,1,0:T(1,128)} %get-tuple-element.12), channel_id=1, source_target_pairs={{8,16},{16,8},{12,20},{20,12},{24,0},{0,24},{28,4},{4,28},{9,17},{... | collective-permute-start | bytes 122888 | tf_op jit(solution)/shard_map/ppermute | solution.py:205
  8.5 10.2 %collective-permute-start = (f32[1,5,3,2048]{3,2,1,0:T(4,128)}, f32[1,5,3,2048]{3,2,1,0:T(4,128)S(1)}, u32[]{:S(2)}, u32[]{:S(2)}) collective-permute-start(f32[1,5,3,2048]{3,2,1,0:T(4,128)} %get-tuple-element.9), channel_id=1, source_target_pairs={{0,4},{4,0},{8,12},{12,8},{16,20},{20,16},{24,28},{28,24},{1,5},{5... | collective-permute-start | bytes 368648 | tf_op jit(solution)/shard_map/ppermute | solution.py:205
  10.0 8.7 %collective-permute-start.1 = (f32[1,5,3,2048]{3,2,1,0:T(4,128)}, f32[1,5,3,2048]{3,2,1,0:T(4,128)S(1)}, u32[]{:S(2)}, u32[]{:S(2)}) collective-permute-start(f32[1,5,3,2048]{3,2,1,0:T(4,128)} %get-tuple-element.10), channel_id=1, source_target_pairs={{4,8},{8,4},{12,16},{16,12},{20,24},{24,20},{28,0},{0,28},{5,9},{9... | collective-permute-start | bytes 368648 | tf_op jit(solution)/shard_map/ppermute | solution.py:205
  18.7 0.6 %copy-start.2 = (f32[1,5,1,2048]{3,2,1,0:T(1,128)}, f32[1,5,1,2048]{3,2,1,0:T(1,128)S(1)}, u32[]{:S(2)}) copy-start(f32[1,5,1,2048]{3,2,1,0:T(1,128)S(1)} %collective-permute-done.2.refs_2_) | copy-start | bytes 122884
  18.7 0.6 %copy-start.3 = (f32[1,5,1,2048]{3,2,1,0:T(1,128)}, f32[1,5,1,2048]{3,2,1,0:T(1,128)S(1)}, u32[]{:S(2)}) copy-start(f32[1,5,1,2048]{3,2,1,0:T(1,128)S(1)} %collective-permute-done.3.refs_3_) | copy-start | bytes 122884
  18.8 0.7 %copy-start = (f32[1,5,3,2048]{3,2,1,0:T(4,128)}, f32[1,5,3,2048]{3,2,1,0:T(4,128)S(1)}, u32[]{:S(2)}) copy-start(f32[1,5,3,2048]{3,2,1,0:T(4,128)S(1)} %collective-permute-done.refs_0_) | copy-start | bytes 368644
  19.4 0.7 %copy-start.1 = (f32[1,5,3,2048]{3,2,1,0:T(4,128)}, f32[1,5,3,2048]{3,2,1,0:T(4,128)S(1)}, u32[]{:S(2)}) copy-start(f32[1,5,3,2048]{3,2,1,0:T(4,128)S(1)} %collective-permute-done.1.refs_1_) | copy-start | bytes 368644

commit v15 on v9

--- a/solution.py
+++ b/solution.py
@@ -109,12 +109,14 @@
             out_ref[0, f] = jnp.where(pick, moments[lo:hi], moments[lo2:hi2])
 
 
-def local_kernel(count, wx_ref, own_ref, rho_ref, mom_ref, energy_ref, out_ref):
+def local_kernel(count, wx_ref, own_ref, rho_ref, mom_ref, energy_ref, out_hbm, out_v, out_sem):
     flux_x, flux_y = plane_fluxes(rho_ref, mom_ref, energy_ref)
     wx = wx_ref[...]
     own = own_ref[...]
+    plane = pl.ds(pl.program_id(0), 1)
     nb = count // WIDTH
     d_all = dot(own, jnp.concatenate(flux_y, axis=1))
+    stores = []
     for f in range(5):
         d_y = d_all[:, f * count : (f + 1) * count]
         fx = flux_x[f]
@@ -129,7 +131,12 @@
                 + parts[b * rows : (b + 1) * rows, WIDTH : 2 * WIDTH]
                 + parts[bn * rows : (bn + 1) * rows, 2 * WIDTH :]
             )
-            out_ref[f, 0, :, b * WIDTH : (b + 1) * WIDTH] = -(d_x + d_y[:, b * WIDTH : (b + 1) * WIDTH])
+            out_v[f, 0, :, b * WIDTH : (b + 1) * WIDTH] = -(d_x + d_y[:, b * WIDTH : (b + 1) * WIDTH])
+        store = pltpu.make_async_copy(out_v.at[f], out_hbm.at[f, plane], out_sem.at[f])
+        store.start()
+        stores.append(store)
+    for store in stores:
+        store.wait()
 
 
 def exchange_plan(groups, shift_list):
@@ -205,8 +212,12 @@
             lambda *r: local_kernel(count, *r),
             grid=(planes,),
             in_specs=[full_spec(wx.shape), full_spec(own.shape)] + plane_specs,
-            out_specs=out_spec,
+            out_specs=pl.BlockSpec(memory_space=pl.ANY),
             out_shape=out_shape,
+            scratch_shapes=[
+                pltpu.VMEM((5, 1, rows, count), jnp.float32),
+                pltpu.SemaphoreType.DMA((5,)),
+            ],
         )(wx, jnp.asarray(own), density, momentum, energy)
         received = jnp.concatenate(received, axis=2)
         return partial - jnp.einsum(

time: 22.1 us -> 22.1 us (level)
  Pallas kernels: 9.66 us -> 9.35 us
  waiting for transfers between devices: 0.23 us -> 0.51 us
    pallas_call x1, Pallas kernels: 6.65 us -> 6.34 us  [local(): pl.pallas_call(lambda *r: local_kernel(count, *r), grid=(planes,), in_spe...]
    ppermute x4, waiting for transfers between devices: 0.23 us -> 0.51 us  [local(): received.append(lax.ppermute(message, 'row', perm))]
  transfers between devices with their start and end apart: 4 -> 4, of which waited for: 1 -> 1; matrix products, arithmetic and copies ran while one was open for 0% -> 0% of each run, Pallas kernels for 30% -> 29%
where the time goes in v15:
time: 22.1 us; the launch traced here: 21.9 us
  Pallas kernels  9.35 us (42%)
  starting transfers between devices  8.31 us (38%)
  matrix products  3.66 us (17%)
  waiting for transfers between devices  0.51 us (2%)
    ppermute x4, starting transfers between devices, local(): received.append(lax.ppermute(message, 'row', perm))  8.31 us
    pallas_call x1, Pallas kernels, local(): pl.pallas_call(lambda *r: local_kernel(count, *r), grid=(planes,), in_spe...  6.34 us
    dot_general x1, matrix products, local(): return partial - jnp.einsum('pr,zfrx->fzpx', spread, received, precision=HI)  3.66 us
    pallas_call x1, Pallas kernels, local(): pl.pallas_call(lambda *r: moments_kernel(split_of, choices, *r), grid=(pl...  3.01 us
    ppermute x4, waiting for transfers between devices, local(): received.append(lax.ppermute(message, 'row', perm))  0.51 us
  transfers between devices with their start and end apart: 4, of which 1 were waited for; matrix products, arithmetic and copies ran while one was open for 0% of the time, Pallas kernels for 29%

profile of v15, /device:TPU:0, one launch (start us, length us, event | category | flops | bytes accessed | tf_op | source)
XLA Modules:
  0.0 21.9 jit_solution(50992644353788558)
XLA Ops:
  0.0 0.0 copy-start
  0.0 0.0 copy-start.1
  0.0 0.0 copy-start.2
  0.0 0.0 copy-start.3
  0.0 3.0 %shard_map.101 = (f32[1,5,3,2048]{3,2,1,0:T(4,128)}, f32[1,5,3,2048]{3,2,1,0:T(4,128)}, f32[1,5,1,2048]{3,2,1,0:T(1,128)}, f32[1,5,1,2048]{3,2,1,0:T(1,128)}) custom-call(s32[1]{0:T(128)} %bitcast.r_0_, f32[8,32]{1,0:T(8,128)} %constant.68.clone.r_1_, f32[1,32,2048]{2,1,0:T(8,128)} %r_2_.3, f32[3,1,32,2048]{3,2,1,0:T(8,128)} %r_3_.3, f32[1,32,2048]{2,1,0:T(8,128)} %r_4_.3), custom_call_target="tpu_custom_call" | custom-call | tf_op jit(solution)/shard_map/pallas_call | solution.py:190
  3.0 3.0 %collective-permute-start.2 = (f32[1,5,1,2048]{3,2,1,0:T(1,128)}, f32[1,5,1,2048]{3,2,1,0:T(1,128)S(1)}, u32[]{:S(2)}, u32[]{:S(2)}) collective-permute-start(f32[1,5,1,2048]{3,2,1,0:T(1,128)} %get-tuple-element.11), channel_id=1, source_target_pairs={{0,8},{8,0},{4,12},{12,4},{16,24},{24,16},{20,28},{28,20},{1,9},{9... | collective-permute-start | bytes 122888 | tf_op jit(solution)/shard_map/ppermute | solution.py:201
  6.0 2.5 %collective-permute-start.3 = (f32[1,5,1,2048]{3,2,1,0:T(1,128)}, f32[1,5,1,2048]{3,2,1,0:T(1,128)S(1)}, u32[]{:S(2)}, u32[]{:S(2)}) collective-permute-start(f32[1,5,1,2048]{3,2,1,0:T(1,128)} %get-tuple-element.12), channel_id=1, source_target_pairs={{8,16},{16,8},{12,20},{20,12},{24,0},{0,24},{28,4},{4,28},{9,17},{... | collective-permute-start | bytes 122888 | tf_op jit(solution)/shard_map/ppermute | solution.py:201
  8.5 1.5 %collective-permute-start = (f32[1,5,3,2048]{3,2,1,0:T(4,128)}, f32[1,5,3,2048]{3,2,1,0:T(4,128)S(1)}, u32[]{:S(2)}, u32[]{:S(2)}) collective-permute-start(f32[1,5,3,2048]{3,2,1,0:T(4,128)} %get-tuple-element.9), channel_id=1, source_target_pairs={{0,4},{4,0},{8,12},{12,8},{16,20},{20,16},{24,28},{28,24},{1,5},{5... | collective-permute-start | bytes 368648 | tf_op jit(solution)/shard_map/ppermute | solution.py:201
  10.0 1.3 %collective-permute-start.1 = (f32[1,5,3,2048]{3,2,1,0:T(4,128)}, f32[1,5,3,2048]{3,2,1,0:T(4,128)S(1)}, u32[]{:S(2)}, u32[]{:S(2)}) collective-permute-start(f32[1,5,3,2048]{3,2,1,0:T(4,128)} %get-tuple-element.10), channel_id=1, source_target_pairs={{4,8},{8,4},{12,16},{16,12},{20,24},{24,20},{28,0},{0,28},{5,9},{9... | collective-permute-start | bytes 368648 | tf_op jit(solution)/shard_map/ppermute | solution.py:201
  11.3 0.0 copy-done
  11.3 0.0 copy-done.1
  11.3 0.0 copy-done.2
  11.4 0.0 copy-done.3
  11.4 6.3 %shard_map.100 = f32[5,1,32,2048]{3,2,1,0:T(8,128)} custom-call(f32[128,384]{1,0:T(8,128)} %constant.73.clone.r_0_, f32[32,32]{1,0:T(8,128)} %constant.74.clone.r_1_, f32[1,32,2048]{2,1,0:T(8,128)} %r_2_.3, f32[3,1,32,2048]{3,2,1,0:T(8,128)} %r_3_.3, f32[1,32,2048]{2,1,0:T(8,128)} %r_4_.3), custom_call_target="tpu_custom_call" | custom-call | tf_op jit(solution)/shard_map/pallas_call | solution.py:211
  17.7 0.0 collective-permute-done.2
  17.7 0.0 collective-permute-done.3
  17.7 0.0 collective-permute-done
  17.8 0.5 %collective-permute-done.1 = f32[1,5,3,2048]{3,2,1,0:T(4,128)S(1)} collective-permute-done((f32[1,5,3,2048]{3,2,1,0:T(4,128)}, f32[1,5,3,2048]{3,2,1,0:T(4,128)S(1)}, u32[]{:S(2)}, u32[]{:S(2)}) %collective-permute-start.1) | collective-permute-done | bytes 122912 | tf_op jit(solution)/shard_map/ppermute | solution.py:201
  18.3 3.7 %fusion = f32[5,1,32,2048]{3,2,1,0:T(8,128)} fusion(f32[5,1,32,2048]{3,2,1,0:T(8,128)} %shard_map.100, f32[1,5,1,2048]{3,2,1,0:T(1,128)S(1)} %collective-permute-done.3, f32[1,5,1,2048]{3,2,1,0:T(1,128)S(1)} %collective-permute-done.2, f32[1,5,3,2048]{3,2,1,0:T(4,128)S(1)} %collective-permute-done.1, f32[1,5,3,2048]{3,2,1,0:T(4,128)S(1)} %collective-permute-done, ...), kind=kOutput, calls=%fused_computation.1 | convolution fusion | flops 32031488 | bytes 2950144 | tf_op jit(solution)/shard_map/pr,zfrx->fzpx/dot_general | solution.py:223
  (2 shorter events, 0.0 us)
Async XLA Ops:
  0.0 11.3 %copy-start = (f32[32,3]{0,1:T(4,128)S(1)}, f32[32,3]{0,1:T(4,128)}, u32[]{:S(2)}) copy-start(f32[32,3]{0,1:T(4,128)} %constant.70.clone) | copy-start | bytes 1156
  0.0 11.3 %copy-start.1 = (f32[32,3]{0,1:T(4,128)S(1)}, f32[32,3]{0,1:T(4,128)}, u32[]{:S(2)}) copy-start(f32[32,3]{0,1:T(4,128)} %constant.69.clone) | copy-start | bytes 1156
  0.0 11.3 %copy-start.2 = (f32[32,1]{0,1:T(1,128)S(1)}, f32[32,1]{0,1:T(1,128)}, u32[]{:S(2)}) copy-start(f32[32,1]{0,1:T(1,128)} %constant.72.clone) | copy-start | bytes 388
  0.0 11.3 %copy-start.3 = (f32[32,1]{0,1:T(1,128)S(1)}, f32[32,1]{0,1:T(1,128)}, u32[]{:S(2)}) copy-start(f32[32,1]{0,1:T(1,128)} %constant.71.clone) | copy-start | bytes 388
  3.0 14.7 %collective-permute-start.2 = (f32[1,5,1,2048]{3,2,1,0:T(1,128)}, f32[1,5,1,2048]{3,2,1,0:T(1,128)S(1)}, u32[]{:S(2)}, u32[]{:S(2)}) collective-permute-start(f32[1,5,1,2048]{3,2,1,0:T(1,128)} %get-tuple-element.11), channel_id=1, source_target_pairs={{0,8},{8,0},{4,12},{12,4},{16,24},{24,16},{20,28},{28,20},{1,9},{9... | collective-permute-start | bytes 122888 | tf_op jit(solution)/shard_map/ppermute | solution.py:201
  6.0 11.7 %collective-permute-start.3 = (f32[1,5,1,2048]{3,2,1,0:T(1,128)}, f32[1,5,1,2048]{3,2,1,0:T(1,128)S(1)}, u32[]{:S(2)}, u32[]{:S(2)}) collective-permute-start(f32[1,5,1,2048]{3,2,1,0:T(1,128)} %get-tuple-element.12), channel_id=1, source_target_pairs={{8,16},{16,8},{12,20},{20,12},{24,0},{0,24},{28,4},{4,28},{9,17},{... | collective-permute-start | bytes 122888 | tf_op jit(solution)/shard_map/ppermute | solution.py:201
  8.5 9.2 %collective-permute-start = (f32[1,5,3,2048]{3,2,1,0:T(4,128)}, f32[1,5,3,2048]{3,2,1,0:T(4,128)S(1)}, u32[]{:S(2)}, u32[]{:S(2)}) collective-permute-start(f32[1,5,3,2048]{3,2,1,0:T(4,128)} %get-tuple-element.9), channel_id=1, source_target_pairs={{0,4},{4,0},{8,12},{12,8},{16,20},{20,16},{24,28},{28,24},{1,5},{5... | collective-permute-start | bytes 368648 | tf_op jit(solution)/shard_map/ppermute | solution.py:201
  10.0 8.2 %collective-permute-start.1 = (f32[1,5,3,2048]{3,2,1,0:T(4,128)}, f32[1,5,3,2048]{3,2,1,0:T(4,128)S(1)}, u32[]{:S(2)}, u32[]{:S(2)}) collective-permute-start(f32[1,5,3,2048]{3,2,1,0:T(4,128)} %get-tuple-element.10), channel_id=1, source_target_pairs={{4,8},{8,4},{12,16},{16,12},{20,24},{24,20},{28,0},{0,28},{5,9},{9... | collective-permute-start | bytes 368648 | tf_op jit(solution)/shard_map/ppermute | solution.py:201

commit v16 on v9

--- a/solution.py
+++ b/solution.py
@@ -96,6 +96,10 @@
     return flux_x, flux_y
 
 
+def side(r, step):
+    return (r // step + (r % 2 if step == 2 else 0)) % 2
+
+
 def moments_kernel(splits, choices, index_ref, weights_ref, rho_ref, mom_ref, energy_ref, *out_refs):
     _, flux_y = plane_fluxes(rho_ref, mom_ref, energy_ref)
     weights = weights_ref[...]
@@ -103,7 +107,7 @@
     for f in range(5):
         moments = dot(weights, flux_y[f])
         for (step, phase, first, second), out_ref in zip(choices, out_refs):
-            pick = (index // step) % 2 != phase
+            pick = side(index, step) != phase
             lo, hi = splits[first]
             lo2, hi2 = splits[second]
             out_ref[0, f] = jnp.where(pick, moments[lo:hi], moments[lo2:hi2])
@@ -139,9 +143,9 @@
     for step, phase in ((1, 0), (1, 1), (2, 0), (2, 1)):
         perm = []
         for r in range(groups):
-            if (r // step) % 2 == phase:
+            if side(r, step) == phase:
                 up = (r + step) % groups
-                assert (up // step) % 2 != phase
+                assert side(up, step) != phase
                 perm += [(r, up), (up, r)]
         plans.append((step, phase, step, groups - step, perm))
     return plans
@@ -192,7 +196,7 @@
         spreads = []
         for (step, phase, first, second, perm), message in zip(plan, messages):
             received.append(lax.ppermute(message, "row", perm))
-            take = ((index // step) % 2 == phase).astype(jnp.float32)
+            take = (side(index, step) == phase).astype(jnp.float32)
             spreads.append(
                 take * jnp.asarray(by_shift[first][0])
                 + (1.0 - take) * jnp.asarray(by_shift[second][0])

time: 22.1 us -> 21.9 us (level)
  transfers between devices with their start and end apart: 4 -> 4, of which waited for: 1 -> 0; matrix products, arithmetic and copies ran while one was open for 0% -> 0% of each run, Pallas kernels for 30% -> 31%
where the time goes in v16:
time: 21.9 us; the launch traced here: 21.7 us
  Pallas kernels  9.67 us (44%)
  starting transfers between devices  8.31 us (38%)
  matrix products  3.67 us (17%)
    ppermute x4, starting transfers between devices, local(): received.append(lax.ppermute(message, 'row', perm))  8.31 us
    pallas_call x1, Pallas kernels, local(): pl.pallas_call(lambda *r: local_kernel(count, *r), grid=(planes,), in_spe...  6.66 us
    dot_general x1, matrix products, local(): return partial - jnp.einsum('pr,zfrx->fzpx', spread, received, precision=HI)  3.67 us
    pallas_call x1, Pallas kernels, local(): pl.pallas_call(lambda *r: moments_kernel(split_of, choices, *r), grid=(pl...  3.01 us
  transfers between devices with their start and end apart: 4, of which 0 were waited for; matrix products, arithmetic and copies ran while one was open for 0% of the time, Pallas kernels for 31%

profile of v16, /device:TPU:0, one launch (start us, length us, event | category | flops | bytes accessed | tf_op | source)
XLA Modules:
  0.0 21.7 jit_solution(9871480006862830422)
XLA Ops:
  0.0 0.0 copy-start
  0.0 0.0 copy-start.1
  0.0 0.0 copy-start.2
  0.0 0.0 copy-start.3
  0.0 3.0 %shard_map.101 = (f32[1,5,3,2048]{3,2,1,0:T(4,128)}, f32[1,5,3,2048]{3,2,1,0:T(4,128)}, f32[1,5,1,2048]{3,2,1,0:T(1,128)}, f32[1,5,1,2048]{3,2,1,0:T(1,128)}) custom-call(s32[1]{0:T(128)} %bitcast.r_0_, f32[8,32]{1,0:T(8,128)} %constant.74.clone.r_1_, f32[1,32,2048]{2,1,0:T(8,128)} %r_2_.3, f32[3,1,32,2048]{3,2,1,0:T(8,128)} %r_3_.3, f32[1,32,2048]{2,1,0:T(8,128)} %r_4_.3), custom_call_target="tpu_custom_call" | custom-call | tf_op jit(solution)/shard_map/pallas_call | solution.py:187
  3.0 3.0 %collective-permute-start.2 = (f32[1,5,1,2048]{3,2,1,0:T(1,128)}, f32[1,5,1,2048]{3,2,1,0:T(1,128)S(1)}, u32[]{:S(2)}, u32[]{:S(2)}) collective-permute-start(f32[1,5,1,2048]{3,2,1,0:T(1,128)} %get-tuple-element.11), channel_id=1, source_target_pairs={{0,8},{8,0},{12,20},{20,12},{16,24},{24,16},{28,4},{4,28},{1,9},{9... | collective-permute-start | bytes 122888 | tf_op jit(solution)/shard_map/ppermute | solution.py:198
  6.0 2.5 %collective-permute-start.3 = (f32[1,5,1,2048]{3,2,1,0:T(1,128)}, f32[1,5,1,2048]{3,2,1,0:T(1,128)S(1)}, u32[]{:S(2)}, u32[]{:S(2)}) collective-permute-start(f32[1,5,1,2048]{3,2,1,0:T(1,128)} %get-tuple-element.12), channel_id=1, source_target_pairs={{4,12},{12,4},{8,16},{16,8},{20,28},{28,20},{24,0},{0,24},{5,13},{... | collective-permute-start | bytes 122888 | tf_op jit(solution)/shard_map/ppermute | solution.py:198
  8.5 1.1 %collective-permute-start = (f32[1,5,3,2048]{3,2,1,0:T(4,128)}, f32[1,5,3,2048]{3,2,1,0:T(4,128)S(1)}, u32[]{:S(2)}, u32[]{:S(2)}) collective-permute-start(f32[1,5,3,2048]{3,2,1,0:T(4,128)} %get-tuple-element.9), channel_id=1, source_target_pairs={{0,4},{4,0},{8,12},{12,8},{16,20},{20,16},{24,28},{28,24},{1,5},{5... | collective-permute-start | bytes 368648 | tf_op jit(solution)/shard_map/ppermute | solution.py:198
  9.6 1.7 %collective-permute-start.1 = (f32[1,5,3,2048]{3,2,1,0:T(4,128)}, f32[1,5,3,2048]{3,2,1,0:T(4,128)S(1)}, u32[]{:S(2)}, u32[]{:S(2)}) collective-permute-start(f32[1,5,3,2048]{3,2,1,0:T(4,128)} %get-tuple-element.10), channel_id=1, source_target_pairs={{4,8},{8,4},{12,16},{16,12},{20,24},{24,20},{28,0},{0,28},{5,9},{9... | collective-permute-start | bytes 368648 | tf_op jit(solution)/shard_map/ppermute | solution.py:198
  11.3 0.0 copy-done
  11.3 0.0 copy-done.1
  11.3 0.0 copy-done.2
  11.4 0.0 copy-done.3
  11.4 6.7 %shard_map.100 = f32[5,1,32,2048]{3,2,1,0:T(8,128)} custom-call(f32[128,384]{1,0:T(8,128)} %constant.79.clone.r_0_, f32[32,32]{1,0:T(8,128)} %constant.80.clone.r_1_, f32[1,32,2048]{2,1,0:T(8,128)} %r_2_.3, f32[3,1,32,2048]{3,2,1,0:T(8,128)} %r_3_.3, f32[1,32,2048]{2,1,0:T(8,128)} %r_4_.3), custom_call_target="tpu_custom_call" | custom-call | tf_op jit(solution)/shard_map/pallas_call | solution.py:208
  18.0 0.0 collective-permute-done.2
  18.0 0.0 collective-permute-done.3
  18.0 0.0 collective-permute-done
  18.1 0.0 collective-permute-done.1
  18.1 3.7 %fusion = f32[5,1,32,2048]{3,2,1,0:T(8,128)} fusion(f32[5,1,32,2048]{3,2,1,0:T(8,128)} %shard_map.100, f32[1,5,1,2048]{3,2,1,0:T(1,128)S(1)} %collective-permute-done.3, f32[1,5,1,2048]{3,2,1,0:T(1,128)S(1)} %collective-permute-done.2, f32[1,5,3,2048]{3,2,1,0:T(4,128)S(1)} %collective-permute-done.1, f32[1,5,3,2048]{3,2,1,0:T(4,128)S(1)} %collective-permute-done, ...), kind=kOutput, calls=%fused_computation.1 | convolution fusion | flops 32031488 | bytes 2950144 | tf_op jit(solution)/shard_map/pr,zfrx->fzpx/dot_general | solution.py:216
  (2 shorter events, 0.0 us)
Async XLA Ops:
  0.0 11.3 %copy-start = (f32[32,3]{0,1:T(4,128)S(1)}, f32[32,3]{0,1:T(4,128)}, u32[]{:S(2)}) copy-start(f32[32,3]{0,1:T(4,128)} %constant.76.clone) | copy-start | bytes 1156
  0.0 11.3 %copy-start.1 = (f32[32,3]{0,1:T(4,128)S(1)}, f32[32,3]{0,1:T(4,128)}, u32[]{:S(2)}) copy-start(f32[32,3]{0,1:T(4,128)} %constant.75.clone) | copy-start | bytes 1156
  0.0 11.3 %copy-start.2 = (f32[32,1]{0,1:T(1,128)S(1)}, f32[32,1]{0,1:T(1,128)}, u32[]{:S(2)}) copy-start(f32[32,1]{0,1:T(1,128)} %constant.78.clone) | copy-start | bytes 388
  0.0 11.4 %copy-start.3 = (f32[32,1]{0,1:T(1,128)S(1)}, f32[32,1]{0,1:T(1,128)}, u32[]{:S(2)}) copy-start(f32[32,1]{0,1:T(1,128)} %constant.77.clone) | copy-start | bytes 388
  3.0 15.0 %collective-permute-start.2 = (f32[1,5,1,2048]{3,2,1,0:T(1,128)}, f32[1,5,1,2048]{3,2,1,0:T(1,128)S(1)}, u32[]{:S(2)}, u32[]{:S(2)}) collective-permute-start(f32[1,5,1,2048]{3,2,1,0:T(1,128)} %get-tuple-element.11), channel_id=1, source_target_pairs={{0,8},{8,0},{12,20},{20,12},{16,24},{24,16},{28,4},{4,28},{1,9},{9... | collective-permute-start | bytes 122888 | tf_op jit(solution)/shard_map/ppermute | solution.py:198
  6.0 12.0 %collective-permute-start.3 = (f32[1,5,1,2048]{3,2,1,0:T(1,128)}, f32[1,5,1,2048]{3,2,1,0:T(1,128)S(1)}, u32[]{:S(2)}, u32[]{:S(2)}) collective-permute-start(f32[1,5,1,2048]{3,2,1,0:T(1,128)} %get-tuple-element.12), channel_id=1, source_target_pairs={{4,12},{12,4},{8,16},{16,8},{20,28},{28,20},{24,0},{0,24},{5,13},{... | collective-permute-start | bytes 122888 | tf_op jit(solution)/shard_map/ppermute | solution.py:198
  8.5 9.5 %collective-permute-start = (f32[1,5,3,2048]{3,2,1,0:T(4,128)}, f32[1,5,3,2048]{3,2,1,0:T(4,128)S(1)}, u32[]{:S(2)}, u32[]{:S(2)}) collective-permute-start(f32[1,5,3,2048]{3,2,1,0:T(4,128)} %get-tuple-element.9), channel_id=1, source_target_pairs={{0,4},{4,0},{8,12},{12,8},{16,20},{20,16},{24,28},{28,24},{1,5},{5... | collective-permute-start | bytes 368648 | tf_op jit(solution)/shard_map/ppermute | solution.py:198
  9.6 8.5 %collective-permute-start.1 = (f32[1,5,3,2048]{3,2,1,0:T(4,128)}, f32[1,5,3,2048]{3,2,1,0:T(4,128)S(1)}, u32[]{:S(2)}, u32[]{:S(2)}) collective-permute-start(f32[1,5,3,2048]{3,2,1,0:T(4,128)} %get-tuple-element.10), channel_id=1, source_target_pairs={{4,8},{8,4},{12,16},{16,12},{20,24},{24,20},{28,0},{0,28},{5,9},{9... | collective-permute-start | bytes 368648 | tf_op jit(solution)/shard_map/ppermute | solution.py:198

commit v17 on v15

--- a/solution.py
+++ b/solution.py
@@ -96,6 +96,10 @@
     return flux_x, flux_y
 
 
+def side(r, step):
+    return (r // step + (r % 2 if step == 2 else 0)) % 2
+
+
 def moments_kernel(splits, choices, index_ref, weights_ref, rho_ref, mom_ref, energy_ref, *out_refs):
     _, flux_y = plane_fluxes(rho_ref, mom_ref, energy_ref)
     weights = weights_ref[...]
@@ -103,7 +107,7 @@
     for f in range(5):
         moments = dot(weights, flux_y[f])
         for (step, phase, first, second), out_ref in zip(choices, out_refs):
-            pick = (index // step) % 2 != phase
+            pick = side(index, step) != phase
             lo, hi = splits[first]
             lo2, hi2 = splits[second]
             out_ref[0, f] = jnp.where(pick, moments[lo:hi], moments[lo2:hi2])
@@ -146,9 +150,9 @@
     for step, phase in ((1, 0), (1, 1), (2, 0), (2, 1)):
         perm = []
         for r in range(groups):
-            if (r // step) % 2 == phase:
+            if side(r, step) == phase:
                 up = (r + step) % groups
-                assert (up // step) % 2 != phase
+                assert side(up, step) != phase
                 perm += [(r, up), (up, r)]
         plans.append((step, phase, step, groups - step, perm))
     return plans
@@ -199,7 +203,7 @@
         spreads = []
         for (step, phase, first, second, perm), message in zip(plan, messages):
             received.append(lax.ppermute(message, "row", perm))
-            take = ((index // step) % 2 == phase).astype(jnp.float32)
+            take = (side(index, step) == phase).astype(jnp.float32)
             spreads.append(
                 take * jnp.asarray(by_shift[first][0])
                 + (1.0 - take) * jnp.asarray(by_shift[second][0])

time: 22.1 us -> 21.7 us (0.982)
  waiting for transfers between devices: 0.51 us -> 0.12 us
    ppermute x4, waiting for transfers between devices: 0.51 us -> 0.12 us  [local(): received.append(lax.ppermute(message, 'row', perm))]
where the time goes in v17:
time: 21.7 us; the launch traced here: 21.6 us
  Pallas kernels  9.36 us (43%)
  starting transfers between devices  8.31 us (38%)
  matrix products  3.67 us (17%)
    ppermute x4, starting transfers between devices, local(): received.append(lax.ppermute(message, 'row', perm))  8.31 us
    pallas_call x1, Pallas kernels, local(): pl.pallas_call(lambda *r: local_kernel(count, *r), grid=(planes,), in_spe...  6.35 us
    dot_general x1, matrix products, local(): return partial - jnp.einsum('pr,zfrx->fzpx', spread, received, precision=HI)  3.67 us
    pallas_call x1, Pallas kernels, local(): pl.pallas_call(lambda *r: moments_kernel(split_of, choices, *r), grid=(pl...  3.01 us
  transfers between devices with their start and end apart: 4, of which 1 were waited for; matrix products, arithmetic and copies ran while one was open for 0% of the time, Pallas kernels for 29%

profile of v17, /device:TPU:0, one launch (start us, length us, event | category | flops | bytes accessed | tf_op | source)
XLA Modules:
  0.0 21.6 jit_solution(5857073801355268961)
XLA Ops:
  0.0 0.0 copy-start
  0.0 0.0 copy-start.1
  0.0 0.0 copy-start.2
  0.0 0.0 copy-start.3
  0.0 3.0 %shard_map.101 = (f32[1,5,3,2048]{3,2,1,0:T(4,128)}, f32[1,5,3,2048]{3,2,1,0:T(4,128)}, f32[1,5,1,2048]{3,2,1,0:T(1,128)}, f32[1,5,1,2048]{3,2,1,0:T(1,128)}) custom-call(s32[1]{0:T(128)} %bitcast.r_0_, f32[8,32]{1,0:T(8,128)} %constant.74.clone.r_1_, f32[1,32,2048]{2,1,0:T(8,128)} %r_2_.3, f32[3,1,32,2048]{3,2,1,0:T(8,128)} %r_3_.3, f32[1,32,2048]{2,1,0:T(8,128)} %r_4_.3), custom_call_target="tpu_custom_call" | custom-call | tf_op jit(solution)/shard_map/pallas_call | solution.py:194
  3.0 3.0 %collective-permute-start.2 = (f32[1,5,1,2048]{3,2,1,0:T(1,128)}, f32[1,5,1,2048]{3,2,1,0:T(1,128)S(1)}, u32[]{:S(2)}, u32[]{:S(2)}) collective-permute-start(f32[1,5,1,2048]{3,2,1,0:T(1,128)} %get-tuple-element.11), channel_id=1, source_target_pairs={{0,8},{8,0},{12,20},{20,12},{16,24},{24,16},{28,4},{4,28},{1,9},{9... | collective-permute-start | bytes 122888 | tf_op jit(solution)/shard_map/ppermute | solution.py:205
  6.0 2.5 %collective-permute-start.3 = (f32[1,5,1,2048]{3,2,1,0:T(1,128)}, f32[1,5,1,2048]{3,2,1,0:T(1,128)S(1)}, u32[]{:S(2)}, u32[]{:S(2)}) collective-permute-start(f32[1,5,1,2048]{3,2,1,0:T(1,128)} %get-tuple-element.12), channel_id=1, source_target_pairs={{4,12},{12,4},{8,16},{16,8},{20,28},{28,20},{24,0},{0,24},{5,13},{... | collective-permute-start | bytes 122888 | tf_op jit(solution)/shard_map/ppermute | solution.py:205
  8.5 1.1 %collective-permute-start = (f32[1,5,3,2048]{3,2,1,0:T(4,128)}, f32[1,5,3,2048]{3,2,1,0:T(4,128)S(1)}, u32[]{:S(2)}, u32[]{:S(2)}) collective-permute-start(f32[1,5,3,2048]{3,2,1,0:T(4,128)} %get-tuple-element.9), channel_id=1, source_target_pairs={{0,4},{4,0},{8,12},{12,8},{16,20},{20,16},{24,28},{28,24},{1,5},{5... | collective-permute-start | bytes 368648 | tf_op jit(solution)/shard_map/ppermute | solution.py:205
  9.6 1.7 %collective-permute-start.1 = (f32[1,5,3,2048]{3,2,1,0:T(4,128)}, f32[1,5,3,2048]{3,2,1,0:T(4,128)S(1)}, u32[]{:S(2)}, u32[]{:S(2)}) collective-permute-start(f32[1,5,3,2048]{3,2,1,0:T(4,128)} %get-tuple-element.10), channel_id=1, source_target_pairs={{4,8},{8,4},{12,16},{16,12},{20,24},{24,20},{28,0},{0,28},{5,9},{9... | collective-permute-start | bytes 368648 | tf_op jit(solution)/shard_map/ppermute | solution.py:205
  11.3 0.0 copy-done
  11.3 0.0 copy-done.1
  11.3 0.0 copy-done.2
  11.4 0.0 copy-done.3
  11.4 6.3 %shard_map.100 = f32[5,1,32,2048]{3,2,1,0:T(8,128)} custom-call(f32[128,384]{1,0:T(8,128)} %constant.79.clone.r_0_, f32[32,32]{1,0:T(8,128)} %constant.80.clone.r_1_, f32[1,32,2048]{2,1,0:T(8,128)} %r_2_.3, f32[3,1,32,2048]{3,2,1,0:T(8,128)} %r_3_.3, f32[1,32,2048]{2,1,0:T(8,128)} %r_4_.3), custom_call_target="tpu_custom_call" | custom-call | tf_op jit(solution)/shard_map/pallas_call | solution.py:215
  17.7 0.0 collective-permute-done.2
  17.7 0.0 collective-permute-done.3
  17.8 0.0 collective-permute-done
  17.8 0.1 collective-permute-done.1
  17.9 3.7 %fusion = f32[5,1,32,2048]{3,2,1,0:T(8,128)} fusion(f32[5,1,32,2048]{3,2,1,0:T(8,128)} %shard_map.100, f32[1,5,1,2048]{3,2,1,0:T(1,128)S(1)} %collective-permute-done.3, f32[1,5,1,2048]{3,2,1,0:T(1,128)S(1)} %collective-permute-done.2, f32[1,5,3,2048]{3,2,1,0:T(4,128)S(1)} %collective-permute-done.1, f32[1,5,3,2048]{3,2,1,0:T(4,128)S(1)} %collective-permute-done, ...), kind=kOutput, calls=%fused_computation.1 | convolution fusion | flops 32031488 | bytes 2950144 | tf_op jit(solution)/shard_map/pr,zfrx->fzpx/dot_general | solution.py:227
  (2 shorter events, 0.0 us)
Async XLA Ops:
  0.0 11.3 %copy-start = (f32[32,3]{0,1:T(4,128)S(1)}, f32[32,3]{0,1:T(4,128)}, u32[]{:S(2)}) copy-start(f32[32,3]{0,1:T(4,128)} %constant.76.clone) | copy-start | bytes 1156
  0.0 11.3 %copy-start.1 = (f32[32,3]{0,1:T(4,128)S(1)}, f32[32,3]{0,1:T(4,128)}, u32[]{:S(2)}) copy-start(f32[32,3]{0,1:T(4,128)} %constant.75.clone) | copy-start | bytes 1156
  0.0 11.3 %copy-start.2 = (f32[32,1]{0,1:T(1,128)S(1)}, f32[32,1]{0,1:T(1,128)}, u32[]{:S(2)}) copy-start(f32[32,1]{0,1:T(1,128)} %constant.78.clone) | copy-start | bytes 388
  0.0 11.4 %copy-start.3 = (f32[32,1]{0,1:T(1,128)S(1)}, f32[32,1]{0,1:T(1,128)}, u32[]{:S(2)}) copy-start(f32[32,1]{0,1:T(1,128)} %constant.77.clone) | copy-start | bytes 388
  3.0 14.7 %collective-permute-start.2 = (f32[1,5,1,2048]{3,2,1,0:T(1,128)}, f32[1,5,1,2048]{3,2,1,0:T(1,128)S(1)}, u32[]{:S(2)}, u32[]{:S(2)}) collective-permute-start(f32[1,5,1,2048]{3,2,1,0:T(1,128)} %get-tuple-element.11), channel_id=1, source_target_pairs={{0,8},{8,0},{12,20},{20,12},{16,24},{24,16},{28,4},{4,28},{1,9},{9... | collective-permute-start | bytes 122888 | tf_op jit(solution)/shard_map/ppermute | solution.py:205
  6.0 11.7 %collective-permute-start.3 = (f32[1,5,1,2048]{3,2,1,0:T(1,128)}, f32[1,5,1,2048]{3,2,1,0:T(1,128)S(1)}, u32[]{:S(2)}, u32[]{:S(2)}) collective-permute-start(f32[1,5,1,2048]{3,2,1,0:T(1,128)} %get-tuple-element.12), channel_id=1, source_target_pairs={{4,12},{12,4},{8,16},{16,8},{20,28},{28,20},{24,0},{0,24},{5,13},{... | collective-permute-start | bytes 122888 | tf_op jit(solution)/shard_map/ppermute | solution.py:205
  8.5 9.2 %collective-permute-start = (f32[1,5,3,2048]{3,2,1,0:T(4,128)}, f32[1,5,3,2048]{3,2,1,0:T(4,128)S(1)}, u32[]{:S(2)}, u32[]{:S(2)}) collective-permute-start(f32[1,5,3,2048]{3,2,1,0:T(4,128)} %get-tuple-element.9), channel_id=1, source_target_pairs={{0,4},{4,0},{8,12},{12,8},{16,20},{20,16},{24,28},{28,24},{1,5},{5... | collective-permute-start | bytes 368648 | tf_op jit(solution)/shard_map/ppermute | solution.py:205
  9.6 8.3 %collective-permute-start.1 = (f32[1,5,3,2048]{3,2,1,0:T(4,128)}, f32[1,5,3,2048]{3,2,1,0:T(4,128)S(1)}, u32[]{:S(2)}, u32[]{:S(2)}) collective-permute-start(f32[1,5,3,2048]{3,2,1,0:T(4,128)} %get-tuple-element.10), channel_id=1, source_target_pairs={{4,8},{8,4},{12,16},{16,12},{20,24},{24,20},{28,0},{0,28},{5,9},{9... | collective-permute-start | bytes 368648 | tf_op jit(solution)/shard_map/ppermute | solution.py:205

commit v18 on v17

--- a/solution.py
+++ b/solution.py
@@ -224,9 +224,10 @@
             ],
         )(wx, jnp.asarray(own), density, momentum, energy)
         received = jnp.concatenate(received, axis=2)
-        return partial - jnp.einsum(
-            "pr,zfrx->fzpx", spread, received, precision=HI
-        )
+        out = partial
+        for r in range(received.shape[2]):
+            out = out - spread[None, None, :, r : r + 1] * jnp.moveaxis(received[:, :, r : r + 1, :], 1, 0)
+        return out
 
     return local
 

time: 21.7 us -> 21.1 us (0.972)
  matrix products: 3.67 us -> 0 us
  other arithmetic: 0.02 us -> 1.86 us
  local copies, waits for them, and re-layouts: 0.01 us -> 1.23 us
    dot_general x1 -> x0, matrix products: 3.67 us -> none  [local(): return partial - jnp.einsum('pr,zfrx->fzpx', spread, received, precision=HI)]
    sub x0 -> x1, other arithmetic: none -> 1.84 us  [local(): out - spread[None, None, :, r:r + 1] * jnp.moveaxis(received[:, :, r:r +...]
    unnamed x8 -> x16, local copies, waits for them, and re-layouts: 0.01 us -> 1.05 us
  transfers between devices with their start and end apart: 4 -> 4, of which waited for: 1 -> 0; matrix products, arithmetic and copies ran while one was open for 0% -> 1% of each run, Pallas kernels for 29% -> 30%
where the time goes in v18:
time: 21.1 us; the launch traced here: 20.9 us
  Pallas kernels  9.36 us (44%)
  starting transfers between devices  8.31 us (39%)
  other arithmetic  1.86 us (9%)
  local copies, waits for them, and re-layouts  1.23 us (6%)
    ppermute x4, starting transfers between devices, local(): received.append(lax.ppermute(message, 'row', perm))  8.31 us
    pallas_call x1, Pallas kernels, local(): pl.pallas_call(lambda *r: local_kernel(count, *r), grid=(planes,), in_spe...  6.35 us
    pallas_call x1, Pallas kernels, local(): pl.pallas_call(lambda *r: moments_kernel(split_of, choices, *r), grid=(pl...  3.02 us
    sub x1, other arithmetic, local(): out - spread[None, None, :, r:r + 1] * jnp.moveaxis(received[:, :, r:r +...  1.84 us
    unnamed x16, local copies, waits for them, and re-layouts  1.05 us
  transfers between devices with their start and end apart: 4, of which 0 were waited for; matrix products, arithmetic and copies ran while one was open for 1% of the time, Pallas kernels for 30%

profile of v18, /device:TPU:0, one launch (start us, length us, event | category | flops | bytes accessed | tf_op | source)
XLA Modules:
  0.0 20.9 jit_solution(4540382930690044943)
XLA Ops:
  0.0 0.0 copy-start.1
  0.0 0.0 copy-start.2
  0.0 0.0 copy-start.3
  0.0 0.0 copy-start.4
  0.0 3.0 %shard_map.101 = (f32[1,5,3,2048]{3,2,1,0:T(4,128)}, f32[1,5,3,2048]{3,2,1,0:T(4,128)}, f32[1,5,1,2048]{3,2,1,0:T(1,128)}, f32[1,5,1,2048]{3,2,1,0:T(1,128)}) custom-call(s32[1]{0:T(128)} %bitcast.1.r_0_, f32[8,32]{1,0:T(8,128)} %constant.74.clone.r_1_, f32[1,32,2048]{2,1,0:T(8,128)} %r_2_.3, f32[3,1,32,2048]{3,2,1,0:T(8,128)} %r_3_.3, f32[1,32,2048]{2,1,0:T(8,128)} %r_4_.3), custom_call_target="tpu_custom_call" | custom-call | tf_op jit(solution)/shard_map/pallas_call | solution.py:194
  3.0 3.0 %collective-permute-start.2 = (f32[1,5,1,2048]{3,2,1,0:T(1,128)}, f32[1,5,1,2048]{3,2,1,0:T(1,128)S(1)}, u32[]{:S(2)}, u32[]{:S(2)}) collective-permute-start(f32[1,5,1,2048]{3,2,1,0:T(1,128)} %get-tuple-element.11), channel_id=1, source_target_pairs={{0,8},{8,0},{12,20},{20,12},{16,24},{24,16},{28,4},{4,28},{1,9},{9... | collective-permute-start | bytes 122888 | tf_op jit(solution)/shard_map/ppermute | solution.py:205
  6.1 2.5 %collective-permute-start.3 = (f32[1,5,1,2048]{3,2,1,0:T(1,128)}, f32[1,5,1,2048]{3,2,1,0:T(1,128)S(1)}, u32[]{:S(2)}, u32[]{:S(2)}) collective-permute-start(f32[1,5,1,2048]{3,2,1,0:T(1,128)} %get-tuple-element.12), channel_id=1, source_target_pairs={{4,12},{12,4},{8,16},{16,8},{20,28},{28,20},{24,0},{0,24},{5,13},{... | collective-permute-start | bytes 122888 | tf_op jit(solution)/shard_map/ppermute | solution.py:205
  8.5 1.1 %collective-permute-start = (f32[1,5,3,2048]{3,2,1,0:T(4,128)}, f32[1,5,3,2048]{3,2,1,0:T(4,128)S(1)}, u32[]{:S(2)}, u32[]{:S(2)}) collective-permute-start(f32[1,5,3,2048]{3,2,1,0:T(4,128)} %get-tuple-element.9), channel_id=1, source_target_pairs={{0,4},{4,0},{8,12},{12,8},{16,20},{20,16},{24,28},{28,24},{1,5},{5... | collective-permute-start | bytes 368648 | tf_op jit(solution)/shard_map/ppermute | solution.py:205
  9.6 1.7 %collective-permute-start.1 = (f32[1,5,3,2048]{3,2,1,0:T(4,128)}, f32[1,5,3,2048]{3,2,1,0:T(4,128)S(1)}, u32[]{:S(2)}, u32[]{:S(2)}) collective-permute-start(f32[1,5,3,2048]{3,2,1,0:T(4,128)} %get-tuple-element.10), channel_id=1, source_target_pairs={{4,8},{8,4},{12,16},{16,12},{20,24},{24,20},{28,0},{0,28},{5,9},{9... | collective-permute-start | bytes 368648 | tf_op jit(solution)/shard_map/ppermute | solution.py:205
  11.3 0.0 copy-done.1
  11.3 0.0 copy-done.2
  11.4 0.0 copy-done.3
  11.4 0.0 copy-done.4
  11.4 6.3 %shard_map.100 = f32[5,1,32,2048]{3,2,1,0:T(8,128)} custom-call(f32[128,384]{1,0:T(8,128)} %constant.79.clone.r_0_, f32[32,32]{1,0:T(8,128)} %constant.80.clone.r_1_, f32[1,32,2048]{2,1,0:T(8,128)} %r_2_.3, f32[3,1,32,2048]{3,2,1,0:T(8,128)} %r_3_.3, f32[1,32,2048]{2,1,0:T(8,128)} %r_4_.3), custom_call_target="tpu_custom_call" | custom-call | tf_op jit(solution)/shard_map/pallas_call | solution.py:215
  17.8 0.0 copy-start
  17.8 0.0 collective-permute-done.2
  17.8 0.0 collective-permute-done.3
  17.8 0.0 collective-permute-done
  17.9 0.1 fusion
  18.0 0.0 collective-permute-done.1
  18.0 0.1 fusion.1
  18.2 0.9 %copy-done = f32[5,1,32,2048]{3,2,1,0:T(8,128)S(1)} copy-done((f32[5,1,32,2048]{3,2,1,0:T(8,128)S(1)}, f32[5,1,32,2048]{3,2,1,0:T(8,128)}, u32[]{:S(2)}) %copy-start) | copy-done | bytes 1310744
  19.1 1.8 %multiply_subtract_fusion = f32[5,1,32,2048]{3,2,1,0:T(8,128)} fusion(f32[5,1,32,2048]{3,2,1,0:T(8,128)S(1)} %copy-done, f32[5,2048]{1,0:T(8,128)S(1)} %bitcast.38, f32[32]{0:T(128)S(1)} %get-tuple-element.28, f32[5,2048]{1,0:T(8,128)S(1)} %bitcast.37, f32[32]{0:T(128)S(1)} %get-tuple-element.27, f32[5,2048]{1,0:T(8,128)S(1)} %get-tuple-element.29, ...), kind=kLoop, calls=%fused_computation | loop fusion | flops 5242880 | bytes 2950144 | tf_op jit(solution)/shard_map/sub | solution.py:229
  (9 shorter events, 0.2 us)
Async XLA Ops:
  0.0 11.3 %copy-start.1 = (f32[32,3]{0,1:T(4,128)S(1)}, f32[32,3]{0,1:T(4,128)}, u32[]{:S(2)}) copy-start(f32[32,3]{0,1:T(4,128)} %constant.76.clone) | copy-start | bytes 1156
  0.0 11.3 %copy-start.2 = (f32[32,3]{0,1:T(4,128)S(1)}, f32[32,3]{0,1:T(4,128)}, u32[]{:S(2)}) copy-start(f32[32,3]{0,1:T(4,128)} %constant.75.clone) | copy-start | bytes 1156
  0.0 11.4 %copy-start.3 = (f32[32,1]{0,1:T(1,128)S(1)}, f32[32,1]{0,1:T(1,128)}, u32[]{:S(2)}) copy-start(f32[32,1]{0,1:T(1,128)} %constant.78.clone) | copy-start | bytes 388
  0.0 11.4 %copy-start.4 = (f32[32,1]{0,1:T(1,128)S(1)}, f32[32,1]{0,1:T(1,128)}, u32[]{:S(2)}) copy-start(f32[32,1]{0,1:T(1,128)} %constant.77.clone) | copy-start | bytes 388
  3.0 14.7 %collective-permute-start.2 = (f32[1,5,1,2048]{3,2,1,0:T(1,128)}, f32[1,5,1,2048]{3,2,1,0:T(1,128)S(1)}, u32[]{:S(2)}, u32[]{:S(2)}) collective-permute-start(f32[1,5,1,2048]{3,2,1,0:T(1,128)} %get-tuple-element.11), channel_id=1, source_target_pairs={{0,8},{8,0},{12,20},{20,12},{16,24},{24,16},{28,4},{4,28},{1,9},{9... | collective-permute-start | bytes 122888 | tf_op jit(solution)/shard_map/ppermute | solution.py:205
  6.1 11.8 %collective-permute-start.3 = (f32[1,5,1,2048]{3,2,1,0:T(1,128)}, f32[1,5,1,2048]{3,2,1,0:T(1,128)S(1)}, u32[]{:S(2)}, u32[]{:S(2)}) collective-permute-start(f32[1,5,1,2048]{3,2,1,0:T(1,128)} %get-tuple-element.12), channel_id=1, source_target_pairs={{4,12},{12,4},{8,16},{16,8},{20,28},{28,20},{24,0},{0,24},{5,13},{... | collective-permute-start | bytes 122888 | tf_op jit(solution)/shard_map/ppermute | solution.py:205
  8.5 9.3 %collective-permute-start = (f32[1,5,3,2048]{3,2,1,0:T(4,128)}, f32[1,5,3,2048]{3,2,1,0:T(4,128)S(1)}, u32[]{:S(2)}, u32[]{:S(2)}) collective-permute-start(f32[1,5,3,2048]{3,2,1,0:T(4,128)} %get-tuple-element.9), channel_id=1, source_target_pairs={{0,4},{4,0},{8,12},{12,8},{16,20},{20,16},{24,28},{28,24},{1,5},{5... | collective-permute-start | bytes 368648 | tf_op jit(solution)/shard_map/ppermute | solution.py:205
  9.6 8.4 %collective-permute-start.1 = (f32[1,5,3,2048]{3,2,1,0:T(4,128)}, f32[1,5,3,2048]{3,2,1,0:T(4,128)S(1)}, u32[]{:S(2)}, u32[]{:S(2)}) collective-permute-start(f32[1,5,3,2048]{3,2,1,0:T(4,128)} %get-tuple-element.10), channel_id=1, source_target_pairs={{4,8},{8,4},{12,16},{16,12},{20,24},{24,20},{28,0},{0,28},{5,9},{9... | collective-permute-start | bytes 368648 | tf_op jit(solution)/shard_map/ppermute | solution.py:205
  17.8 1.3 %copy-start = (f32[5,1,32,2048]{3,2,1,0:T(8,128)S(1)}, f32[5,1,32,2048]{3,2,1,0:T(8,128)}, u32[]{:S(2)}) copy-start(f32[5,1,32,2048]{3,2,1,0:T(8,128)} %shard_map.100) | copy-start | bytes 3932164
